TPU v7x, 768 devices: a whole 4x8x12 slice. The times are simulated.
768 devices in a mesh: rep: 12 (over z_lo, core), row: 8 (over x, z_hi), col: 8 (over y).
Axes of the slice: x: 4, y: 8, z: 12 (z_hi: 2, z_lo: 6; z = z_hi * 6 + z_lo), core: 2. Of those that a mesh axis runs over, the one named last changes fastest.
Arguments:
- tokens: bfloat16 [1536, 4096], P('rep', 'row'), may hold values from -6 to 6
- gate_weight: bfloat16 [8, 1920, 4096], P('col', 'rep', 'row'), may hold values from -0.09375 to 0.09375
- up_weight: bfloat16 [8, 1920, 4096], P('col', 'rep', 'row'), may hold values from -0.09375 to 0.09375
- cotangent: bfloat16 [1536, 15360], P(('rep', 'row'), 'col'), may hold values from -5 to 5
Outputs:
- hidden: bfloat16 [1536, 15360], P(('rep', 'row'), 'col')
- grad_tokens: bfloat16 [1536, 4096], P(('rep', 'col'), 'row')
- grad_gate_weight: bfloat16 [8, 1920, 4096], P('col', 'rep', 'row')
- grad_up_weight: bfloat16 [8, 1920, 4096], P('col', 'rep', 'row')
All inputs are finite; a program needn't handle non-finite values.
Results may differ from a plain program's by a relative error of at most 0.017.
Values may be sent and summed in bfloat16 or wider, within the bound.
No kernel may reach another device: no remote copies, remote signals or barrier semaphores. Data moves between devices by JAX's collectives and lax.ppermute only.
A program may use at most 32 MiB of HBM per device.

v0:
```python
import jax
import jax.numpy as jnp
from jax import lax
from jax.sharding import PartitionSpec as P


def body(tokens, gate_weight, up_weight, cotangent):
    replicas = lax.axis_size("rep")
    gate_whole, up_whole = (
        lax.all_gather(gate_weight, "rep", axis=1, tiled=True),
        lax.all_gather(up_weight, "rep", axis=1, tiled=True),
    )
    weight_pair = jnp.concatenate([gate_whole, up_whole], 0)
    piece_rows = tokens
    summed = lax.psum_scatter(
        jnp.einsum("td,kfd->tkf", piece_rows, weight_pair, preferred_element_type=jnp.float32),
        "row",
        scatter_dimension=0,
        tiled=True,
    )
    gate_pre = summed[:, 0]
    up_pre = summed[:, 1]
    sigmoid_val = jax.nn.sigmoid(gate_pre)
    gated = gate_pre * sigmoid_val
    hidden = (gated * up_pre).astype(jnp.bfloat16)
    upstream = cotangent.astype(jnp.float32)
    grad_gate_pre = (
        upstream * up_pre * sigmoid_val * (1.0 + gate_pre * (1.0 - sigmoid_val))
    ).astype(jnp.bfloat16)
    grad_up_pre = (upstream * gated).astype(jnp.bfloat16)
    pair_grads = jnp.stack([grad_gate_pre, grad_up_pre], 1)
    gathered = lax.all_gather(pair_grads, "row", axis=0, tiled=True)
    replica_terms = jnp.einsum("tkf,td->kfd", gathered, tokens, preferred_element_type=jnp.float32)
    reduced = lax.psum_scatter(
        replica_terms.astype(jnp.bfloat16), "rep", scatter_dimension=1, tiled=True
    ).astype(jnp.float32)
    piece_rows = gathered
    grad_tokens = lax.psum_scatter(
        jnp.einsum("tkf,kfd->td", piece_rows, weight_pair, preferred_element_type=jnp.float32),
        "col",
        scatter_dimension=0,
        tiled=True,
    )
    inverse = 1.0 / replicas
    averaged = reduced * inverse
    grad_gate_weight = averaged[0:1].astype(jnp.bfloat16)
    grad_up_weight = averaged[1:2].astype(jnp.bfloat16)
    return (hidden, grad_tokens.astype(jnp.bfloat16), grad_gate_weight, grad_up_weight)


def solution(mesh):
    in_specs = (
        P("rep", "row"),
        P("col", "rep", "row"),
        P("col", "rep", "row"),
        P(("rep", "row"), "col"),
    )
    out_specs = (
        P(("rep", "row"), "col"),
        P(("rep", "col"), "row"),
        P("col", "rep", "row"),
        P("col", "rep", "row"),
    )
    return jax.shard_map(body, mesh=mesh, in_specs=in_specs, out_specs=out_specs, check_vma=False)
```

profile of v0, /device:TPU:6, one launch (start us, length us, event | category | flops | bytes accessed | tf_op | source)
XLA Modules:
  0.0 663.3 jit_solution(8262062425893699670)
XLA Ops:
  7.2 0.0 copy-start
  7.2 0.0 all-gather.3.cloned.1.call-start
  7.2 0.7 all-gather.3.cloned.1.call-update
  7.9 0.0 all-gather.5.cloned.1.call-start
  8.0 0.7 all-gather.5.cloned.1.call-update
  8.7 0.0 all-reduce.3.cloned.1.call-start
  8.7 78.9 %all-gather.3.cloned.1.call-done = bf16[1,1920,512]{2,1,0:T(8,128)(2,1)} async-done(((bf16[1,160,512]{2,1,0:T(8,128)(2,1)}), bf16[1,1920,512]{2,1,0:T(8,128)(2,1)}) %all-gather.3.cloned.1.call-update) | async-done | bytes 1966096 | tf_op jit(solution)/shard_map/all_gather | solution.py:10
  87.7 3.0 constant_dynamic-update-slice_fusion.1
  90.6 69.9 %all-gather.5.cloned.1.call-done = bf16[1,1920,512]{2,1,0:T(8,128)(2,1)} async-done(((bf16[1,160,512]{2,1,0:T(8,128)(2,1)}), bf16[1,1920,512]{2,1,0:T(8,128)(2,1)}) %all-gather.5.cloned.1.call-update) | async-done | bytes 1966096 | tf_op jit(solution)/shard_map/all_gather | solution.py:11
  160.5 2.9 constant_dynamic-update-slice_fusion
  163.4 0.0 copy-done
  163.4 3.3 convolution_bitcast_fusion
  166.7 0.0 copy-start.1
  166.8 2.5 copy.12
  169.3 0.0 all-reduce.3.cloned.1.call-update
  169.3 0.0 reduce-scatter.3.cloned.1.call-start
  169.4 1.3 dynamic-slice
  171.3 277.6 %all-reduce.3.cloned.1.call-done = f32[128,2,1920]{2,1,0:T(2,128)} async-done(((f32[128,2,1920]{2,1,0:T(2,128)}), f32[128,2,1920]{2,1,0:T(2,128)}) %all-reduce.3.cloned.1.call-update) | async-done | bytes 1966096
  448.8 1.3 constant_dynamic-slice_fusion
  450.1 0.0 copy-done.1
  450.1 0.7 fusion.11
  450.8 0.1 copy.14
  451.0 69.7 %all_gather.11 = bf16[128,2,1920]{2,1,0:T(2,128)(2,1)S(1)} all-gather(bf16[16,2,1920]{2,1,0:T(2,128)(2,1)S(1)} %copy.14), channel_id=1, replica_groups=mesh['rep'=12,'row'=8,'col'=8] {'row'}, dimensions={0}, use_global_device_ids=true | all-gather | bytes 1105920 | tf_op jit(solution)/shard_map/all_gather | solution.py:32
  520.6 3.5 convolution_bitcast_fusion.1
  524.1 0.0 reduce-scatter.3.cloned.1.call-update
  524.1 0.0 reduce-scatter.5.cloned.1.call-start
  524.2 3.1 convolution_convert_fusion
  527.3 0.0 reduce-scatter.5.cloned.1.call-update
  527.3 43.9 %reduce-scatter.3.cloned.1.call-done = f32[16,512]{1,0:T(8,128)} async-done(((f32[128,512]{1,0:T(8,128)}), f32[16,512]{1,0:T(8,128)}) %reduce-scatter.3.cloned.1.call-update) | async-done | bytes 32784 | tf_op jit(solution)/shard_map/reduce_scatter | solution.py:38
  571.2 1.4 convert_element_type.27
  572.6 82.5 %reduce-scatter.5.cloned.1.call-done = bf16[2,160,512]{2,1,0:T(8,128)(2,1)} async-done(((bf16[2,1920,512]{2,1,0:T(8,128)(2,1)}), bf16[2,160,512]{2,1,0:T(8,128)(2,1)}) %reduce-scatter.5.cloned.1.call-update) | async-done | bytes 327696 | tf_op jit(solution)/shard_map/reduce_scatter | solution.py:34
  655.0 1.0 multiply_convert_fusion
  656.1 0.7 fusion.12
  (1 shorter events, 0.0 us)
Async XLA Ops:
  7.2 156.3 %copy-start = (bf16[128,512]{1,0:T(8,128)(2,1)S(1)}, bf16[128,512]{1,0:T(8,128)(2,1)}, u32[]{:S(2)}) copy-start(bf16[128,512]{1,0:T(8,128)(2,1)} %param.4) | copy-start | bytes 393220
  7.2 80.5 %all-gather.3.cloned.1.call-start = ((), (), s32[]{:S(2)}) async-start(), calls=%async_computation.2 | async-start | bytes 2129920 | tf_op jit(solution)/shard_map/all_gather | solution.py:10
  7.9 152.6 %all-gather.5.cloned.1.call-start = ((), (), s32[]{:S(2)}) async-start(), calls=%async_computation.3 | async-start | bytes 2129920 | tf_op jit(solution)/shard_map/all_gather | solution.py:11
  8.7 440.2 %all-reduce.3.cloned.1.call-start = ((), (), s32[]{:S(2)}) async-start(), calls=%async_computation.6 | async-start | bytes 3932160
  166.7 283.4 %copy-start.1 = (bf16[16,1920]{1,0:T(8,128)(2,1)S(1)}, bf16[16,1920]{1,0:T(8,128)(2,1)}, u32[]{:S(2)}) copy-start(bf16[16,1920]{1,0:T(8,128)(2,1)} %param.7) | copy-start | bytes 184324
  169.3 401.9 %reduce-scatter.3.cloned.1.call-start = ((), (), s32[]{:S(2)}) async-start(), calls=%async_computation.4 | async-start | bytes 294912 | tf_op jit(solution)/shard_map/reduce_scatter | solution.py:38
  524.1 130.9 %reduce-scatter.5.cloned.1.call-start = ((), (), s32[]{:S(2)}) async-start(), calls=%async_computation.5 | async-start | bytes 4259840 | tf_op jit(solution)/shard_map/reduce_scatter | solution.py:34
Sparse Core Ops, SparseCore 0:
  10.4 77.2 all-gather.2
  90.0 70.4 all-gather.4
  169.4 279.3 all-reduce.2
  524.3 46.8 reduce-scatter.2
  574.2 80.7 reduce-scatter.4
where the time goes:
time: 664 us; the launch traced here: 663 us
  waiting for transfers between devices  554 us (83%)
  blocking collectives  69.7 us (10%)
  between operations  14.5 us (2%)
  local copies, waits for them, and re-layouts  11.8 us (2%)
  matrix products  9.86 us (1%)
    unnamed x6, waiting for transfers between devices  279 us
    reduce_scatter x1, waiting for transfers between devices, body(): lax.psum_scatter(replica_terms.astype(jnp.bfloat16), 'rep', scatter_dimen...  82.5 us
    all_gather x1, waiting for transfers between devices, body(): lax.all_gather(gate_weight, 'rep', axis=1, tiled=True)  78.9 us
    all_gather x1, waiting for transfers between devices, body(): lax.all_gather(up_weight, 'rep', axis=1, tiled=True)  69.9 us
    all_gather x1, blocking collectives, body(): gathered = lax.all_gather(pair_grads, 'row', axis=0, tiled=True)  69.7 us
    reduce_scatter x1, waiting for transfers between devices, body(): lax.psum_scatter(jnp.einsum('tkf,kfd->td', piece_rows, weight_pair, prefe...  43.9 us
  transfers between devices with their start and end apart: 5, of which 5 were waited for; matrix products, arithmetic and copies ran while one was open for 1% of the time, Pallas kernels for 0%

commit v1 on v0

v1 whole, which is shorter than its diff:
```python
import jax
import jax.numpy as jnp
from jax import lax
from jax.sharding import Mesh
from jax.sharding import PartitionSpec as P

REP = ("zl", "core")
ROW = ("x", "zh")


def body(tokens, gate_weight, up_weight, cotangent):
    replicas = lax.axis_size(REP)
    pair = jnp.concatenate([gate_weight, up_weight], 0)
    weight_pair = lax.all_gather(pair, REP, axis=1, tiled=True)
    hidden_units = weight_pair.shape[1]
    weight_rows = weight_pair.reshape(2 * hidden_units, weight_pair.shape[2])
    partial = jnp.einsum("td,hd->th", tokens, weight_rows, preferred_element_type=jnp.float32)
    summed = lax.psum_scatter(partial, "x", scatter_dimension=0, tiled=True)
    summed = lax.psum_scatter(summed, "zh", scatter_dimension=0, tiled=True)
    gate_pre = summed[:, :hidden_units]
    up_pre = summed[:, hidden_units:]
    sigmoid_val = jax.nn.sigmoid(gate_pre)
    gated = gate_pre * sigmoid_val
    hidden = (gated * up_pre).astype(jnp.bfloat16)
    upstream = cotangent.astype(jnp.float32)
    grad_gate_pre = (
        upstream * up_pre * sigmoid_val * (1.0 + gate_pre * (1.0 - sigmoid_val))
    ).astype(jnp.bfloat16)
    grad_up_pre = (upstream * gated).astype(jnp.bfloat16)
    pair_grads = jnp.concatenate([grad_gate_pre, grad_up_pre], 1)
    gathered = lax.all_gather(pair_grads, "zh", axis=0, tiled=True)
    gathered = lax.all_gather(gathered, "x", axis=0, tiled=True)
    replica_terms = jnp.einsum("th,td->hd", gathered, tokens, preferred_element_type=jnp.float32)
    replica_terms = replica_terms.reshape(weight_pair.shape)
    reduced = lax.psum_scatter(
        replica_terms.astype(jnp.bfloat16), REP, scatter_dimension=1, tiled=True
    ).astype(jnp.float32)
    grad_tokens = lax.psum_scatter(
        jnp.einsum("th,hd->td", gathered, weight_rows, preferred_element_type=jnp.float32),
        "col",
        scatter_dimension=0,
        tiled=True,
    )
    inverse = 1.0 / replicas
    averaged = reduced * inverse
    grad_gate_weight = averaged[0:1].astype(jnp.bfloat16)
    grad_up_weight = averaged[1:2].astype(jnp.bfloat16)
    return (hidden, grad_tokens.astype(jnp.bfloat16), grad_gate_weight, grad_up_weight)


def solution(mesh):
    n_rep, n_row, n_col = (mesh.shape[a] for a in ("rep", "row", "col"))
    devices = mesh.devices.reshape(n_rep // 2, 2, n_row // 2, 2, n_col)
    fine = Mesh(devices, ("zl", "core", "x", "zh", "col"))
    in_specs = (
        P(REP, ROW),
        P("col", REP, ROW),
        P("col", REP, ROW),
        P(REP + ROW, "col"),
    )
    out_specs = (
        P(REP + ROW, "col"),
        P(REP + ("col",), ROW),
        P("col", REP, ROW),
        P("col", REP, ROW),
    )
    return jax.shard_map(body, mesh=fine, in_specs=in_specs, out_specs=out_specs, check_vma=False)
```

time: 664 us -> 345 us (0.52)
  waiting for transfers between devices: 554 us -> 283 us
  blocking collectives: 69.7 us -> 29.1 us
  local copies, waits for them, and re-layouts: 11.8 us -> 2.54 us
    unnamed x6, waiting for transfers between devices: 279 us -> 33.4 us
    all_gather x2 -> x1, waiting for transfers between devices: 149 us -> 84.8 us  [body(): weight_pair = lax.all_gather(pair, REP, axis=1, tiled=True)]
    all_gather x1 -> x2, blocking collectives: 69.7 us -> 29.1 us  [the longest x1 15 us: body(): gathered = lax.all_gather(gathered, 'x', axis=0, tiled=True)]
    reduce_scatter x2 -> x3, waiting for transfers between devices: 126 us -> 165 us  [the longest x1 82.9 us: body(): lax.psum_scatter(replica_terms.astype(jnp.bfloat16), REP, scatter_dimensi...]
where the time goes in v1:
time: 345 us; the launch traced here: 344 us
  waiting for transfers between devices  283 us (82%)
  blocking collectives  29.1 us (8%)
  between operations  13.8 us (4%)
  matrix products  9.87 us (3%)
  other arithmetic  5.84 us (2%)
    all_gather x1, waiting for transfers between devices, body(): weight_pair = lax.all_gather(pair, REP, axis=1, tiled=True)  84.8 us
    reduce_scatter x1, waiting for transfers between devices, body(): lax.psum_scatter(replica_terms.astype(jnp.bfloat16), REP, scatter_dimensi...  82.9 us
    reduce_scatter x1, waiting for transfers between devices, body(): summed = lax.psum_scatter(summed, 'zh', scatter_dimension=0, tiled=True)  47.4 us
    reduce_scatter x1, waiting for transfers between devices, body(): lax.psum_scatter(jnp.einsum('th,hd->td', gathered, weight_rows, preferred...  34.4 us
    unnamed x6, waiting for transfers between devices  33.4 us
    all_gather x1, blocking collectives, body(): gathered = lax.all_gather(gathered, 'x', axis=0, tiled=True)  15 us
    all_gather x1, blocking collectives, body(): gathered = lax.all_gather(pair_grads, 'zh', axis=0, tiled=True)  14.1 us
  transfers between devices with their start and end apart: 5, of which 5 were waited for; matrix products, arithmetic and copies ran while one was open for 1% of the time, Pallas kernels for 0%

profile of v1, /device:TPU:6, one launch (start us, length us, event | category | flops | bytes accessed | tf_op | source)
XLA Modules:
  0.0 344.3 jit_solution(6337718626353473565)
XLA Ops:
  7.2 0.0 copy-start
  7.2 0.0 all-gather.2.cloned.1.call-start
  7.2 1.8 pad_maximum_fusion
  9.0 0.0 all-gather.2.cloned.1.call-update
  9.0 0.0 reduce-scatter.13.cloned.1.call-start
  9.1 84.8 %all-gather.2.cloned.1.call-done = bf16[2,1920,512]{2,1,0:T(8,128)(2,1)} async-done(((bf16[2,160,512]{2,1,0:T(8,128)(2,1)}), bf16[2,1920,512]{2,1,0:T(8,128)(2,1)}) %all-gather.2.cloned.1.call-update) | async-done | bytes 3932176 | tf_op jit(solution)/shard_map/all_gather | solution.py:14
  93.8 0.0 copy-done
  93.8 3.3 convolution_bitcast_fusion
  97.1 0.0 copy-start.1
  97.1 1.8 copy.16
  98.9 0.0 reduce-scatter.13.cloned.1.call-update
  98.9 0.0 reduce-scatter.15.cloned.1.call-start
  99.0 33.4 %reduce-scatter.13.cloned.1.call-done = f32[32,3840]{1,0:T(8,128)} async-done(((f32[128,3840]{1,0:T(8,128)}), f32[32,3840]{1,0:T(8,128)}) %reduce-scatter.13.cloned.1.call-update) | async-done | bytes 491536
  132.4 0.0 reduce-scatter.15.cloned.1.call-update
  132.4 0.0 reduce-scatter.9.cloned.1.call-start
  132.4 47.4 %reduce-scatter.15.cloned.1.call-done = f32[16,3840]{1,0:T(8,128)} async-done(((f32[32,3840]{1,0:T(8,128)}), f32[16,3840]{1,0:T(8,128)}) %reduce-scatter.15.cloned.1.call-update) | async-done | bytes 245776 | tf_op jit(solution)/shard_map/reduce_scatter | solution.py:19
  179.8 0.0 copy-done.1
  179.8 1.7 fusion.2
  181.5 14.1 %all_gather.10 = bf16[32,3840]{1,0:T(8,128)(2,1)S(1)} all-gather(bf16[16,3840]{1,0:T(8,128)(2,1)S(1)} %pad_maximum_fusion.1), channel_id=1, replica_groups=mesh['zl'=6,'core'=2,'x'=4,'zh'=2,'col'=8] {'zh'}, dimensions={0}, use_global_device_ids=true | all-gather | bytes 368640 | tf_op jit(solution)/shard_map/all_gather | solution.py:31
  195.6 15.0 %all_gather.11 = bf16[128,3840]{1,0:T(8,128)(2,1)S(1)} all-gather(bf16[32,3840]{1,0:T(8,128)(2,1)S(1)} %all_gather.10), channel_id=1, replica_groups=mesh['zl'=6,'core'=2,'x'=4,'zh'=2,'col'=8] {'x'}, dimensions={0}, use_global_device_ids=true | all-gather | bytes 1228800 | tf_op jit(solution)/shard_map/all_gather | solution.py:32
  210.6 3.5 %fusion.6 = f32[128,512]{1,0:T(8,128)} fusion(bf16[128,3840]{1,0:T(8,128)(2,1)S(1)} %all_gather.11, bf16[3840,512]{1,0:T(8,128)(2,1)} %bitcast.14), kind=kOutput, calls=%fused_computation.15 | convolution fusion | flops 503316480 | bytes 5177344 | tf_op jit(solution)/shard_map/th,hd->td/dot_general | solution.py:39
  214.1 0.0 reduce-scatter.9.cloned.1.call-update
  214.1 0.0 reduce-scatter.11.cloned.1.call-start
  214.2 3.1 convolution_convert_fusion
  217.2 0.0 reduce-scatter.11.cloned.1.call-update
  217.3 34.4 %reduce-scatter.9.cloned.1.call-done = f32[16,512]{1,0:T(8,128)} async-done(((f32[128,512]{1,0:T(8,128)}), f32[16,512]{1,0:T(8,128)}) %reduce-scatter.9.cloned.1.call-update) | async-done | bytes 32784 | tf_op jit(solution)/shard_map/reduce_scatter | solution.py:38
  251.7 1.4 convert_element_type.30
  253.1 82.9 %reduce-scatter.11.cloned.1.call-done = bf16[2,160,512]{2,1,0:T(8,128)(2,1)} async-done(((bf16[2,1920,512]{2,1,0:T(8,128)(2,1)}), bf16[2,160,512]{2,1,0:T(8,128)(2,1)}) %reduce-scatter.11.cloned.1.call-update) | async-done | bytes 327696 | tf_op jit(solution)/shard_map/reduce_scatter | solution.py:35
  336.0 1.0 multiply_convert_fusion
  337.0 0.7 fusion.5
  (1 shorter events, 0.0 us)
Async XLA Ops:
  7.2 86.7 %copy-start = (bf16[128,512]{1,0:T(8,128)(2,1)S(1)}, bf16[128,512]{1,0:T(8,128)(2,1)}, u32[]{:S(2)}) copy-start(bf16[128,512]{1,0:T(8,128)(2,1)} %param.4) | copy-start | bytes 393220
  7.2 86.6 %all-gather.2.cloned.1.call-start = ((), (), s32[]{:S(2)}) async-start(), calls=%async_computation.4 | async-start | bytes 4259840 | tf_op jit(solution)/shard_map/all_gather | solution.py:14
  9.0 123.3 %reduce-scatter.13.cloned.1.call-start = ((), (), s32[]{:S(2)}) async-start(), calls=%async_computation.7 | async-start | bytes 2457600
  97.1 82.7 %copy-start.1 = (bf16[16,1920]{1,0:T(8,128)(2,1)S(1)}, bf16[16,1920]{1,0:T(8,128)(2,1)}, u32[]{:S(2)}) copy-start(bf16[16,1920]{1,0:T(8,128)(2,1)} %param.7) | copy-start | bytes 184324
  98.9 80.9 %reduce-scatter.15.cloned.1.call-start = ((), (), s32[]{:S(2)}) async-start(), calls=%async_computation.8 | async-start | bytes 737280 | tf_op jit(solution)/shard_map/reduce_scatter | solution.py:19
  132.4 119.3 %reduce-scatter.9.cloned.1.call-start = ((), (), s32[]{:S(2)}) async-start(), calls=%async_computation.5 | async-start | bytes 294912 | tf_op jit(solution)/shard_map/reduce_scatter | solution.py:38
  214.1 121.9 %reduce-scatter.11.cloned.1.call-start = ((), (), s32[]{:S(2)}) async-start(), calls=%async_computation.6 | async-start | bytes 4259840 | tf_op jit(solution)/shard_map/reduce_scatter | solution.py:35
Sparse Core Ops, SparseCore 0:
  10.4 83.3 all-gather.1
  99.1 33.2 reduce-scatter.12
  135.5 44.3 reduce-scatter.14
  214.2 37.4 reduce-scatter.8
  255.0 80.9 reduce-scatter.10

commit v2 on v1

--- a/solution.py
+++ b/solution.py
@@ -11,12 +11,17 @@
 def body(tokens, gate_weight, up_weight, cotangent):
     replicas = lax.axis_size(REP)
     pair = jnp.concatenate([gate_weight, up_weight], 0)
+    shard_units = pair.shape[1]
     weight_pair = lax.all_gather(pair, REP, axis=1, tiled=True)
+    copies = jnp.broadcast_to(tokens[None], (replicas,) + tokens.shape)
+    all_tokens = lax.all_to_all(copies, REP, 0, 0, tiled=True)
     hidden_units = weight_pair.shape[1]
     weight_rows = weight_pair.reshape(2 * hidden_units, weight_pair.shape[2])
     partial = jnp.einsum("td,hd->th", tokens, weight_rows, preferred_element_type=jnp.float32)
     summed = lax.psum_scatter(partial, "x", scatter_dimension=0, tiled=True)
-    summed = lax.psum_scatter(summed, "zh", scatter_dimension=0, tiled=True)
+    summed = lax.psum_scatter(
+        summed.astype(jnp.bfloat16), "zh", scatter_dimension=0, tiled=True
+    ).astype(jnp.float32)
     gate_pre = summed[:, :hidden_units]
     up_pre = summed[:, hidden_units:]
     sigmoid_val = jax.nn.sigmoid(gate_pre)
@@ -30,19 +35,18 @@
     pair_grads = jnp.concatenate([grad_gate_pre, grad_up_pre], 1)
     gathered = lax.all_gather(pair_grads, "zh", axis=0, tiled=True)
     gathered = lax.all_gather(gathered, "x", axis=0, tiled=True)
-    replica_terms = jnp.einsum("th,td->hd", gathered, tokens, preferred_element_type=jnp.float32)
-    replica_terms = replica_terms.reshape(weight_pair.shape)
-    reduced = lax.psum_scatter(
-        replica_terms.astype(jnp.bfloat16), REP, scatter_dimension=1, tiled=True
-    ).astype(jnp.float32)
     grad_tokens = lax.psum_scatter(
         jnp.einsum("th,hd->td", gathered, weight_rows, preferred_element_type=jnp.float32),
         "col",
         scatter_dimension=0,
         tiled=True,
     )
-    inverse = 1.0 / replicas
-    averaged = reduced * inverse
+    rows = gathered.shape[0]
+    by_owner = gathered.reshape(rows, 2, replicas, shard_units).transpose(2, 0, 1, 3)
+    owned = lax.all_to_all(by_owner, REP, 0, 0, tiled=True)
+    terms = jnp.einsum("qtkh,qtd->qkhd", owned, all_tokens, preferred_element_type=jnp.float32)
+    rounded = lax.reduce_precision(terms, exponent_bits=8, mantissa_bits=7)
+    averaged = jnp.sum(rounded, axis=0) * (1.0 / replicas)
     grad_gate_weight = averaged[0:1].astype(jnp.bfloat16)
     grad_up_weight = averaged[1:2].astype(jnp.bfloat16)
     return (hidden, grad_tokens.astype(jnp.bfloat16), grad_gate_weight, grad_up_weight)

time: 345 us -> 266 us (0.77)
  waiting for transfers between devices: 283 us -> 186 us
  starting transfers between devices: 0.2 us -> 15.1 us
  local copies, waits for them, and re-layouts: 2.54 us -> 8.07 us
    reduce_scatter x2 -> x1, waiting for transfers between devices: 130 us -> 34 us  [body(): lax.psum_scatter(summed.astype(jnp.bfloat16), 'zh', scatter_dimension=0,...]
    all_to_all x0 -> x2, starting transfers between devices: none -> 15 us  [the longest x1 8.9 us: body(): owned = lax.all_to_all(by_owner, REP, 0, 0, tiled=True)]
    unnamed x6 -> x5, waiting for transfers between devices: 33.4 us -> 26 us
    reduce_scatter x1, waiting for transfers between devices: 34.4 us -> 41.4 us  [body(): lax.psum_scatter(jnp.einsum('th,hd->td', gathered, weight_rows, preferred...]
  transfers between devices with their start and end apart: 5 -> 6, of which waited for: 5 -> 4; matrix products, arithmetic and copies ran while one was open for 1% -> 5% of each run, Pallas kernels for 0% -> 0%
where the time goes in v2:
time: 266 us
  waiting for transfers between devices  186 us (70%)
  blocking collectives  29.7 us (11%)
  starting transfers between devices  15.1 us (6%)
  between operations  13.9 us (5%)
  local copies, waits for them, and re-layouts  8.07 us (3%)
  matrix products  7.98 us (3%)
  other arithmetic  4.79 us (2%)
    all_gather x1, waiting for transfers between devices, body(): weight_pair = lax.all_gather(pair, REP, axis=1, tiled=True)  84.8 us
    reduce_scatter x1, waiting for transfers between devices, body(): lax.psum_scatter(jnp.einsum('th,hd->td', gathered, weight_rows, preferred...  41.4 us
    reduce_scatter x1, waiting for transfers between devices, body(): lax.psum_scatter(summed.astype(jnp.bfloat16), 'zh', scatter_dimension=0,...  34 us
    unnamed x5, waiting for transfers between devices  26 us
    all_gather x1, blocking collectives, body(): gathered = lax.all_gather(gathered, 'x', axis=0, tiled=True)  17.7 us
    all_gather x1, blocking collectives, body(): gathered = lax.all_gather(pair_grads, 'zh', axis=0, tiled=True)  11.9 us
    all_to_all x1, starting transfers between devices, body(): owned = lax.all_to_all(by_owner, REP, 0, 0, tiled=True)  8.9 us
    all_to_all x1, starting transfers between devices, body(): all_tokens = lax.all_to_all(copies, REP, 0, 0, tiled=True)  6.06 us
  transfers between devices with their start and end apart: 6, of which 4 were waited for; matrix products, arithmetic and copies ran while one was open for 5% of the time, Pallas kernels for 0%

profile of v2, /device:TPU:6, one launch (start us, length us, event | category | flops | bytes accessed | tf_op | source)
XLA Modules:
  0.0 265.7 jit_solution(427079735919259317)
XLA Ops:
  7.2 0.0 all-gather.2.cloned.1.call-start
  7.2 1.7 pad_maximum_fusion
  8.9 0.0 all-gather.2.cloned.1.call-update
  9.0 0.0 reduce-scatter.10.cloned.1.call-start
  9.0 84.8 %all-gather.2.cloned.1.call-done = bf16[2,1920,512]{2,1,0:T(8,128)(2,1)} async-done(((bf16[2,160,512]{2,1,0:T(8,128)(2,1)}), bf16[2,1920,512]{2,1,0:T(8,128)(2,1)}) %all-gather.2.cloned.1.call-update) | async-done | bytes 3932176 | tf_op jit(solution)/shard_map/all_gather | solution.py:15
  93.8 3.3 %convolution_bitcast_fusion = f32[128,3840]{0,1:T(8,128)S(1)} fusion(bf16[3840,512]{1,0:T(8,128)(2,1)} %bitcast.19, bf16[128,512]{1,0:T(8,128)(2,1)} %param.4), kind=kOutput, calls=%fused_computation.1 | convolution fusion | flops 503316480 | bytes 6029312 | tf_op jit(solution)/shard_map/td,hd->th/dot_general | solution.py:20
  97.1 0.0 copy-start
  97.1 1.8 copy.25
  98.9 0.0 reduce-scatter.10.cloned.1.call-update
  99.0 0.0 copy-done
  99.0 0.0 copy-start.1
  99.0 1.3 broadcast_in_dim.2
  100.3 6.1 %all-to-all-start.1 = ((bf16[12,128,512]{2,1,0:T(8,128)(2,1)}), bf16[12,128,512]{2,1,0:T(8,128)(2,1)S(1)}, u32[]{:S(2)}, u32[]{:S(2)}) async-start(bf16[12,128,512]{2,1,0:T(8,128)(2,1)} %broadcast_in_dim.2), calls=%async_computation.2 | async-start | bytes 3145728 | tf_op jit(solution)/shard_map/all_to_all | solution.py:17
  106.3 0.0 reduce-scatter.12.cloned.1.call-start
  106.4 26.0 %reduce-scatter.10.cloned.1.call-done = f32[32,3840]{1,0:T(8,128)} async-done(((f32[128,3840]{1,0:T(8,128)}), f32[32,3840]{1,0:T(8,128)}) %reduce-scatter.10.cloned.1.call-update) | async-done | bytes 491536
  132.4 1.5 copy.26
  133.9 1.0 copy.27
  134.9 0.0 reduce-scatter.12.cloned.1.call-update
  134.9 34.0 %reduce-scatter.12.cloned.1.call-done = bf16[16,3840]{1,0:T(8,128)(2,1)} async-done(((bf16[32,3840]{1,0:T(8,128)(2,1)}), bf16[16,3840]{1,0:T(8,128)(2,1)}) %reduce-scatter.12.cloned.1.call-update) | async-done | bytes 122896 | tf_op jit(solution)/shard_map/reduce_scatter | solution.py:22
  168.9 0.9 convert_element_type.24
  169.9 0.0 copy-done.1
  169.9 0.7 fusion.3
  170.6 11.9 %all_gather.10 = bf16[32,3840]{1,0:T(8,128)(2,1)S(1)} all-gather(bf16[16,3840]{1,0:T(8,128)(2,1)S(1)} %pad_maximum_fusion.1), channel_id=1, replica_groups=mesh['zl'=6,'core'=2,'x'=4,'zh'=2,'col'=8] {'zh'}, dimensions={0}, use_global_device_ids=true | all-gather | bytes 368640 | tf_op jit(solution)/shard_map/all_gather | solution.py:36
  182.5 17.7 %all_gather.11 = bf16[128,3840]{1,0:T(8,128)(2,1)S(1)} all-gather(bf16[32,3840]{1,0:T(8,128)(2,1)S(1)} %all_gather.10), channel_id=1, replica_groups=mesh['zl'=6,'core'=2,'x'=4,'zh'=2,'col'=8] {'x'}, dimensions={0}, use_global_device_ids=true | all-gather | bytes 1228800 | tf_op jit(solution)/shard_map/all_gather | solution.py:37
  200.2 0.6 copy.22
  200.9 1.0 copy.30
  201.9 0.0 all-to-all-done.1
  201.9 8.9 %all-to-all-start = ((bf16[12,128,2,160]{1,3,2,0:T(8,128)(2,1)}), bf16[12,128,2,160]{1,3,2,0:T(8,128)(2,1)S(1)}, u32[]{:S(2)}, u32[]{:S(2)}) async-start(bf16[12,128,2,160]{1,3,2,0:T(8,128)(2,1)} %bitcast.18), calls=%async_computation.1 | async-start | bytes 1966080 | tf_op jit(solution)/shard_map/all_to_all | solution.py:46
  210.8 0.0 reduce-scatter.8.cloned.1.call-start
  210.9 3.5 %fusion.7 = f32[128,512]{1,0:T(8,128)} fusion(bf16[128,3840]{1,0:T(8,128)(2,1)S(1)} %all_gather.11, bf16[3840,512]{1,0:T(8,128)(2,1)} %bitcast.20), kind=kOutput, calls=%fused_computation.17 | convolution fusion | flops 503316480 | bytes 5177344 | tf_op jit(solution)/shard_map/th,hd->td/dot_general | solution.py:39
  214.4 0.0 reduce-scatter.8.cloned.1.call-update
  214.4 41.4 %reduce-scatter.8.cloned.1.call-done = f32[16,512]{1,0:T(8,128)} async-done(((f32[128,512]{1,0:T(8,128)}), f32[16,512]{1,0:T(8,128)}) %reduce-scatter.8.cloned.1.call-update) | async-done | bytes 32784 | tf_op jit(solution)/shard_map/reduce_scatter | solution.py:38
  255.8 1.4 convert_element_type.29
  257.2 0.0 all-to-all-done
  257.2 1.2 reduce-precision_reduce_fusion
  258.4 0.1 multiply_convert_fusion
  258.4 0.7 fusion.6
  (1 shorter events, 0.0 us)
Async XLA Ops:
  7.2 86.6 %all-gather.2.cloned.1.call-start = ((), (), s32[]{:S(2)}) async-start(), calls=%async_computation.5 | async-start | bytes 4259840 | tf_op jit(solution)/shard_map/all_gather | solution.py:15
  9.0 123.4 %reduce-scatter.10.cloned.1.call-start = ((), (), s32[]{:S(2)}) async-start(), calls=%async_computation.7 | async-start | bytes 2457600
  97.1 1.8 copy-start
  99.0 70.9 %copy-start.1 = (bf16[16,1920]{1,0:T(8,128)(2,1)S(1)}, bf16[16,1920]{1,0:T(8,128)(2,1)}, u32[]{:S(2)}) copy-start(bf16[16,1920]{1,0:T(8,128)(2,1)} %param.7) | copy-start | bytes 184324
  100.3 101.7 %all-to-all-start.1 = ((bf16[12,128,512]{2,1,0:T(8,128)(2,1)}), bf16[12,128,512]{2,1,0:T(8,128)(2,1)S(1)}, u32[]{:S(2)}, u32[]{:S(2)}) async-start(bf16[12,128,512]{2,1,0:T(8,128)(2,1)} %broadcast_in_dim.2), calls=%async_computation.2 | async-start | bytes 3145728 | tf_op jit(solution)/shard_map/all_to_all | solution.py:17
  106.3 62.6 %reduce-scatter.12.cloned.1.call-start = ((), (), s32[]{:S(2)}) async-start(), calls=%async_computation.8 | async-start | bytes 368640 | tf_op jit(solution)/shard_map/reduce_scatter | solution.py:22
  201.9 55.3 %all-to-all-start = ((bf16[12,128,2,160]{1,3,2,0:T(8,128)(2,1)}), bf16[12,128,2,160]{1,3,2,0:T(8,128)(2,1)S(1)}, u32[]{:S(2)}, u32[]{:S(2)}) async-start(bf16[12,128,2,160]{1,3,2,0:T(8,128)(2,1)} %bitcast.18), calls=%async_computation.1 | async-start | bytes 1966080 | tf_op jit(solution)/shard_map/all_to_all | solution.py:46
  210.8 45.0 %reduce-scatter.8.cloned.1.call-start = ((), (), s32[]{:S(2)}) async-start(), calls=%async_computation.6 | async-start | bytes 294912 | tf_op jit(solution)/shard_map/reduce_scatter | solution.py:38
Sparse Core Ops, SparseCore 0:
  10.4 83.3 all-gather.1
  99.1 33.2 reduce-scatter.9
  135.4 33.4 reduce-scatter.11
  214.5 41.2 reduce-scatter.7

commit v3 on v2

--- a/solution.py
+++ b/solution.py
@@ -10,9 +10,11 @@
 
 def body(tokens, gate_weight, up_weight, cotangent):
     replicas = lax.axis_size(REP)
-    pair = jnp.concatenate([gate_weight, up_weight], 0)
-    shard_units = pair.shape[1]
-    weight_pair = lax.all_gather(pair, REP, axis=1, tiled=True)
+    shard_units = gate_weight.shape[1]
+    gate_whole = lax.all_gather(gate_weight, REP, axis=1, tiled=True)
+    up_copies = jnp.broadcast_to(up_weight, (replicas,) + up_weight.shape[1:])
+    up_whole = lax.all_to_all(up_copies, REP, 0, 0, tiled=True)
+    weight_pair = jnp.concatenate([gate_whole, up_whole.reshape(gate_whole.shape)], 0)
     copies = jnp.broadcast_to(tokens[None], (replicas,) + tokens.shape)
     all_tokens = lax.all_to_all(copies, REP, 0, 0, tiled=True)
     hidden_units = weight_pair.shape[1]
@@ -35,12 +37,10 @@
     pair_grads = jnp.concatenate([grad_gate_pre, grad_up_pre], 1)
     gathered = lax.all_gather(pair_grads, "zh", axis=0, tiled=True)
     gathered = lax.all_gather(gathered, "x", axis=0, tiled=True)
-    grad_tokens = lax.psum_scatter(
-        jnp.einsum("th,hd->td", gathered, weight_rows, preferred_element_type=jnp.float32),
-        "col",
-        scatter_dimension=0,
-        tiled=True,
-    )
+    n_col = lax.axis_size("col")
+    token_partial = jnp.einsum("th,hd->td", gathered, weight_rows, preferred_element_type=jnp.float32)
+    token_chunks = token_partial.reshape(n_col, token_partial.shape[0] // n_col, token_partial.shape[1])
+    grad_tokens = jnp.sum(lax.all_to_all(token_chunks, "col", 0, 0, tiled=True), axis=0)
     rows = gathered.shape[0]
     by_owner = gathered.reshape(rows, 2, replicas, shard_units).transpose(2, 0, 1, 3)
     owned = lax.all_to_all(by_owner, REP, 0, 0, tiled=True)

time: 266 us -> 300 us (1.13)
  starting transfers between devices: 15.1 us -> 37.8 us
  waiting for transfers between devices: 186 us -> 198 us
  local copies, waits for them, and re-layouts: 8.07 us -> 12.3 us
  blocking collectives: 29.7 us -> 26.6 us
    reduce_scatter x1 -> x0, waiting for transfers between devices: 41.4 us -> none  [body(): lax.psum_scatter(jnp.einsum('th,hd->td', gathered, weight_rows, preferred...]
    all_to_all x1, waiting for transfers between devices: 0.01 us -> 35.1 us  [body(): owned = lax.all_to_all(by_owner, REP, 0, 0, tiled=True)]
    all_to_all x0 -> x2, starting transfers between devices: none -> 18.6 us  [the longest x1 12.1 us: body(): up_whole = lax.all_to_all(up_copies, REP, 0, 0, tiled=True)]
    all_to_all x0 -> x2, waiting for transfers between devices: none -> 8.9 us  [the longest x1 8.9 us: body(): lax.all_to_all(token_chunks, 'col', 0, 0, tiled=True)]
    all_gather x1, waiting for transfers between devices: 84.8 us -> 92.4 us  [body(): gate_whole = lax.all_gather(gate_weight, REP, axis=1, tiled=True)]
    all_to_all x1, starting transfers between devices: 8.9 us -> 12.7 us  [body(): owned = lax.all_to_all(by_owner, REP, 0, 0, tiled=True)]
    all_gather x1, blocking collectives: 17.7 us -> 14.6 us  [body(): gathered = lax.all_gather(gathered, 'x', axis=0, tiled=True)]
    unnamed x5 -> x4, waiting for transfers between devices: 26 us -> 28.9 us
  transfers between devices with their start and end apart: 6 -> 7, of which waited for: 4 -> 5; matrix products, arithmetic and copies ran while one was open for 5% -> 4% of each run, Pallas kernels for 0% -> 0%
where the time goes in v3:
time: 300 us
  waiting for transfers between devices  198 us (66%)
  starting transfers between devices  37.8 us (13%)
  blocking collectives  26.6 us (9%)
  between operations  13.8 us (5%)
  local copies, waits for them, and re-layouts  12.3 us (4%)
  matrix products  5.82 us (2%)
  other arithmetic  5.21 us (2%)
    all_gather x1, waiting for transfers between devices, body(): gate_whole = lax.all_gather(gate_weight, REP, axis=1, tiled=True)  92.4 us
    all_to_all x1, waiting for transfers between devices, body(): owned = lax.all_to_all(by_owner, REP, 0, 0, tiled=True)  35.1 us
    reduce_scatter x1, waiting for transfers between devices, body(): lax.psum_scatter(summed.astype(jnp.bfloat16), 'zh', scatter_dimension=0,...  32.7 us
    unnamed x4, waiting for transfers between devices  28.9 us
    all_gather x1, blocking collectives, body(): gathered = lax.all_gather(gathered, 'x', axis=0, tiled=True)  14.6 us
    all_to_all x1, starting transfers between devices, body(): owned = lax.all_to_all(by_owner, REP, 0, 0, tiled=True)  12.7 us
    all_to_all x1, starting transfers between devices, body(): up_whole = lax.all_to_all(up_copies, REP, 0, 0, tiled=True)  12.1 us
    all_gather x1, blocking collectives, body(): gathered = lax.all_gather(pair_grads, 'zh', axis=0, tiled=True)  12 us
  transfers between devices with their start and end apart: 7, of which 5 were waited for; matrix products, arithmetic and copies ran while one was open for 4% of the time, Pallas kernels for 0%

profile of v3, /device:TPU:6, one launch (start us, length us, event | category | flops | bytes accessed | tf_op | source)
XLA Modules:
  0.0 299.5 jit_solution(13334083338983462349)
XLA Ops:
  7.2 2.3 broadcast_in_dim.14
  9.5 12.1 %all-to-all-start = ((bf16[12,160,512]{2,1,0:T(8,128)(2,1)}), bf16[12,160,512]{2,1,0:T(8,128)(2,1)S(1)}, u32[]{:S(2)}, u32[]{:S(2)}) async-start(bf16[12,160,512]{2,1,0:T(8,128)(2,1)} %broadcast_in_dim.14), calls=%async_computation | async-start | bytes 3932160 | tf_op jit(solution)/shard_map/all_to_all | solution.py:16
  21.6 0.0 all-gather.2.cloned.1.call-start
  21.7 0.7 all-gather.2.cloned.1.call-update
  22.4 0.0 reduce-scatter.7.cloned.1.call-start
  22.4 92.4 %all-gather.2.cloned.1.call-done = bf16[1,1920,512]{2,1,0:T(8,128)(2,1)} async-done(((bf16[1,160,512]{2,1,0:T(8,128)(2,1)}), bf16[1,1920,512]{2,1,0:T(8,128)(2,1)}) %all-gather.2.cloned.1.call-update) | async-done | bytes 1966096 | tf_op jit(solution)/shard_map/all_gather | solution.py:14
  114.8 0.0 all-to-all-done
  114.8 0.0 copy-start.1
  114.8 1.9 pad_maximum_fusion
  116.8 0.0 copy-start
  116.8 1.9 copy-done
  118.7 0.0 copy-done.1
  118.7 1.2 convolution_bitcast_fusion
  119.8 1.9 copy.30
  121.7 0.0 reduce-scatter.7.cloned.1.call-update
  121.7 1.3 broadcast_in_dim.15
  123.0 6.4 %all-to-all-start.3 = ((bf16[12,128,512]{2,1,0:T(8,128)(2,1)}), bf16[12,128,512]{2,1,0:T(8,128)(2,1)S(1)}, u32[]{:S(2)}, u32[]{:S(2)}) async-start(bf16[12,128,512]{2,1,0:T(8,128)(2,1)} %broadcast_in_dim.15), calls=%async_computation.3 | async-start | bytes 3145728 | tf_op jit(solution)/shard_map/all_to_all | solution.py:19
  129.5 0.0 copy-start.2
  129.5 0.0 reduce-scatter.9.cloned.1.call-start
  129.5 28.2 %reduce-scatter.7.cloned.1.call-done = f32[32,3840]{1,0:T(8,128)} async-done(((f32[128,3840]{1,0:T(8,128)}), f32[32,3840]{1,0:T(8,128)}) %reduce-scatter.7.cloned.1.call-update) | async-done | bytes 491536
  157.7 1.5 copy.31
  159.2 1.0 copy.32
  160.3 0.0 reduce-scatter.9.cloned.1.call-update
  160.3 32.7 %reduce-scatter.9.cloned.1.call-done = bf16[16,3840]{1,0:T(8,128)(2,1)} async-done(((bf16[32,3840]{1,0:T(8,128)(2,1)}), bf16[16,3840]{1,0:T(8,128)(2,1)}) %reduce-scatter.9.cloned.1.call-update) | async-done | bytes 122896 | tf_op jit(solution)/shard_map/reduce_scatter | solution.py:24
  192.9 0.9 convert_element_type.24
  193.9 0.0 copy-done.2
  193.9 0.7 fusion.3
  194.6 12.0 %all_gather.10 = bf16[32,3840]{1,0:T(8,128)(2,1)S(1)} all-gather(bf16[16,3840]{1,0:T(8,128)(2,1)S(1)} %pad_maximum_fusion.1), channel_id=1, replica_groups=mesh['zl'=6,'core'=2,'x'=4,'zh'=2,'col'=8] {'zh'}, dimensions={0}, use_global_device_ids=true | all-gather | bytes 368640 | tf_op jit(solution)/shard_map/all_gather | solution.py:38
  206.6 14.6 %all_gather.11 = bf16[128,3840]{1,0:T(8,128)(2,1)S(1)} all-gather(bf16[32,3840]{1,0:T(8,128)(2,1)S(1)} %all_gather.10), channel_id=1, replica_groups=mesh['zl'=6,'core'=2,'x'=4,'zh'=2,'col'=8] {'x'}, dimensions={0}, use_global_device_ids=true | all-gather | bytes 1228800 | tf_op jit(solution)/shard_map/all_gather | solution.py:39
  221.2 3.5 %fusion.7 = f32[8,16,512]{2,1,0:T(8,128)} fusion(bf16[8,16,3840]{2,1,0:T(8,128)(2,1)S(1)} %bitcast.26, bf16[3840,512,1]{1,0,2:T(8,128)(2,1)} %bitcast.25), kind=kOutput, calls=%fused_computation.17 | convolution fusion | flops 503316480 | bytes 5177344 | tf_op jit(solution)/shard_map/th,hd->td/dot_general | solution.py:41
  224.6 0.0 all-to-all-done.3
  224.6 6.4 %all-to-all-start.1 = ((f32[8,16,512]{2,1,0:T(8,128)}), f32[8,16,512]{2,1,0:T(8,128)}, u32[]{:S(2)}, u32[]{:S(2)}) async-start(f32[8,16,512]{2,1,0:T(8,128)} %fusion.7), calls=%async_computation.1 | async-start | bytes 524288 | tf_op jit(solution)/shard_map/all_to_all | solution.py:43
  231.1 0.6 copy.27
  231.7 1.0 copy.35
  232.8 8.9 %all-to-all-done.1 = f32[8,16,512]{2,1,0:T(8,128)} async-done(((f32[8,16,512]{2,1,0:T(8,128)}), f32[8,16,512]{2,1,0:T(8,128)}, u32[]{:S(2)}, u32[]{:S(2)}) %all-to-all-start.1) | async-done | bytes 262176 | tf_op jit(solution)/shard_map/all_to_all | solution.py:43
  241.7 12.7 %all-to-all-start.2 = ((bf16[12,128,2,160]{1,3,2,0:T(8,128)(2,1)}), bf16[12,128,2,160]{1,3,2,0:T(8,128)(2,1)S(1)}, u32[]{:S(2)}, u32[]{:S(2)}) async-start(bf16[12,128,2,160]{1,3,2,0:T(8,128)(2,1)} %bitcast.23), calls=%async_computation.2 | async-start | bytes 1966080 | tf_op jit(solution)/shard_map/all_to_all | solution.py:46
  254.4 1.6 reduce_sum.18
  256.0 35.1 %all-to-all-done.2 = bf16[12,128,2,160]{1,3,2,0:T(8,128)(2,1)S(1)} async-done(((bf16[12,128,2,160]{1,3,2,0:T(8,128)(2,1)}), bf16[12,128,2,160]{1,3,2,0:T(8,128)(2,1)S(1)}, u32[]{:S(2)}, u32[]{:S(2)}) %all-to-all-start.2) | async-done | bytes 983072 | tf_op jit(solution)/shard_map/all_to_all | solution.py:46
  291.0 1.2 reduce-precision_reduce_fusion
  292.2 0.1 multiply_convert_fusion
  292.3 0.7 fusion.6
  (1 shorter events, 0.0 us)
Async XLA Ops:
  9.5 105.3 %all-to-all-start = ((bf16[12,160,512]{2,1,0:T(8,128)(2,1)}), bf16[12,160,512]{2,1,0:T(8,128)(2,1)S(1)}, u32[]{:S(2)}, u32[]{:S(2)}) async-start(bf16[12,160,512]{2,1,0:T(8,128)(2,1)} %broadcast_in_dim.14), calls=%async_computation | async-start | bytes 3932160 | tf_op jit(solution)/shard_map/all_to_all | solution.py:16
  21.6 93.2 %all-gather.2.cloned.1.call-start = ((), (), s32[]{:S(2)}) async-start(), calls=%async_computation.6 | async-start | bytes 2129920 | tf_op jit(solution)/shard_map/all_gather | solution.py:14
  22.4 135.4 %reduce-scatter.7.cloned.1.call-start = ((), (), s32[]{:S(2)}) async-start(), calls=%async_computation.7 | async-start | bytes 2457600
  114.8 3.8 %copy-start.1 = (bf16[128,512]{1,0:T(8,128)(2,1)S(1)}, bf16[128,512]{1,0:T(8,128)(2,1)}, u32[]{:S(2)}) copy-start(bf16[128,512]{1,0:T(8,128)(2,1)} %param.4) | copy-start | bytes 393220
  116.8 1.9 copy-start
  123.0 101.6 %all-to-all-start.3 = ((bf16[12,128,512]{2,1,0:T(8,128)(2,1)}), bf16[12,128,512]{2,1,0:T(8,128)(2,1)S(1)}, u32[]{:S(2)}, u32[]{:S(2)}) async-start(bf16[12,128,512]{2,1,0:T(8,128)(2,1)} %broadcast_in_dim.15), calls=%async_computation.3 | async-start | bytes 3145728 | tf_op jit(solution)/shard_map/all_to_all | solution.py:19
  129.5 64.4 %copy-start.2 = (bf16[16,1920]{1,0:T(8,128)(2,1)S(1)}, bf16[16,1920]{1,0:T(8,128)(2,1)}, u32[]{:S(2)}) copy-start(bf16[16,1920]{1,0:T(8,128)(2,1)} %param.7) | copy-start | bytes 184324
  129.5 63.5 %reduce-scatter.9.cloned.1.call-start = ((), (), s32[]{:S(2)}) async-start(), calls=%async_computation.8 | async-start | bytes 368640 | tf_op jit(solution)/shard_map/reduce_scatter | solution.py:24
  224.6 17.0 %all-to-all-start.1 = ((f32[8,16,512]{2,1,0:T(8,128)}), f32[8,16,512]{2,1,0:T(8,128)}, u32[]{:S(2)}, u32[]{:S(2)}) async-start(f32[8,16,512]{2,1,0:T(8,128)} %fusion.7), calls=%async_computation.1 | async-start | bytes 524288 | tf_op jit(solution)/shard_map/all_to_all | solution.py:43
  241.7 49.4 %all-to-all-start.2 = ((bf16[12,128,2,160]{1,3,2,0:T(8,128)(2,1)}), bf16[12,128,2,160]{1,3,2,0:T(8,128)(2,1)S(1)}, u32[]{:S(2)}, u32[]{:S(2)}) async-start(bf16[12,128,2,160]{1,3,2,0:T(8,128)(2,1)} %bitcast.23), calls=%async_computation.2 | async-start | bytes 1966080 | tf_op jit(solution)/shard_map/all_to_all | solution.py:46
Sparse Core Ops, SparseCore 0:
  24.9 89.9 all-gather.1
  121.9 35.8 reduce-scatter.6
  160.8 32.0 reduce-scatter.8

commit v4 on v2

--- a/solution.py
+++ b/solution.py
@@ -18,10 +18,7 @@
     hidden_units = weight_pair.shape[1]
     weight_rows = weight_pair.reshape(2 * hidden_units, weight_pair.shape[2])
     partial = jnp.einsum("td,hd->th", tokens, weight_rows, preferred_element_type=jnp.float32)
-    summed = lax.psum_scatter(partial, "x", scatter_dimension=0, tiled=True)
-    summed = lax.psum_scatter(
-        summed.astype(jnp.bfloat16), "zh", scatter_dimension=0, tiled=True
-    ).astype(jnp.float32)
+    summed = lax.psum_scatter(partial, ROW, scatter_dimension=0, tiled=True)
     gate_pre = summed[:, :hidden_units]
     up_pre = summed[:, hidden_units:]
     sigmoid_val = jax.nn.sigmoid(gate_pre)
@@ -33,8 +30,7 @@
     ).astype(jnp.bfloat16)
     grad_up_pre = (upstream * gated).astype(jnp.bfloat16)
     pair_grads = jnp.concatenate([grad_gate_pre, grad_up_pre], 1)
-    gathered = lax.all_gather(pair_grads, "zh", axis=0, tiled=True)
-    gathered = lax.all_gather(gathered, "x", axis=0, tiled=True)
+    gathered = lax.all_gather(pair_grads, ROW, axis=0, tiled=True)
     grad_tokens = lax.psum_scatter(
         jnp.einsum("th,hd->td", gathered, weight_rows, preferred_element_type=jnp.float32),
         "col",

time: 266 us -> 393 us (1.48)
  waiting for transfers between devices: 186 us -> 275 us
  blocking collectives: 29.7 us -> 73.4 us
    reduce_scatter x1, waiting for transfers between devices: 34 us -> 149 us  [body(): summed = lax.psum_scatter(partial, ROW, scatter_dimension=0, tiled=True)]
    all_gather x2 -> x1, blocking collectives: 29.7 us -> 73.4 us  [body(): gathered = lax.all_gather(pair_grads, ROW, axis=0, tiled=True)]
    unnamed x5 -> x3, waiting for transfers between devices: 26 us -> 0.05 us
  transfers between devices with their start and end apart: 6 -> 5, of which waited for: 4 -> 3; matrix products, arithmetic and copies ran while one was open for 5% -> 2% of each run, Pallas kernels for 0% -> 0%
where the time goes in v4:
time: 393 us
  waiting for transfers between devices  275 us (70%)
  blocking collectives  73.4 us (19%)
  between operations  13.8 us (4%)
  starting transfers between devices  12.1 us (3%)
  matrix products  7.99 us (2%)
  local copies, waits for them, and re-layouts  5.54 us (1%)
  other arithmetic  4.83 us (1%)
    reduce_scatter x1, waiting for transfers between devices, body(): summed = lax.psum_scatter(partial, ROW, scatter_dimension=0, tiled=True)  149 us
    all_gather x1, waiting for transfers between devices, body(): weight_pair = lax.all_gather(pair, REP, axis=1, tiled=True)  84.8 us
    all_gather x1, blocking collectives, body(): gathered = lax.all_gather(pair_grads, ROW, axis=0, tiled=True)  73.4 us
    reduce_scatter x1, waiting for transfers between devices, body(): lax.psum_scatter(jnp.einsum('th,hd->td', gathered, weight_rows, preferred...  40.6 us
  transfers between devices with their start and end apart: 5, of which 3 were waited for; matrix products, arithmetic and copies ran while one was open for 2% of the time, Pallas kernels for 0%

profile of v4, /device:TPU:6, one launch (start us, length us, event | category | flops | bytes accessed | tf_op | source)
XLA Modules:
  0.0 392.7 jit_solution(8406739948470334438)
XLA Ops:
  7.2 0.0 all-gather.2.cloned.1.call-start
  7.2 1.7 pad_maximum_fusion
  8.9 0.0 all-gather.2.cloned.1.call-update
  9.0 0.0 reduce-scatter.7.cloned.1.call-start
  9.0 84.8 %all-gather.2.cloned.1.call-done = bf16[2,1920,512]{2,1,0:T(8,128)(2,1)} async-done(((bf16[2,160,512]{2,1,0:T(8,128)(2,1)}), bf16[2,1920,512]{2,1,0:T(8,128)(2,1)}) %all-gather.2.cloned.1.call-update) | async-done | bytes 3932176 | tf_op jit(solution)/shard_map/all_gather | solution.py:15
  93.8 3.3 convolution_bitcast_fusion
  97.1 0.0 copy-start
  97.1 1.8 copy.26
  98.9 0.0 copy-start.1
  98.9 0.0 reduce-scatter.7.cloned.1.call-update
  99.0 0.0 copy-done
  99.0 1.3 broadcast_in_dim.2
  100.3 6.1 %all-to-all-start.1 = ((bf16[12,128,512]{2,1,0:T(8,128)(2,1)}), bf16[12,128,512]{2,1,0:T(8,128)(2,1)S(1)}, u32[]{:S(2)}, u32[]{:S(2)}) async-start(bf16[12,128,512]{2,1,0:T(8,128)(2,1)} %broadcast_in_dim.2), calls=%async_computation.2 | async-start | bytes 3145728 | tf_op jit(solution)/shard_map/all_to_all | solution.py:17
  106.3 149.5 %reduce-scatter.7.cloned.1.call-done = f32[16,3840]{1,0:T(8,128)} async-done(((f32[128,3840]{1,0:T(8,128)}), f32[16,3840]{1,0:T(8,128)}) %reduce-scatter.7.cloned.1.call-update) | async-done | bytes 245776 | tf_op jit(solution)/shard_map/reduce_scatter | solution.py:21
  255.8 0.0 copy-done.1
  255.8 1.7 fusion.3
  257.5 73.4 %all_gather.7 = bf16[128,3840]{1,0:T(8,128)(2,1)S(1)} all-gather(bf16[16,3840]{1,0:T(8,128)(2,1)S(1)} %pad_maximum_fusion.1), channel_id=1, replica_groups=mesh['zl'=6,'core'=2,'x'=4,'zh'=2,'col'=8] {'x','zh'}, dimensions={0}, use_global_device_ids=true | all-gather | bytes 1105920 | tf_op jit(solution)/shard_map/all_gather | solution.py:33
  330.9 0.6 copy.23
  331.6 1.0 copy.29
  332.6 0.0 all-to-all-done.1
  332.6 5.9 %all-to-all-start = ((bf16[12,128,2,160]{1,3,2,0:T(8,128)(2,1)}), bf16[12,128,2,160]{1,3,2,0:T(8,128)(2,1)S(1)}, u32[]{:S(2)}, u32[]{:S(2)}) async-start(bf16[12,128,2,160]{1,3,2,0:T(8,128)(2,1)} %bitcast.17), calls=%async_computation.1 | async-start | bytes 1966080 | tf_op jit(solution)/shard_map/all_to_all | solution.py:42
  338.6 0.0 reduce-scatter.5.cloned.1.call-start
  338.6 3.5 fusion.7
  342.2 0.0 reduce-scatter.5.cloned.1.call-update
  342.2 40.6 %reduce-scatter.5.cloned.1.call-done = f32[16,512]{1,0:T(8,128)} async-done(((f32[128,512]{1,0:T(8,128)}), f32[16,512]{1,0:T(8,128)}) %reduce-scatter.5.cloned.1.call-update) | async-done | bytes 32784 | tf_op jit(solution)/shard_map/reduce_scatter | solution.py:34
  382.8 1.4 convert_element_type.21
  384.1 0.0 all-to-all-done
  384.1 1.2 reduce-precision_reduce_fusion
  385.3 0.1 multiply_convert_fusion
  385.4 0.7 fusion.6
  (1 shorter events, 0.0 us)
Async XLA Ops:
  7.2 86.6 %all-gather.2.cloned.1.call-start = ((), (), s32[]{:S(2)}) async-start(), calls=%async_computation.4 | async-start | bytes 4259840 | tf_op jit(solution)/shard_map/all_gather | solution.py:15
  9.0 246.9 %reduce-scatter.7.cloned.1.call-start = ((), (), s32[]{:S(2)}) async-start(), calls=%async_computation.6 | async-start | bytes 2211840 | tf_op jit(solution)/shard_map/reduce_scatter | solution.py:21
  97.1 1.8 copy-start
  98.9 156.9 %copy-start.1 = (bf16[16,1920]{1,0:T(8,128)(2,1)S(1)}, bf16[16,1920]{1,0:T(8,128)(2,1)}, u32[]{:S(2)}) copy-start(bf16[16,1920]{1,0:T(8,128)(2,1)} %param.7) | copy-start | bytes 184324
  100.3 232.4 %all-to-all-start.1 = ((bf16[12,128,512]{2,1,0:T(8,128)(2,1)}), bf16[12,128,512]{2,1,0:T(8,128)(2,1)S(1)}, u32[]{:S(2)}, u32[]{:S(2)}) async-start(bf16[12,128,512]{2,1,0:T(8,128)(2,1)} %broadcast_in_dim.2), calls=%async_computation.2 | async-start | bytes 3145728 | tf_op jit(solution)/shard_map/all_to_all | solution.py:17
  332.6 51.5 %all-to-all-start = ((bf16[12,128,2,160]{1,3,2,0:T(8,128)(2,1)}), bf16[12,128,2,160]{1,3,2,0:T(8,128)(2,1)S(1)}, u32[]{:S(2)}, u32[]{:S(2)}) async-start(bf16[12,128,2,160]{1,3,2,0:T(8,128)(2,1)} %bitcast.17), calls=%async_computation.1 | async-start | bytes 1966080 | tf_op jit(solution)/shard_map/all_to_all | solution.py:42
  338.6 44.2 %reduce-scatter.5.cloned.1.call-start = ((), (), s32[]{:S(2)}) async-start(), calls=%async_computation.5 | async-start | bytes 294912 | tf_op jit(solution)/shard_map/reduce_scatter | solution.py:34
Sparse Core Ops, SparseCore 0:
  10.4 83.3 all-gather.1
  99.1 156.7 reduce-scatter.6
  342.5 40.2 reduce-scatter.4

commit v5 on v4

--- a/solution.py
+++ b/solution.py
@@ -18,19 +18,30 @@
     hidden_units = weight_pair.shape[1]
     weight_rows = weight_pair.reshape(2 * hidden_units, weight_pair.shape[2])
     partial = jnp.einsum("td,hd->th", tokens, weight_rows, preferred_element_type=jnp.float32)
-    summed = lax.psum_scatter(partial, ROW, scatter_dimension=0, tiled=True)
+    swap = [(0, 1), (1, 0)]
+    upper = lax.axis_index("zh")
+    partner_cot = lax.ppermute(cotangent, "zh", swap)
+    summed = lax.psum_scatter(partial, "x", scatter_dimension=0, tiled=True)
+    summed = summed + lax.ppermute(summed.astype(jnp.bfloat16), "zh", swap).astype(jnp.float32)
     gate_pre = summed[:, :hidden_units]
     up_pre = summed[:, hidden_units:]
     sigmoid_val = jax.nn.sigmoid(gate_pre)
     gated = gate_pre * sigmoid_val
     hidden = (gated * up_pre).astype(jnp.bfloat16)
-    upstream = cotangent.astype(jnp.float32)
+    pair_cot = jnp.where(
+        upper == 0,
+        jnp.concatenate([cotangent, partner_cot], 0),
+        jnp.concatenate([partner_cot, cotangent], 0),
+    )
+    upstream = pair_cot.astype(jnp.float32)
     grad_gate_pre = (
         upstream * up_pre * sigmoid_val * (1.0 + gate_pre * (1.0 - sigmoid_val))
     ).astype(jnp.bfloat16)
     grad_up_pre = (upstream * gated).astype(jnp.bfloat16)
     pair_grads = jnp.concatenate([grad_gate_pre, grad_up_pre], 1)
-    gathered = lax.all_gather(pair_grads, ROW, axis=0, tiled=True)
+    gathered = lax.all_gather(pair_grads, "x", axis=0, tiled=True)
+    own_rows = cotangent.shape[0]
+    hidden = lax.dynamic_slice_in_dim(hidden, upper * own_rows, own_rows, 0)
     grad_tokens = lax.psum_scatter(
         jnp.einsum("th,hd->td", gathered, weight_rows, preferred_element_type=jnp.float32),
         "col",

time: 393 us -> 261 us (0.66)
  waiting for transfers between devices: 275 us -> 163 us
  blocking collectives: 73.4 us -> 14.7 us
  starting transfers between devices: 12.1 us -> 47.2 us
    reduce_scatter x1, waiting for transfers between devices: 149 us -> 26 us  [body(): summed = lax.psum_scatter(partial, 'x', scatter_dimension=0, tiled=True)]
    all_gather x1, blocking collectives: 73.4 us -> 14.7 us  [body(): gathered = lax.all_gather(pair_grads, 'x', axis=0, tiled=True)]
    all_to_all x1, starting transfers between devices: 5.94 us -> 28.4 us  [body(): owned = lax.all_to_all(by_owner, REP, 0, 0, tiled=True)]
    ppermute x0 -> x2, starting transfers between devices: none -> 12.7 us  [the longest x1 10.8 us: body(): lax.ppermute(summed.astype(jnp.bfloat16), 'zh', swap).astype(jnp.float32)]
    ppermute x0 -> x2, waiting for transfers between devices: none -> 12.5 us  [the longest x1 8.44 us: body(): lax.ppermute(summed.astype(jnp.bfloat16), 'zh', swap).astype(jnp.float32)]
  transfers between devices with their start and end apart: 5 -> 7, of which waited for: 3 -> 5; matrix products, arithmetic and copies ran while one was open for 2% -> 5% of each run, Pallas kernels for 0% -> 0%
where the time goes in v5:
time: 261 us; the launch traced here: 260 us
  waiting for transfers between devices  163 us (62%)
  starting transfers between devices  47.2 us (18%)
  blocking collectives  14.7 us (6%)
  between operations  13.9 us (5%)
  matrix products  7.98 us (3%)
  other arithmetic  7.76 us (3%)
  local copies, waits for them, and re-layouts  5.6 us (2%)
    all_gather x1, waiting for transfers between devices, body(): weight_pair = lax.all_gather(pair, REP, axis=1, tiled=True)  84.8 us
    reduce_scatter x1, waiting for transfers between devices, body(): lax.psum_scatter(jnp.einsum('th,hd->td', gathered, weight_rows, preferred...  39.5 us
    all_to_all x1, starting transfers between devices, body(): owned = lax.all_to_all(by_owner, REP, 0, 0, tiled=True)  28.4 us
    reduce_scatter x1, waiting for transfers between devices, body(): summed = lax.psum_scatter(partial, 'x', scatter_dimension=0, tiled=True)  26 us
    all_gather x1, blocking collectives, body(): gathered = lax.all_gather(pair_grads, 'x', axis=0, tiled=True)  14.7 us
    ppermute x1, starting transfers between devices, body(): lax.ppermute(summed.astype(jnp.bfloat16), 'zh', swap).astype(jnp.float32)  10.8 us
    ppermute x1, waiting for transfers between devices, body(): lax.ppermute(summed.astype(jnp.bfloat16), 'zh', swap).astype(jnp.float32)  8.44 us
    all_to_all x1, starting transfers between devices, body(): all_tokens = lax.all_to_all(copies, REP, 0, 0, tiled=True)  6.06 us
  transfers between devices with their start and end apart: 7, of which 5 were waited for; matrix products, arithmetic and copies ran while one was open for 5% of the time, Pallas kernels for 0%

profile of v5, /device:TPU:6, one launch (start us, length us, event | category | flops | bytes accessed | tf_op | source)
XLA Modules:
  0.0 260.0 jit_solution(5472994762123865016)
XLA Ops:
  7.2 0.0 all-gather.2.cloned.1.call-start
  7.2 1.7 pad_maximum_fusion
  8.9 0.0 all-gather.2.cloned.1.call-update
  9.0 0.0 reduce-scatter.7.cloned.1.call-start
  9.0 84.8 %all-gather.2.cloned.1.call-done = bf16[2,1920,512]{2,1,0:T(8,128)(2,1)} async-done(((bf16[2,160,512]{2,1,0:T(8,128)(2,1)}), bf16[2,1920,512]{2,1,0:T(8,128)(2,1)}) %all-gather.2.cloned.1.call-update) | async-done | bytes 3932176 | tf_op jit(solution)/shard_map/all_gather | solution.py:15
  93.8 3.3 %convolution_bitcast_fusion = f32[128,3840]{0,1:T(8,128)S(1)} fusion(bf16[3840,512]{1,0:T(8,128)(2,1)} %bitcast.18, bf16[128,512]{1,0:T(8,128)(2,1)} %param.4), kind=kOutput, calls=%fused_computation.1 | convolution fusion | flops 503316480 | bytes 6029312 | tf_op jit(solution)/shard_map/td,hd->th/dot_general | solution.py:20
  97.1 0.0 copy-start
  97.1 1.9 copy.34
  99.0 0.0 copy-start.1
  99.0 0.0 reduce-scatter.7.cloned.1.call-update
  99.0 0.0 copy-done
  99.0 1.3 broadcast_in_dim.2
  100.3 6.1 %all-to-all-start.1 = ((bf16[12,128,512]{2,1,0:T(8,128)(2,1)}), bf16[12,128,512]{2,1,0:T(8,128)(2,1)S(1)}, u32[]{:S(2)}, u32[]{:S(2)}) async-start(bf16[12,128,512]{2,1,0:T(8,128)(2,1)} %broadcast_in_dim.2), calls=%async_computation.2 | async-start | bytes 3145728 | tf_op jit(solution)/shard_map/all_to_all | solution.py:17
  106.4 26.0 %reduce-scatter.7.cloned.1.call-done = f32[32,3840]{1,0:T(8,128)} async-done(((f32[128,3840]{1,0:T(8,128)}), f32[32,3840]{1,0:T(8,128)}) %reduce-scatter.7.cloned.1.call-update) | async-done | bytes 491536 | tf_op jit(solution)/shard_map/reduce_scatter | solution.py:24
  132.4 1.1 convert_element_type.23
  133.5 10.8 %collective-permute-start = (bf16[32,3840]{1,0:T(8,128)(2,1)S(1)}, bf16[32,3840]{1,0:T(8,128)(2,1)S(1)}, u32[]{:S(2)}, u32[]{:S(2)}) collective-permute-start(bf16[32,3840]{1,0:T(8,128)(2,1)S(1)} %convert_element_type.23), channel_id=1, source_target_pairs={{0,8},{8,0},{1,9},{9,1},{2,10},{10,2},{3,11},{11,3},{4,12},{12,4},... | collective-permute-start | bytes 737288 | tf_op jit(solution)/shard_map/ppermute | solution.py:25
  144.3 0.0 copy-done.1
  144.3 1.9 collective-permute-start.1
  146.2 8.4 %collective-permute-done = bf16[32,3840]{1,0:T(8,128)(2,1)S(1)} collective-permute-done((bf16[32,3840]{1,0:T(8,128)(2,1)S(1)}, bf16[32,3840]{1,0:T(8,128)(2,1)S(1)}, u32[]{:S(2)}, u32[]{:S(2)}) %collective-permute-start) | collective-permute-done | bytes 245792 | tf_op jit(solution)/shard_map/ppermute | solution.py:25
  154.6 1.1 convert_add_fusion
  155.7 4.0 %collective-permute-done.1 = bf16[16,1920]{1,0:T(8,128)(2,1)S(1)} collective-permute-done((bf16[16,1920]{1,0:T(8,128)(2,1)S(1)}, bf16[16,1920]{1,0:T(8,128)(2,1)S(1)}, u32[]{:S(2)}, u32[]{:S(2)}) %collective-permute-start.1) | collective-permute-done | bytes 61472 | tf_op jit(solution)/shard_map/ppermute | solution.py:23
  159.7 0.9 fusion.3
  160.6 14.7 %all_gather.7 = bf16[128,3840]{1,0:T(8,128)(2,1)S(1)} all-gather(bf16[32,3840]{1,0:T(8,128)(2,1)S(1)} %pad_maximum_fusion.1), channel_id=1, replica_groups=mesh['zl'=6,'core'=2,'x'=4,'zh'=2,'col'=8] {'x'}, dimensions={0}, use_global_device_ids=true | all-gather | bytes 1228800 | tf_op jit(solution)/shard_map/all_gather | solution.py:42
  175.3 0.6 copy.31
  176.0 1.0 copy.37
  177.0 0.0 all-to-all-done.1
  177.0 28.4 %all-to-all-start = ((bf16[12,128,2,160]{1,3,2,0:T(8,128)(2,1)}), bf16[12,128,2,160]{1,3,2,0:T(8,128)(2,1)S(1)}, u32[]{:S(2)}, u32[]{:S(2)}) async-start(bf16[12,128,2,160]{1,3,2,0:T(8,128)(2,1)} %bitcast.17), calls=%async_computation.1 | async-start | bytes 1966080 | tf_op jit(solution)/shard_map/all_to_all | solution.py:53
  205.4 0.0 reduce-scatter.5.cloned.1.call-start
  205.4 3.5 %fusion.8 = f32[128,512]{1,0:T(8,128)} fusion(bf16[128,3840]{1,0:T(8,128)(2,1)S(1)} %all_gather.7, bf16[3840,512]{1,0:T(8,128)(2,1)} %bitcast.19), kind=kOutput, calls=%fused_computation.20 | convolution fusion | flops 503316480 | bytes 5177344 | tf_op jit(solution)/shard_map/th,hd->td/dot_general | solution.py:46
  209.0 0.0 reduce-scatter.5.cloned.1.call-update
  209.0 1.6 fusion.6
  210.6 39.5 %reduce-scatter.5.cloned.1.call-done = f32[16,512]{1,0:T(8,128)} async-done(((f32[128,512]{1,0:T(8,128)}), f32[16,512]{1,0:T(8,128)}) %reduce-scatter.5.cloned.1.call-update) | async-done | bytes 32784 | tf_op jit(solution)/shard_map/reduce_scatter | solution.py:45
  250.1 1.4 convert_element_type.29
  251.5 0.0 all-to-all-done
  251.5 1.2 reduce-precision_reduce_fusion
  252.6 0.1 multiply_convert_fusion
  252.7 0.7 fusion.7
  (1 shorter events, 0.0 us)
Async XLA Ops:
  7.2 86.6 %all-gather.2.cloned.1.call-start = ((), (), s32[]{:S(2)}) async-start(), calls=%async_computation.4 | async-start | bytes 4259840 | tf_op jit(solution)/shard_map/all_gather | solution.py:15
  9.0 123.4 %reduce-scatter.7.cloned.1.call-start = ((), (), s32[]{:S(2)}) async-start(), calls=%async_computation.6 | async-start | bytes 2457600 | tf_op jit(solution)/shard_map/reduce_scatter | solution.py:24
  97.1 1.9 copy-start
  99.0 45.3 %copy-start.1 = (bf16[16,1920]{1,0:T(8,128)(2,1)S(1)}, bf16[16,1920]{1,0:T(8,128)(2,1)}, u32[]{:S(2)}) copy-start(bf16[16,1920]{1,0:T(8,128)(2,1)} %param.7) | copy-start | bytes 184324
  100.3 76.7 %all-to-all-start.1 = ((bf16[12,128,512]{2,1,0:T(8,128)(2,1)}), bf16[12,128,512]{2,1,0:T(8,128)(2,1)S(1)}, u32[]{:S(2)}, u32[]{:S(2)}) async-start(bf16[12,128,512]{2,1,0:T(8,128)(2,1)} %broadcast_in_dim.2), calls=%async_computation.2 | async-start | bytes 3145728 | tf_op jit(solution)/shard_map/all_to_all | solution.py:17
  133.5 21.2 %collective-permute-start = (bf16[32,3840]{1,0:T(8,128)(2,1)S(1)}, bf16[32,3840]{1,0:T(8,128)(2,1)S(1)}, u32[]{:S(2)}, u32[]{:S(2)}) collective-permute-start(bf16[32,3840]{1,0:T(8,128)(2,1)S(1)} %convert_element_type.23), channel_id=1, source_target_pairs={{0,8},{8,0},{1,9},{9,1},{2,10},{10,2},{3,11},{11,3},{4,12},{12,4},... | collective-permute-start | bytes 737288 | tf_op jit(solution)/shard_map/ppermute | solution.py:25
  144.3 15.5 %collective-permute-start.1 = (bf16[16,1920]{1,0:T(8,128)(2,1)S(1)}, bf16[16,1920]{1,0:T(8,128)(2,1)S(1)}, u32[]{:S(2)}, u32[]{:S(2)}) collective-permute-start(bf16[16,1920]{1,0:T(8,128)(2,1)S(1)} %copy-done.1), channel_id=1, source_target_pairs={{0,8},{8,0},{1,9},{9,1},{2,10},{10,2},{3,11},{11,3},{4,12},{12,4},... | collective-permute-start | bytes 184328 | tf_op jit(solution)/shard_map/ppermute | solution.py:23
  177.0 74.4 %all-to-all-start = ((bf16[12,128,2,160]{1,3,2,0:T(8,128)(2,1)}), bf16[12,128,2,160]{1,3,2,0:T(8,128)(2,1)S(1)}, u32[]{:S(2)}, u32[]{:S(2)}) async-start(bf16[12,128,2,160]{1,3,2,0:T(8,128)(2,1)} %bitcast.17), calls=%async_computation.1 | async-start | bytes 1966080 | tf_op jit(solution)/shard_map/all_to_all | solution.py:53
  205.4 44.7 %reduce-scatter.5.cloned.1.call-start = ((), (), s32[]{:S(2)}) async-start(), calls=%async_computation.5 | async-start | bytes 294912 | tf_op jit(solution)/shard_map/reduce_scatter | solution.py:45
Sparse Core Ops, SparseCore 0:
  10.4 83.3 all-gather.1
  99.1 33.2 reduce-scatter.6
  209.3 40.7 reduce-scatter.4

commit v6 on v5

--- a/solution.py
+++ b/solution.py
@@ -6,6 +6,25 @@
 
 REP = ("zl", "core")
 ROW = ("x", "zh")
+
+
+def ring_reduce_scatter(values, axis):
+    n = lax.axis_size(axis)
+    i = lax.axis_index(axis)
+    blocks = values.reshape(n, values.shape[0] // n, values.shape[1])
+    half = values.shape[1] // 2
+    forward = [(j, (j + 1) % n) for j in range(n)]
+    backward = [(j, (j - 1) % n) for j in range(n)]
+
+    def own(block, lo):
+        return lax.dynamic_index_in_dim(blocks, block % n, 0, keepdims=False)[:, lo:lo + half]
+
+    right = own(i + n - 1, 0)
+    left = own(i + 1, half)
+    for step in range(n - 1):
+        right = lax.ppermute(right, axis, forward) + own(i + 2 * n - 2 - step, 0)
+        left = lax.ppermute(left, axis, backward) + own(i + 2 + step, half)
+    return jnp.concatenate([right, left], 1)
 
 
 def body(tokens, gate_weight, up_weight, cotangent):
@@ -21,7 +40,7 @@
     swap = [(0, 1), (1, 0)]
     upper = lax.axis_index("zh")
     partner_cot = lax.ppermute(cotangent, "zh", swap)
-    summed = lax.psum_scatter(partial, "x", scatter_dimension=0, tiled=True)
+    summed = ring_reduce_scatter(partial, "x")
     summed = summed + lax.ppermute(summed.astype(jnp.bfloat16), "zh", swap).astype(jnp.float32)
     gate_pre = summed[:, :hidden_units]
     up_pre = summed[:, hidden_units:]

time: 261 us -> 292 us (1.12)
  starting transfers between devices: 47.2 us -> 66 us
  waiting for transfers between devices: 163 us -> 178 us
    ppermute x0 -> x6, waiting for transfers between devices: none -> 27.4 us  [the longest x3 18.1 us: ring_reduce_scatter(): left = lax.ppermute(left, axis, backward) + own(i + 2 + step, half)]
    reduce_scatter x1 -> x0, waiting for transfers between devices: 26 us -> none  [body(): summed = lax.psum_scatter(partial, 'x', scatter_dimension=0, tiled=True)]
    ppermute x1, waiting for transfers between devices: 8.44 us -> 24.5 us  [body(): lax.ppermute(summed.astype(jnp.bfloat16), 'zh', swap).astype(jnp.float32)]
    ppermute x0 -> x6, starting transfers between devices: none -> 16 us  [the longest x3 8.4 us: ring_reduce_scatter(): left = lax.ppermute(left, axis, backward) + own(i + 2 + step, half)]
    all_to_all x1, starting transfers between devices: 28.4 us -> 34.1 us  [body(): owned = lax.all_to_all(by_owner, REP, 0, 0, tiled=True)]
    ppermute x1, waiting for transfers between devices: 4.02 us -> 1.08 us  [body(): partner_cot = lax.ppermute(cotangent, 'zh', swap)]
  transfers between devices with their start and end apart: 7 -> 12, of which waited for: 5 -> 10; matrix products, arithmetic and copies ran while one was open for 5% -> 4% of each run, Pallas kernels for 0% -> 0%
where the time goes in v6:
time: 292 us; the launch traced here: 291 us
  waiting for transfers between devices  178 us (61%)
  starting transfers between devices  66 us (23%)
  blocking collectives  14.8 us (5%)
  between operations  14.3 us (5%)
  matrix products  8.16 us (3%)
  other arithmetic  5.95 us (2%)
  local copies, waits for them, and re-layouts  4.02 us (1%)
    all_gather x1, waiting for transfers between devices, body(): weight_pair = lax.all_gather(pair, REP, axis=1, tiled=True)  84.7 us
    reduce_scatter x1, waiting for transfers between devices, body(): lax.psum_scatter(jnp.einsum('th,hd->td', gathered, weight_rows, preferred...  39.6 us
    all_to_all x1, starting transfers between devices, body(): owned = lax.all_to_all(by_owner, REP, 0, 0, tiled=True)  34.1 us
    ppermute x1, waiting for transfers between devices, body(): lax.ppermute(summed.astype(jnp.bfloat16), 'zh', swap).astype(jnp.float32)  24.5 us
    ppermute x3, waiting for transfers between devices, ring_reduce_scatter(): left = lax.ppermute(left, axis, backward) + own(i + 2 + step, half)  18.1 us
    all_gather x1, blocking collectives, body(): gathered = lax.all_gather(pair_grads, 'x', axis=0, tiled=True)  14.8 us
    ppermute x3, waiting for transfers between devices, ring_reduce_scatter(): right = lax.ppermute(right, axis, forward) + own(i + 2 * n - 2 - step, 0)  9.38 us
    ppermute x1, starting transfers between devices, body(): lax.ppermute(summed.astype(jnp.bfloat16), 'zh', swap).astype(jnp.float32)  9.38 us
  transfers between devices with their start and end apart: 12, of which 10 were waited for; matrix products, arithmetic and copies ran while one was open for 4% of the time, Pallas kernels for 0%

profile of v6, /device:TPU:6, one launch (start us, length us, event | category | flops | bytes accessed | tf_op | source)
XLA Modules:
  0.0 290.9 jit_solution(12810723881703378348)
XLA Ops:
  7.2 0.0 all-gather.2.cloned.1.call-start
  7.2 1.7 pad_maximum_fusion.1
  9.0 0.0 all-gather.2.cloned.1.call-update
  9.1 84.7 %all-gather.2.cloned.1.call-done = bf16[2,1920,512]{2,1,0:T(8,128)(2,1)} async-done(((bf16[2,160,512]{2,1,0:T(8,128)(2,1)}), bf16[2,1920,512]{2,1,0:T(8,128)(2,1)}) %all-gather.2.cloned.1.call-update) | async-done | bytes 3932176 | tf_op jit(solution)/shard_map/all_gather | solution.py:34
  93.8 3.5 %fusion.10 = f32[3840,128]{0,1:T(8,128)S(1)} fusion(bf16[3840,512]{1,0:T(8,128)(2,1)} %bitcast.30, bf16[128,512]{1,0:T(8,128)(2,1)} %param.4), kind=kOutput, calls=%fused_computation.34 | convolution fusion | flops 503316480 | bytes 6029312 | tf_op jit(solution)/shard_map/td,hd->th/dot_general | solution.py:39
  97.3 0.0 copy-start
  97.3 0.2 dynamic-slice_bitcast_fusion.3
  97.6 2.8 collective-permute-start.3
  100.4 6.5 %collective-permute-done.3 = f32[32,1920]{1,0:T(8,128)S(1)} collective-permute-done((f32[32,1920]{1,0:T(8,128)S(1)}, f32[32,1920]{1,0:T(8,128)S(1)}, u32[]{:S(2)}, u32[]{:S(2)}) %collective-permute-start.3) | collective-permute-done | bytes 245792 | tf_op jit(solution)/shard_map/ppermute | solution.py:26
  106.9 1.9 collective-permute-start.4
  108.8 7.4 %collective-permute-done.4 = f32[32,1920]{1,0:T(8,128)S(1)} collective-permute-done((f32[32,1920]{1,0:T(8,128)S(1)}, f32[32,1920]{1,0:T(8,128)S(1)}, u32[]{:S(2)}, u32[]{:S(2)}) %collective-permute-start.4) | collective-permute-done | bytes 245792 | tf_op jit(solution)/shard_map/ppermute | solution.py:26
  116.3 1.9 collective-permute-start
  118.2 7.1 %collective-permute-done = f32[32,1920]{1,0:T(8,128)S(1)} collective-permute-done((f32[32,1920]{1,0:T(8,128)S(1)}, f32[32,1920]{1,0:T(8,128)S(1)}, u32[]{:S(2)}, u32[]{:S(2)}) %collective-permute-start) | collective-permute-done | bytes 245792 | tf_op jit(solution)/shard_map/ppermute | solution.py:25
  125.4 0.0 copy-start.1
  125.4 2.3 collective-permute-start.1
  127.7 0.0 copy-done
  127.7 1.3 broadcast_in_dim.2
  129.0 3.7 %all-to-all-start.1 = ((bf16[12,128,512]{2,1,0:T(8,128)(2,1)}), bf16[12,128,512]{2,1,0:T(8,128)(2,1)S(1)}, u32[]{:S(2)}, u32[]{:S(2)}) async-start(bf16[12,128,512]{2,1,0:T(8,128)(2,1)} %broadcast_in_dim.2), calls=%async_computation.2 | async-start | bytes 3145728 | tf_op jit(solution)/shard_map/all_to_all | solution.py:36
  132.7 3.7 %collective-permute-start.5 = (f32[32,1920]{1,0:T(8,128)S(1)}, f32[32,1920]{1,0:T(8,128)S(1)}, u32[]{:S(2)}, u32[]{:S(2)}) collective-permute-start(f32[32,1920]{1,0:T(8,128)S(1)} %get-tuple-element.21), channel_id=1, source_target_pairs={{0,48},{16,0},{32,16},{48,32},{1,49},{17,1},{33,17},{49,33},{2,50}... | collective-permute-start | bytes 737288 | tf_op jit(solution)/shard_map/ppermute | solution.py:26
  136.4 0.0 collective-permute-done.1
  136.5 3.4 %collective-permute-start.2 = (f32[32,1920]{1,0:T(8,128)S(1)}, f32[32,1920]{1,0:T(8,128)S(1)}, u32[]{:S(2)}, u32[]{:S(2)}) collective-permute-start(f32[32,1920]{1,0:T(8,128)S(1)} %slice_add_fusion.4), channel_id=1, source_target_pairs={{0,16},{16,32},{32,48},{48,0},{1,17},{17,33},{33,49},{49,1},{2,18}... | collective-permute-start | bytes 737288 | tf_op jit(solution)/shard_map/ppermute | solution.py:25
  139.8 4.2 %collective-permute-done.5 = f32[32,1920]{1,0:T(8,128)S(1)} collective-permute-done((f32[32,1920]{1,0:T(8,128)S(1)}, f32[32,1920]{1,0:T(8,128)S(1)}, u32[]{:S(2)}, u32[]{:S(2)}) %collective-permute-start.5) | collective-permute-done | bytes 245792 | tf_op jit(solution)/shard_map/ppermute | solution.py:26
  144.0 2.2 collective-permute-done.2
  146.3 0.1 slice_add_fusion.3
  146.4 9.4 %collective-permute-start.6 = (bf16[32,3840]{1,0:T(8,128)(2,1)S(1)}, bf16[32,3840]{1,0:T(8,128)(2,1)S(1)}, u32[]{:S(2)}, u32[]{:S(2)}) collective-permute-start(bf16[32,3840]{1,0:T(8,128)(2,1)S(1)} %fusion.1), channel_id=1, source_target_pairs={{0,8},{8,0},{1,9},{9,1},{2,10},{10,2},{3,11},{11,3},{4,12},{12,4},... | collective-permute-start | bytes 737288 | tf_op jit(solution)/shard_map/ppermute | solution.py:44
  155.8 0.0 copy-done.1
  155.8 2.8 collective-permute-start.7
  158.6 24.5 %collective-permute-done.6 = bf16[32,3840]{1,0:T(8,128)(2,1)S(1)} collective-permute-done((bf16[32,3840]{1,0:T(8,128)(2,1)S(1)}, bf16[32,3840]{1,0:T(8,128)(2,1)S(1)}, u32[]{:S(2)}, u32[]{:S(2)}) %collective-permute-start.6) | collective-permute-done | bytes 245792 | tf_op jit(solution)/shard_map/ppermute | solution.py:44
  183.1 1.1 collective-permute-done.7
  184.2 0.9 fusion.4
  185.1 14.8 %all_gather.7 = bf16[128,3840]{1,0:T(8,128)(2,1)S(1)} all-gather(bf16[32,3840]{1,0:T(8,128)(2,1)S(1)} %pad_maximum_fusion.2), channel_id=1, replica_groups=mesh['zl'=6,'core'=2,'x'=4,'zh'=2,'col'=8] {'x'}, dimensions={0}, use_global_device_ids=true | all-gather | bytes 1228800 | tf_op jit(solution)/shard_map/all_gather | solution.py:61
  199.8 0.6 copy.19
  200.5 1.1 copy.23
  201.5 0.3 all-to-all-done.1
  201.9 34.1 %all-to-all-start = ((bf16[12,128,2,160]{1,3,2,0:T(8,128)(2,1)}), bf16[12,128,2,160]{1,3,2,0:T(8,128)(2,1)S(1)}, u32[]{:S(2)}, u32[]{:S(2)}) async-start(bf16[12,128,2,160]{1,3,2,0:T(8,128)(2,1)} %bitcast.29), calls=%async_computation.1 | async-start | bytes 1966080 | tf_op jit(solution)/shard_map/all_to_all | solution.py:72
  236.0 0.0 reduce-scatter.2.cloned.1.call-start
  236.0 3.5 %fusion.11 = f32[128,512]{1,0:T(8,128)} fusion(bf16[128,3840]{1,0:T(8,128)(2,1)S(1)} %all_gather.7, bf16[3840,512]{1,0:T(8,128)(2,1)} %bitcast.31), kind=kOutput, calls=%fused_computation.35 | convolution fusion | flops 503316480 | bytes 5177344 | tf_op jit(solution)/shard_map/th,hd->td/dot_general | solution.py:65
  239.5 0.0 reduce-scatter.2.cloned.1.call-update
  239.5 1.6 fusion.7
  241.1 39.6 %reduce-scatter.2.cloned.1.call-done = f32[16,512]{1,0:T(8,128)} async-done(((f32[128,512]{1,0:T(8,128)}), f32[16,512]{1,0:T(8,128)}) %reduce-scatter.2.cloned.1.call-update) | async-done | bytes 32784 | tf_op jit(solution)/shard_map/reduce_scatter | solution.py:64
  280.7 1.4 convert_element_type.29
  282.1 0.0 all-to-all-done
  282.1 1.2 reduce-precision_reduce_fusion
  283.3 0.1 multiply_convert_fusion
  283.3 0.7 fusion.9
  (8 shorter events, 0.2 us)
Async XLA Ops:
  7.2 86.6 %all-gather.2.cloned.1.call-start = ((), (), s32[]{:S(2)}) async-start(), calls=%async_computation.3 | async-start | bytes 4259840 | tf_op jit(solution)/shard_map/all_gather | solution.py:34
  97.3 30.4 %copy-start = (bf16[128,512]{1,0:T(8,128)(2,1)S(1)}, bf16[128,512]{1,0:T(8,128)(2,1)}, u32[]{:S(2)}) copy-start(bf16[128,512]{1,0:T(8,128)(2,1)} %param.4) | copy-start | bytes 393220
  97.6 9.3 %collective-permute-start.3 = (f32[32,1920]{1,0:T(8,128)S(1)}, f32[32,1920]{1,0:T(8,128)S(1)}, u32[]{:S(2)}, u32[]{:S(2)}) collective-permute-start(f32[32,1920]{1,0:T(8,128)S(1)} %slice.54), channel_id=1, source_target_pairs={{0,48},{16,0},{32,16},{48,32},{1,49},{17,1},{33,17},{49,33},{2,50}... | collective-permute-start | bytes 737288 | tf_op jit(solution)/shard_map/ppermute | solution.py:26
  106.9 9.3 %collective-permute-start.4 = (f32[32,1920]{1,0:T(8,128)S(1)}, f32[32,1920]{1,0:T(8,128)S(1)}, u32[]{:S(2)}, u32[]{:S(2)}) collective-permute-start(f32[32,1920]{1,0:T(8,128)S(1)} %slice_add_fusion.2), channel_id=1, source_target_pairs={{0,48},{16,0},{32,16},{48,32},{1,49},{17,1},{33,17},{49,33},{2,50}... | collective-permute-start | bytes 737288 | tf_op jit(solution)/shard_map/ppermute | solution.py:26
  116.3 9.1 %collective-permute-start = (f32[32,1920]{1,0:T(8,128)S(1)}, f32[32,1920]{1,0:T(8,128)S(1)}, u32[]{:S(2)}, u32[]{:S(2)}) collective-permute-start(f32[32,1920]{1,0:T(8,128)S(1)} %get-tuple-element.20), channel_id=1, source_target_pairs={{0,16},{16,32},{32,48},{48,0},{1,17},{17,33},{33,49},{49,1},{2,18}... | collective-permute-start | bytes 737288 | tf_op jit(solution)/shard_map/ppermute | solution.py:25
  125.4 30.4 %copy-start.1 = (bf16[16,1920]{1,0:T(8,128)(2,1)S(1)}, bf16[16,1920]{1,0:T(8,128)(2,1)}, u32[]{:S(2)}) copy-start(bf16[16,1920]{1,0:T(8,128)(2,1)} %param.7) | copy-start | bytes 184324
  125.4 11.1 %collective-permute-start.1 = (f32[32,1920]{1,0:T(8,128)S(1)}, f32[32,1920]{1,0:T(8,128)S(1)}, u32[]{:S(2)}, u32[]{:S(2)}) collective-permute-start(f32[32,1920]{1,0:T(8,128)S(1)} %slice_add_fusion.5), channel_id=1, source_target_pairs={{0,16},{16,32},{32,48},{48,0},{1,17},{17,33},{33,49},{49,1},{2,18}... | collective-permute-start | bytes 737288 | tf_op jit(solution)/shard_map/ppermute | solution.py:25
  129.0 72.9 %all-to-all-start.1 = ((bf16[12,128,512]{2,1,0:T(8,128)(2,1)}), bf16[12,128,512]{2,1,0:T(8,128)(2,1)S(1)}, u32[]{:S(2)}, u32[]{:S(2)}) async-start(bf16[12,128,512]{2,1,0:T(8,128)(2,1)} %broadcast_in_dim.2), calls=%async_computation.2 | async-start | bytes 3145728 | tf_op jit(solution)/shard_map/all_to_all | solution.py:36
  132.7 11.3 %collective-permute-start.5 = (f32[32,1920]{1,0:T(8,128)S(1)}, f32[32,1920]{1,0:T(8,128)S(1)}, u32[]{:S(2)}, u32[]{:S(2)}) collective-permute-start(f32[32,1920]{1,0:T(8,128)S(1)} %get-tuple-element.21), channel_id=1, source_target_pairs={{0,48},{16,0},{32,16},{48,32},{1,49},{17,1},{33,17},{49,33},{2,50}... | collective-permute-start | bytes 737288 | tf_op jit(solution)/shard_map/ppermute | solution.py:26
  136.5 9.8 %collective-permute-start.2 = (f32[32,1920]{1,0:T(8,128)S(1)}, f32[32,1920]{1,0:T(8,128)S(1)}, u32[]{:S(2)}, u32[]{:S(2)}) collective-permute-start(f32[32,1920]{1,0:T(8,128)S(1)} %slice_add_fusion.4), channel_id=1, source_target_pairs={{0,16},{16,32},{32,48},{48,0},{1,17},{17,33},{33,49},{49,1},{2,18}... | collective-permute-start | bytes 737288 | tf_op jit(solution)/shard_map/ppermute | solution.py:25
  146.4 36.6 %collective-permute-start.6 = (bf16[32,3840]{1,0:T(8,128)(2,1)S(1)}, bf16[32,3840]{1,0:T(8,128)(2,1)S(1)}, u32[]{:S(2)}, u32[]{:S(2)}) collective-permute-start(bf16[32,3840]{1,0:T(8,128)(2,1)S(1)} %fusion.1), channel_id=1, source_target_pairs={{0,8},{8,0},{1,9},{9,1},{2,10},{10,2},{3,11},{11,3},{4,12},{12,4},... | collective-permute-start | bytes 737288 | tf_op jit(solution)/shard_map/ppermute | solution.py:44
  155.8 28.4 %collective-permute-start.7 = (bf16[16,1920]{1,0:T(8,128)(2,1)S(1)}, bf16[16,1920]{1,0:T(8,128)(2,1)S(1)}, u32[]{:S(2)}, u32[]{:S(2)}) collective-permute-start(bf16[16,1920]{1,0:T(8,128)(2,1)S(1)} %copy-done.1), channel_id=1, source_target_pairs={{0,8},{8,0},{1,9},{9,1},{2,10},{10,2},{3,11},{11,3},{4,12},{12,4},... | collective-permute-start | bytes 184328 | tf_op jit(solution)/shard_map/ppermute | solution.py:42
  201.9 80.2 %all-to-all-start = ((bf16[12,128,2,160]{1,3,2,0:T(8,128)(2,1)}), bf16[12,128,2,160]{1,3,2,0:T(8,128)(2,1)S(1)}, u32[]{:S(2)}, u32[]{:S(2)}) async-start(bf16[12,128,2,160]{1,3,2,0:T(8,128)(2,1)} %bitcast.29), calls=%async_computation.1 | async-start | bytes 1966080 | tf_op jit(solution)/shard_map/all_to_all | solution.py:72
  236.0 44.8 %reduce-scatter.2.cloned.1.call-start = ((), (), s32[]{:S(2)}) async-start(), calls=%async_computation.4 | async-start | bytes 294912 | tf_op jit(solution)/shard_map/reduce_scatter | solution.py:64
Sparse Core Ops, SparseCore 0:
  10.4 83.3 all-gather.1
  239.9 40.7 reduce-scatter.1

commit v7 on v5

--- a/solution.py
+++ b/solution.py
@@ -12,12 +12,12 @@
     replicas = lax.axis_size(REP)
     pair = jnp.concatenate([gate_weight, up_weight], 0)
     shard_units = pair.shape[1]
-    weight_pair = lax.all_gather(pair, REP, axis=1, tiled=True)
+    stacked = lax.all_gather(pair, REP, axis=0, tiled=False)
     copies = jnp.broadcast_to(tokens[None], (replicas,) + tokens.shape)
     all_tokens = lax.all_to_all(copies, REP, 0, 0, tiled=True)
-    hidden_units = weight_pair.shape[1]
-    weight_rows = weight_pair.reshape(2 * hidden_units, weight_pair.shape[2])
-    partial = jnp.einsum("td,hd->th", tokens, weight_rows, preferred_element_type=jnp.float32)
+    hidden_units = replicas * shard_units
+    partial = jnp.einsum("td,rkjd->tkrj", tokens, stacked, preferred_element_type=jnp.float32)
+    partial = partial.reshape(tokens.shape[0], 2 * hidden_units)
     swap = [(0, 1), (1, 0)]
     upper = lax.axis_index("zh")
     partner_cot = lax.ppermute(cotangent, "zh", swap)
@@ -43,7 +43,12 @@
     own_rows = cotangent.shape[0]
     hidden = lax.dynamic_slice_in_dim(hidden, upper * own_rows, own_rows, 0)
     grad_tokens = lax.psum_scatter(
-        jnp.einsum("th,hd->td", gathered, weight_rows, preferred_element_type=jnp.float32),
+        jnp.einsum(
+            "tkrj,rkjd->td",
+            gathered.reshape(gathered.shape[0], 2, replicas, shard_units),
+            stacked,
+            preferred_element_type=jnp.float32,
+        ),
         "col",
         scatter_dimension=0,
         tiled=True,

time: 261 us -> 261 us (level)
  no operation moved by 1% of the time
where the time goes in v7:
time: 261 us; the launch traced here: 260 us
  waiting for transfers between devices  162 us (62%)
  starting transfers between devices  47.6 us (18%)
  blocking collectives  14.7 us (6%)
  between operations  13.9 us (5%)
  matrix products  8.01 us (3%)
  other arithmetic  7.76 us (3%)
  local copies, waits for them, and re-layouts  5.73 us (2%)
    all_gather x1, waiting for transfers between devices, body(): stacked = lax.all_gather(pair, REP, axis=0, tiled=False)  84.8 us
    reduce_scatter x1, waiting for transfers between devices, body(): lax.psum_scatter(jnp.einsum('tkrj,rkjd->td', gathered.reshape(gathered.sh...  39.4 us
    all_to_all x1, starting transfers between devices, body(): owned = lax.all_to_all(by_owner, REP, 0, 0, tiled=True)  28.6 us
    reduce_scatter x1, waiting for transfers between devices, body(): summed = lax.psum_scatter(partial, 'x', scatter_dimension=0, tiled=True)  25.8 us
    all_gather x1, blocking collectives, body(): gathered = lax.all_gather(pair_grads, 'x', axis=0, tiled=True)  14.7 us
    ppermute x1, starting transfers between devices, body(): lax.ppermute(summed.astype(jnp.bfloat16), 'zh', swap).astype(jnp.float32)  10.8 us
    ppermute x1, waiting for transfers between devices, body(): lax.ppermute(summed.astype(jnp.bfloat16), 'zh', swap).astype(jnp.float32)  8.43 us
    all_to_all x1, starting transfers between devices, body(): all_tokens = lax.all_to_all(copies, REP, 0, 0, tiled=True)  6.19 us
  transfers between devices with their start and end apart: 7, of which 5 were waited for; matrix products, arithmetic and copies ran while one was open for 5% of the time, Pallas kernels for 0%

profile of v7, /device:TPU:6, one launch (start us, length us, event | category | flops | bytes accessed | tf_op | source)
XLA Modules:
  0.0 260.1 jit_solution(8479225549784165225)
XLA Ops:
  7.2 0.0 all-gather.3.cloned.1.call-start
  7.2 1.7 pad_maximum_fusion
  8.9 0.0 all-gather.3.cloned.1.call-update
  9.0 0.0 reduce-scatter.7.cloned.1.call-start
  9.0 84.8 %all-gather.3.cloned.1.call-done = bf16[24,160,512]{2,1,0:T(8,128)(2,1)} async-done(((bf16[2,160,512]{2,1,0:T(8,128)(2,1)}), bf16[24,160,512]{2,1,0:T(8,128)(2,1)}) %all-gather.3.cloned.1.call-update) | async-done | bytes 3932176 | tf_op jit(solution)/shard_map/all_gather | solution.py:15
  93.8 3.3 %convolution_bitcast_fusion = f32[128,2,12,160]{0,3,1,2:T(8,128)S(1)} fusion(bf16[12,2,160,512]{3,2,1,0:T(8,128)(2,1)} %bitcast.25, bf16[128,512]{1,0:T(8,128)(2,1)} %param.4), kind=kOutput, calls=%fused_computation.3 | convolution fusion | flops 503316480 | bytes 6029312 | tf_op jit(solution)/shard_map/td,rkjd->tkrj/dot_general | solution.py:19
  97.1 0.1 copy.29
  97.3 0.0 copy-start
  97.3 1.9 copy.38
  99.1 0.0 copy-start.1
  99.1 0.0 reduce-scatter.7.cloned.1.call-update
  99.1 0.0 copy-done
  99.2 1.3 broadcast_in_dim.2
  100.5 6.2 %all-to-all-start.1 = ((bf16[12,128,512]{2,1,0:T(8,128)(2,1)}), bf16[12,128,512]{2,1,0:T(8,128)(2,1)S(1)}, u32[]{:S(2)}, u32[]{:S(2)}) async-start(bf16[12,128,512]{2,1,0:T(8,128)(2,1)} %broadcast_in_dim.2), calls=%async_computation.2 | async-start | bytes 3145728 | tf_op jit(solution)/shard_map/all_to_all | solution.py:17
  106.7 25.8 %reduce-scatter.7.cloned.1.call-done = f32[32,3840]{1,0:T(8,128)} async-done(((f32[128,3840]{1,0:T(8,128)}), f32[32,3840]{1,0:T(8,128)}) %reduce-scatter.7.cloned.1.call-update) | async-done | bytes 491536 | tf_op jit(solution)/shard_map/reduce_scatter | solution.py:24
  132.4 1.1 convert_element_type.23
  133.5 10.8 %collective-permute-start = (bf16[32,3840]{1,0:T(8,128)(2,1)S(1)}, bf16[32,3840]{1,0:T(8,128)(2,1)S(1)}, u32[]{:S(2)}, u32[]{:S(2)}) collective-permute-start(bf16[32,3840]{1,0:T(8,128)(2,1)S(1)} %convert_element_type.23), channel_id=1, source_target_pairs={{0,8},{8,0},{1,9},{9,1},{2,10},{10,2},{3,11},{11,3},{4,12},{12,4},... | collective-permute-start | bytes 737288 | tf_op jit(solution)/shard_map/ppermute | solution.py:25
  144.3 0.0 copy-done.1
  144.3 1.9 collective-permute-start.1
  146.2 8.4 %collective-permute-done = bf16[32,3840]{1,0:T(8,128)(2,1)S(1)} collective-permute-done((bf16[32,3840]{1,0:T(8,128)(2,1)S(1)}, bf16[32,3840]{1,0:T(8,128)(2,1)S(1)}, u32[]{:S(2)}, u32[]{:S(2)}) %collective-permute-start) | collective-permute-done | bytes 245792 | tf_op jit(solution)/shard_map/ppermute | solution.py:25
  154.7 1.1 convert_add_fusion
  155.8 4.0 %collective-permute-done.1 = bf16[16,1920]{1,0:T(8,128)(2,1)S(1)} collective-permute-done((bf16[16,1920]{1,0:T(8,128)(2,1)S(1)}, bf16[16,1920]{1,0:T(8,128)(2,1)S(1)}, u32[]{:S(2)}, u32[]{:S(2)}) %collective-permute-start.1) | collective-permute-done | bytes 61472 | tf_op jit(solution)/shard_map/ppermute | solution.py:23
  159.7 0.9 fusion.8
  160.6 14.7 %all_gather.11 = bf16[128,3840]{1,0:T(8,128)(2,1)S(1)} all-gather(bf16[32,3840]{1,0:T(8,128)(2,1)S(1)} %pad_maximum_fusion.1), channel_id=1, replica_groups=mesh['zl'=6,'core'=2,'x'=4,'zh'=2,'col'=8] {'x'}, dimensions={0}, use_global_device_ids=true | all-gather | bytes 1228800 | tf_op jit(solution)/shard_map/all_gather | solution.py:42
  175.3 0.6 copy.32
  175.9 1.0 copy.34
  177.0 0.0 all-to-all-done.1
  177.0 28.6 %all-to-all-start = ((bf16[12,128,2,160]{1,3,2,0:T(8,128)(2,1)}), bf16[12,128,2,160]{1,3,2,0:T(8,128)(2,1)S(1)}, u32[]{:S(2)}, u32[]{:S(2)}) async-start(bf16[12,128,2,160]{1,3,2,0:T(8,128)(2,1)} %copy.34), calls=%async_computation.1 | async-start | bytes 1966080 | tf_op jit(solution)/shard_map/all_to_all | solution.py:58
  205.5 0.0 reduce-scatter.5.cloned.1.call-start
  205.6 3.5 %fusion.3 = f32[128,512]{1,0:T(8,128)} fusion(bf16[128,2,12,160]{0,3,2,1:T(8,128)(2,1)S(1)} %bitcast.29, bf16[12,2,160,512]{3,2,1,0:T(8,128)(2,1)} %bitcast.26), kind=kOutput, calls=%fused_computation.5 | convolution fusion | flops 503316480 | bytes 5177344 | tf_op jit(solution)/shard_map/tkrj,rkjd->td/dot_general | solution.py:46
  209.1 0.0 reduce-scatter.5.cloned.1.call-update
  209.2 1.6 fusion.12
  210.8 39.4 %reduce-scatter.5.cloned.1.call-done = f32[16,512]{1,0:T(8,128)} async-done(((f32[128,512]{1,0:T(8,128)}), f32[16,512]{1,0:T(8,128)}) %reduce-scatter.5.cloned.1.call-update) | async-done | bytes 32784 | tf_op jit(solution)/shard_map/reduce_scatter | solution.py:45
  250.2 1.4 convert_element_type.29
  251.6 0.0 all-to-all-done
  251.6 1.2 reduce-precision_reduce_fusion
  252.8 0.1 multiply_convert_fusion
  252.8 0.7 fusion.13
  (1 shorter events, 0.0 us)
Async XLA Ops:
  7.2 86.6 %all-gather.3.cloned.1.call-start = ((), (), s32[]{:S(2)}) async-start(), calls=%async_computation.5 | async-start | bytes 4259840 | tf_op jit(solution)/shard_map/all_gather | solution.py:15
  9.0 123.5 %reduce-scatter.7.cloned.1.call-start = ((), (), s32[]{:S(2)}) async-start(), calls=%async_computation.6 | async-start | bytes 2457600 | tf_op jit(solution)/shard_map/reduce_scatter | solution.py:24
  97.3 1.9 copy-start
  99.1 45.2 %copy-start.1 = (bf16[16,1920]{1,0:T(8,128)(2,1)S(1)}, bf16[16,1920]{1,0:T(8,128)(2,1)}, u32[]{:S(2)}) copy-start(bf16[16,1920]{1,0:T(8,128)(2,1)} %param.7) | copy-start | bytes 184324
  100.5 76.5 %all-to-all-start.1 = ((bf16[12,128,512]{2,1,0:T(8,128)(2,1)}), bf16[12,128,512]{2,1,0:T(8,128)(2,1)S(1)}, u32[]{:S(2)}, u32[]{:S(2)}) async-start(bf16[12,128,512]{2,1,0:T(8,128)(2,1)} %broadcast_in_dim.2), calls=%async_computation.2 | async-start | bytes 3145728 | tf_op jit(solution)/shard_map/all_to_all | solution.py:17
  133.5 21.2 %collective-permute-start = (bf16[32,3840]{1,0:T(8,128)(2,1)S(1)}, bf16[32,3840]{1,0:T(8,128)(2,1)S(1)}, u32[]{:S(2)}, u32[]{:S(2)}) collective-permute-start(bf16[32,3840]{1,0:T(8,128)(2,1)S(1)} %convert_element_type.23), channel_id=1, source_target_pairs={{0,8},{8,0},{1,9},{9,1},{2,10},{10,2},{3,11},{11,3},{4,12},{12,4},... | collective-permute-start | bytes 737288 | tf_op jit(solution)/shard_map/ppermute | solution.py:25
  144.3 15.4 %collective-permute-start.1 = (bf16[16,1920]{1,0:T(8,128)(2,1)S(1)}, bf16[16,1920]{1,0:T(8,128)(2,1)S(1)}, u32[]{:S(2)}, u32[]{:S(2)}) collective-permute-start(bf16[16,1920]{1,0:T(8,128)(2,1)S(1)} %copy-done.1), channel_id=1, source_target_pairs={{0,8},{8,0},{1,9},{9,1},{2,10},{10,2},{3,11},{11,3},{4,12},{12,4},... | collective-permute-start | bytes 184328 | tf_op jit(solution)/shard_map/ppermute | solution.py:23
  177.0 74.6 %all-to-all-start = ((bf16[12,128,2,160]{1,3,2,0:T(8,128)(2,1)}), bf16[12,128,2,160]{1,3,2,0:T(8,128)(2,1)S(1)}, u32[]{:S(2)}, u32[]{:S(2)}) async-start(bf16[12,128,2,160]{1,3,2,0:T(8,128)(2,1)} %copy.34), calls=%async_computation.1 | async-start | bytes 1966080 | tf_op jit(solution)/shard_map/all_to_all | solution.py:58
  205.5 44.7 %reduce-scatter.5.cloned.1.call-start = ((), (), s32[]{:S(2)}) async-start(), calls=%async_computation.4 | async-start | bytes 294912 | tf_op jit(solution)/shard_map/reduce_scatter | solution.py:45
Sparse Core Ops, SparseCore 0:
  10.4 83.3 all-gather.2
  99.3 33.1 reduce-scatter.6
  209.5 40.6 reduce-scatter.4

commit v8 on v7

--- a/solution.py
+++ b/solution.py
@@ -42,17 +42,15 @@
     gathered = lax.all_gather(pair_grads, "x", axis=0, tiled=True)
     own_rows = cotangent.shape[0]
     hidden = lax.dynamic_slice_in_dim(hidden, upper * own_rows, own_rows, 0)
-    grad_tokens = lax.psum_scatter(
-        jnp.einsum(
-            "tkrj,rkjd->td",
-            gathered.reshape(gathered.shape[0], 2, replicas, shard_units),
-            stacked,
-            preferred_element_type=jnp.float32,
-        ),
-        "col",
-        scatter_dimension=0,
-        tiled=True,
+    token_partial = jnp.einsum(
+        "tkrj,rkjd->td",
+        gathered.reshape(gathered.shape[0], 2, replicas, shard_units),
+        stacked,
+        preferred_element_type=jnp.float32,
     )
+    n_col = lax.axis_size("col")
+    token_chunks = token_partial.reshape(n_col, token_partial.shape[0] // n_col, token_partial.shape[1])
+    grad_tokens = jnp.sum(lax.all_to_all(token_chunks, "col", 0, 0, tiled=True), axis=0)
     rows = gathered.shape[0]
     by_owner = gathered.reshape(rows, 2, replicas, shard_units).transpose(2, 0, 1, 3)
     owned = lax.all_to_all(by_owner, REP, 0, 0, tiled=True)

time: 261 us -> 274 us (1.050)
  starting transfers between devices: 47.6 us -> 56.3 us
    reduce_scatter x1 -> x0, waiting for transfers between devices: 39.4 us -> none  [body(): lax.psum_scatter(jnp.einsum('tkrj,rkjd->td', gathered.reshape(gathered.sh...]
    all_to_all x1, waiting for transfers between devices: 0.01 us -> 35.3 us  [body(): owned = lax.all_to_all(by_owner, REP, 0, 0, tiled=True)]
    all_to_all x0 -> x1, waiting for transfers between devices: none -> 9.44 us  [body(): lax.all_to_all(token_chunks, 'col', 0, 0, tiled=True)]
    all_to_all x0 -> x1, starting transfers between devices: none -> 6.74 us  [body(): lax.all_to_all(token_chunks, 'col', 0, 0, tiled=True)]
  transfers between devices with their start and end apart: 7 -> 7, of which waited for: 5 -> 6; matrix products, arithmetic and copies ran while one was open for 5% -> 5% of each run, Pallas kernels for 0% -> 0%
where the time goes in v8:
time: 274 us
  waiting for transfers between devices  164 us (60%)
  starting transfers between devices  56.3 us (21%)
  blocking collectives  16.6 us (6%)
  between operations  14.2 us (5%)
  matrix products  8.49 us (3%)
  local copies, waits for them, and re-layouts  8.21 us (3%)
  other arithmetic  6.05 us (2%)
    all_gather x1, waiting for transfers between devices, body(): stacked = lax.all_gather(pair, REP, axis=0, tiled=False)  84.8 us
    all_to_all x1, waiting for transfers between devices, body(): owned = lax.all_to_all(by_owner, REP, 0, 0, tiled=True)  35.3 us
    all_to_all x1, starting transfers between devices, body(): owned = lax.all_to_all(by_owner, REP, 0, 0, tiled=True)  30.5 us
    reduce_scatter x1, waiting for transfers between devices, body(): summed = lax.psum_scatter(partial, 'x', scatter_dimension=0, tiled=True)  24.8 us
    all_gather x1, blocking collectives, body(): gathered = lax.all_gather(pair_grads, 'x', axis=0, tiled=True)  16.6 us
    ppermute x1, starting transfers between devices, body(): lax.ppermute(summed.astype(jnp.bfloat16), 'zh', swap).astype(jnp.float32)  10.8 us
    all_to_all x1, waiting for transfers between devices, body(): lax.all_to_all(token_chunks, 'col', 0, 0, tiled=True)  9.44 us
    ppermute x1, waiting for transfers between devices, body(): lax.ppermute(summed.astype(jnp.bfloat16), 'zh', swap).astype(jnp.float32)  8.3 us
  transfers between devices with their start and end apart: 7, of which 6 were waited for; matrix products, arithmetic and copies ran while one was open for 5% of the time, Pallas kernels for 0%

profile of v8, /device:TPU:6, one launch (start us, length us, event | category | flops | bytes accessed | tf_op | source)
XLA Modules:
  0.0 273.8 jit_solution(4941684715782930762)
XLA Ops:
  7.2 0.0 all-gather.3.cloned.1.call-start
  7.2 1.7 pad_maximum_fusion
  8.9 0.0 all-gather.3.cloned.1.call-update
  9.0 0.0 reduce-scatter.4.cloned.1.call-start
  9.0 84.8 %all-gather.3.cloned.1.call-done = bf16[24,160,512]{2,1,0:T(8,128)(2,1)} async-done(((bf16[2,160,512]{2,1,0:T(8,128)(2,1)}), bf16[24,160,512]{2,1,0:T(8,128)(2,1)}) %all-gather.3.cloned.1.call-update) | async-done | bytes 3932176 | tf_op jit(solution)/shard_map/all_gather | solution.py:15
  93.8 3.3 %convolution_bitcast_fusion = f32[128,2,12,160]{0,3,1,2:T(8,128)S(1)} fusion(bf16[12,2,160,512]{3,2,1,0:T(8,128)(2,1)} %bitcast.31, bf16[128,512]{1,0:T(8,128)(2,1)} %param.4), kind=kOutput, calls=%fused_computation.3 | convolution fusion | flops 503316480 | bytes 6029312 | tf_op jit(solution)/shard_map/td,rkjd->tkrj/dot_general | solution.py:19
  97.1 0.1 copy.30
  97.3 1.9 copy.43
  99.1 0.0 copy-start.2
  99.1 0.0 reduce-scatter.4.cloned.1.call-update
  99.2 0.9 copy-done.2
  100.0 1.3 broadcast_in_dim.2
  101.4 0.0 copy-start.3
  101.4 6.3 %all-to-all-start.2 = ((bf16[12,128,512]{2,1,0:T(8,128)(2,1)}), bf16[12,128,512]{2,1,0:T(8,128)(2,1)S(1)}, u32[]{:S(2)}, u32[]{:S(2)}) async-start(bf16[12,128,512]{2,1,0:T(8,128)(2,1)} %broadcast_in_dim.2), calls=%async_computation.2 | async-start | bytes 3145728 | tf_op jit(solution)/shard_map/all_to_all | solution.py:17
  107.7 24.8 %reduce-scatter.4.cloned.1.call-done = f32[32,3840]{1,0:T(8,128)} async-done(((f32[128,3840]{1,0:T(8,128)}), f32[32,3840]{1,0:T(8,128)}) %reduce-scatter.4.cloned.1.call-update) | async-done | bytes 491536 | tf_op jit(solution)/shard_map/reduce_scatter | solution.py:24
  132.5 1.1 convert_element_type.23
  133.5 10.8 %collective-permute-start = (bf16[32,3840]{1,0:T(8,128)(2,1)S(1)}, bf16[32,3840]{1,0:T(8,128)(2,1)S(1)}, u32[]{:S(2)}, u32[]{:S(2)}) collective-permute-start(bf16[32,3840]{1,0:T(8,128)(2,1)S(1)} %convert_element_type.23), channel_id=1, source_target_pairs={{0,8},{8,0},{1,9},{9,1},{2,10},{10,2},{3,11},{11,3},{4,12},{12,4},... | collective-permute-start | bytes 737288 | tf_op jit(solution)/shard_map/ppermute | solution.py:25
  144.3 0.0 copy-done.3
  144.3 1.9 collective-permute-start.1
  146.3 8.3 %collective-permute-done = bf16[32,3840]{1,0:T(8,128)(2,1)S(1)} collective-permute-done((bf16[32,3840]{1,0:T(8,128)(2,1)S(1)}, bf16[32,3840]{1,0:T(8,128)(2,1)S(1)}, u32[]{:S(2)}, u32[]{:S(2)}) %collective-permute-start) | collective-permute-done | bytes 245792 | tf_op jit(solution)/shard_map/ppermute | solution.py:25
  154.6 1.1 convert_add_fusion
  155.6 1.3 collective-permute-done.1
  156.9 0.8 fusion.8
  157.8 16.6 %all_gather.11 = bf16[128,3840]{1,0:T(8,128)(2,1)S(1)} all-gather(bf16[32,3840]{1,0:T(8,128)(2,1)S(1)} %pad_maximum_fusion.1), channel_id=1, replica_groups=mesh['zl'=6,'core'=2,'x'=4,'zh'=2,'col'=8] {'x'}, dimensions={0}, use_global_device_ids=true | all-gather | bytes 1228800 | tf_op jit(solution)/shard_map/all_gather | solution.py:42
  174.4 0.6 copy.33
  175.0 1.6 copy.34
  176.6 4.0 %fusion.3 = f32[8,16,512]{2,1,0:T(8,128)} fusion(bf16[8,16,160,2,12]{2,1,0,4,3:T(8,128)(2,1)} %bitcast.36, bf16[12,2,160,512,1]{3,2,1,0,4:T(8,128)(2,1)} %bitcast.32), kind=kOutput, calls=%fused_computation.5 | convolution fusion | flops 503316480 | bytes 5177344 | tf_op jit(solution)/shard_map/tkrj,rkjd->td/dot_general | solution.py:45
  180.6 0.0 all-to-all-done.2
  180.6 6.7 %all-to-all-start = ((f32[8,16,512]{2,1,0:T(8,128)}), f32[8,16,512]{2,1,0:T(8,128)S(1)}, u32[]{:S(2)}, u32[]{:S(2)}) async-start(f32[8,16,512]{2,1,0:T(8,128)} %fusion.3), calls=%async_computation | async-start | bytes 524288 | tf_op jit(solution)/shard_map/all_to_all | solution.py:53
  187.4 0.0 copy-start
  187.4 0.0 copy-start.1
  187.4 1.0 copy.50
  188.4 9.4 %all-to-all-done = f32[8,16,512]{2,1,0:T(8,128)S(1)} async-done(((f32[8,16,512]{2,1,0:T(8,128)}), f32[8,16,512]{2,1,0:T(8,128)S(1)}, u32[]{:S(2)}, u32[]{:S(2)}) %all-to-all-start) | async-done | bytes 262176 | tf_op jit(solution)/shard_map/all_to_all | solution.py:53
  197.8 30.5 %all-to-all-start.1 = ((bf16[12,128,2,160]{1,3,2,0:T(8,128)(2,1)}), bf16[12,128,2,160]{1,3,2,0:T(8,128)(2,1)S(1)}, u32[]{:S(2)}, u32[]{:S(2)}) async-start(bf16[12,128,2,160]{1,3,2,0:T(8,128)(2,1)} %bitcast.30), calls=%async_computation.1 | async-start | bytes 1966080 | tf_op jit(solution)/shard_map/all_to_all | solution.py:56
  228.3 0.0 copy-done
  228.3 0.0 copy-done.1
  228.3 0.6 fusion.12
  229.0 0.6 reduce_sum.18
  229.6 35.3 %all-to-all-done.1 = bf16[12,128,2,160]{1,3,2,0:T(8,128)(2,1)S(1)} async-done(((bf16[12,128,2,160]{1,3,2,0:T(8,128)(2,1)}), bf16[12,128,2,160]{1,3,2,0:T(8,128)(2,1)S(1)}, u32[]{:S(2)}, u32[]{:S(2)}) %all-to-all-start.1) | async-done | bytes 983072 | tf_op jit(solution)/shard_map/all_to_all | solution.py:56
  265.0 1.2 reduce-precision_reduce_fusion
  266.1 0.1 multiply_convert_fusion
  266.2 0.7 fusion.13
  (1 shorter events, 0.0 us)
Async XLA Ops:
  7.2 86.6 %all-gather.3.cloned.1.call-start = ((), (), s32[]{:S(2)}) async-start(), calls=%async_computation.4 | async-start | bytes 4259840 | tf_op jit(solution)/shard_map/all_gather | solution.py:15
  9.0 123.5 %reduce-scatter.4.cloned.1.call-start = ((), (), s32[]{:S(2)}) async-start(), calls=%async_computation.5 | async-start | bytes 2457600 | tf_op jit(solution)/shard_map/reduce_scatter | solution.py:24
  99.1 0.9 copy-start.2
  101.4 43.0 %copy-start.3 = (bf16[16,1920]{1,0:T(8,128)(2,1)S(1)}, bf16[16,1920]{1,0:T(8,128)(2,1)}, u32[]{:S(2)}) copy-start(bf16[16,1920]{1,0:T(8,128)(2,1)} %param.7) | copy-start | bytes 184324
  101.4 79.3 %all-to-all-start.2 = ((bf16[12,128,512]{2,1,0:T(8,128)(2,1)}), bf16[12,128,512]{2,1,0:T(8,128)(2,1)S(1)}, u32[]{:S(2)}, u32[]{:S(2)}) async-start(bf16[12,128,512]{2,1,0:T(8,128)(2,1)} %broadcast_in_dim.2), calls=%async_computation.2 | async-start | bytes 3145728 | tf_op jit(solution)/shard_map/all_to_all | solution.py:17
  133.5 21.1 %collective-permute-start = (bf16[32,3840]{1,0:T(8,128)(2,1)S(1)}, bf16[32,3840]{1,0:T(8,128)(2,1)S(1)}, u32[]{:S(2)}, u32[]{:S(2)}) collective-permute-start(bf16[32,3840]{1,0:T(8,128)(2,1)S(1)} %convert_element_type.23), channel_id=1, source_target_pairs={{0,8},{8,0},{1,9},{9,1},{2,10},{10,2},{3,11},{11,3},{4,12},{12,4},... | collective-permute-start | bytes 737288 | tf_op jit(solution)/shard_map/ppermute | solution.py:25
  144.3 12.6 %collective-permute-start.1 = (bf16[16,1920]{1,0:T(8,128)(2,1)S(1)}, bf16[16,1920]{1,0:T(8,128)(2,1)S(1)}, u32[]{:S(2)}, u32[]{:S(2)}) collective-permute-start(bf16[16,1920]{1,0:T(8,128)(2,1)S(1)} %copy-done.3), channel_id=1, source_target_pairs={{0,8},{8,0},{1,9},{9,1},{2,10},{10,2},{3,11},{11,3},{4,12},{12,4},... | collective-permute-start | bytes 184328 | tf_op jit(solution)/shard_map/ppermute | solution.py:23
  180.6 17.2 %all-to-all-start = ((f32[8,16,512]{2,1,0:T(8,128)}), f32[8,16,512]{2,1,0:T(8,128)S(1)}, u32[]{:S(2)}, u32[]{:S(2)}) async-start(f32[8,16,512]{2,1,0:T(8,128)} %fusion.3), calls=%async_computation | async-start | bytes 524288 | tf_op jit(solution)/shard_map/all_to_all | solution.py:53
  187.4 41.0 %copy-start = (f32[32,1920]{1,0:T(8,128)S(1)}, f32[32,1920]{1,0:T(8,128)}, u32[]{:S(2)}) copy-start(f32[32,1920]{1,0:T(8,128)} %get-tuple-element.14) | copy-start | bytes 737284
  187.4 41.0 %copy-start.1 = (f32[32,1920]{1,0:T(8,128)S(1)}, f32[32,1920]{1,0:T(8,128)}, u32[]{:S(2)}) copy-start(f32[32,1920]{1,0:T(8,128)} %get-tuple-element.15) | copy-start | bytes 737284
  197.8 67.1 %all-to-all-start.1 = ((bf16[12,128,2,160]{1,3,2,0:T(8,128)(2,1)}), bf16[12,128,2,160]{1,3,2,0:T(8,128)(2,1)S(1)}, u32[]{:S(2)}, u32[]{:S(2)}) async-start(bf16[12,128,2,160]{1,3,2,0:T(8,128)(2,1)} %bitcast.30), calls=%async_computation.1 | async-start | bytes 1966080 | tf_op jit(solution)/shard_map/all_to_all | solution.py:56
Sparse Core Ops, SparseCore 0:
  10.4 83.3 all-gather.2
  99.3 33.1 reduce-scatter.3

commit v9 on v7

--- a/solution.py
+++ b/solution.py
@@ -12,7 +12,9 @@
     replicas = lax.axis_size(REP)
     pair = jnp.concatenate([gate_weight, up_weight], 0)
     shard_units = pair.shape[1]
-    stacked = lax.all_gather(pair, REP, axis=0, tiled=False)
+    stacked = lax.all_gather(pair, "zl", axis=0, tiled=False)
+    stacked = lax.all_gather(stacked, "core", axis=1, tiled=False)
+    stacked = stacked.reshape((replicas,) + pair.shape)
     copies = jnp.broadcast_to(tokens[None], (replicas,) + tokens.shape)
     all_tokens = lax.all_to_all(copies, REP, 0, 0, tiled=True)
     hidden_units = replicas * shard_units

time: 261 us -> 270 us (1.034)
  waiting for transfers between devices: 162 us -> 169 us
  starting transfers between devices: 47.6 us -> 51.2 us
    all_gather x1 -> x2, waiting for transfers between devices: 84.8 us -> 91.9 us  [the longest x1 69 us: body(): stacked = lax.all_gather(pair, 'zl', axis=0, tiled=False)]
    ppermute x1, waiting for transfers between devices: 3.98 us -> 1.08 us  [body(): partner_cot = lax.ppermute(cotangent, 'zh', swap)]
  transfers between devices with their start and end apart: 7 -> 8, of which waited for: 5 -> 7; matrix products, arithmetic and copies ran while one was open for 5% -> 5% of each run, Pallas kernels for 0% -> 0%
where the time goes in v9:
time: 270 us
  waiting for transfers between devices  169 us (63%)
  starting transfers between devices  51.2 us (19%)
  blocking collectives  14.3 us (5%)
  between operations  13.9 us (5%)
  matrix products  7.98 us (3%)
  other arithmetic  7.77 us (3%)
  local copies, waits for them, and re-layouts  5.71 us (2%)
    all_gather x1, waiting for transfers between devices, body(): stacked = lax.all_gather(pair, 'zl', axis=0, tiled=False)  69 us
    reduce_scatter x1, waiting for transfers between devices, body(): lax.psum_scatter(jnp.einsum('tkrj,rkjd->td', gathered.reshape(gathered.sh...  39.3 us
    all_to_all x1, starting transfers between devices, body(): owned = lax.all_to_all(by_owner, REP, 0, 0, tiled=True)  29.8 us
    reduce_scatter x1, waiting for transfers between devices, body(): summed = lax.psum_scatter(partial, 'x', scatter_dimension=0, tiled=True)  26.5 us
    all_gather x1, waiting for transfers between devices, body(): stacked = lax.all_gather(stacked, 'core', axis=1, tiled=False)  22.9 us
    all_gather x1, blocking collectives, body(): gathered = lax.all_gather(pair_grads, 'x', axis=0, tiled=True)  14.3 us
    ppermute x1, starting transfers between devices, body(): lax.ppermute(summed.astype(jnp.bfloat16), 'zh', swap).astype(jnp.float32)  10.8 us
    all_to_all x1, starting transfers between devices, body(): all_tokens = lax.all_to_all(copies, REP, 0, 0, tiled=True)  8.49 us
  transfers between devices with their start and end apart: 8, of which 7 were waited for; matrix products, arithmetic and copies ran while one was open for 5% of the time, Pallas kernels for 0%

profile of v9, /device:TPU:6, one launch (start us, length us, event | category | flops | bytes accessed | tf_op | source)
XLA Modules:
  0.0 269.6 jit_solution(9199357714065820505)
XLA Ops:
  7.2 0.0 all-gather.5.cloned.1.call-start
  7.2 1.7 pad_maximum_fusion
  9.0 0.0 all-gather.5.cloned.1.call-update
  9.0 0.0 all-gather.7.cloned.1.call-start
  9.0 69.0 %all-gather.5.cloned.1.call-done = bf16[12,160,512]{2,1,0:T(8,128)(2,1)} async-done(((bf16[2,160,512]{2,1,0:T(8,128)(2,1)}), bf16[12,160,512]{2,1,0:T(8,128)(2,1)}) %all-gather.5.cloned.1.call-update) | async-done | bytes 1966096 | tf_op jit(solution)/shard_map/all_gather | solution.py:15
  78.0 0.0 all-gather.7.cloned.1.call-update
  78.0 0.0 reduce-scatter.7.cloned.1.call-start
  78.1 22.9 %all-gather.7.cloned.1.call-done = bf16[6,4,160,512]{3,2,1,0:T(8,128)(2,1)} async-done(((bf16[6,2,160,512]{3,2,1,0:T(8,128)(2,1)}), bf16[6,4,160,512]{3,2,1,0:T(8,128)(2,1)}) %all-gather.7.cloned.1.call-update) | async-done | bytes 3932176 | tf_op jit(solution)/shard_map/all_gather | solution.py:16
  101.0 3.3 %convolution_bitcast_fusion = f32[128,2,12,160]{0,3,1,2:T(8,128)S(1)} fusion(bf16[12,2,160,512]{3,2,1,0:T(8,128)(2,1)} %bitcast.26, bf16[128,512]{1,0:T(8,128)(2,1)} %param.4), kind=kOutput, calls=%fused_computation.3 | convolution fusion | flops 503316480 | bytes 6029312 | tf_op jit(solution)/shard_map/td,rkjd->tkrj/dot_general | solution.py:21
  104.3 0.1 copy.29
  104.4 0.0 copy-start
  104.5 1.8 copy.38
  106.3 0.0 copy-start.1
  106.3 0.0 reduce-scatter.7.cloned.1.call-update
  106.3 0.0 copy-done
  106.3 1.3 broadcast_in_dim.2
  107.6 8.5 %all-to-all-start.1 = ((bf16[12,128,512]{2,1,0:T(8,128)(2,1)}), bf16[12,128,512]{2,1,0:T(8,128)(2,1)S(1)}, u32[]{:S(2)}, u32[]{:S(2)}) async-start(bf16[12,128,512]{2,1,0:T(8,128)(2,1)} %broadcast_in_dim.2), calls=%async_computation.2 | async-start | bytes 3145728 | tf_op jit(solution)/shard_map/all_to_all | solution.py:19
  116.1 26.5 %reduce-scatter.7.cloned.1.call-done = f32[32,3840]{1,0:T(8,128)} async-done(((f32[128,3840]{1,0:T(8,128)}), f32[32,3840]{1,0:T(8,128)}) %reduce-scatter.7.cloned.1.call-update) | async-done | bytes 491536 | tf_op jit(solution)/shard_map/reduce_scatter | solution.py:26
  142.6 1.1 convert_element_type.23
  143.7 10.8 %collective-permute-start = (bf16[32,3840]{1,0:T(8,128)(2,1)S(1)}, bf16[32,3840]{1,0:T(8,128)(2,1)S(1)}, u32[]{:S(2)}, u32[]{:S(2)}) collective-permute-start(bf16[32,3840]{1,0:T(8,128)(2,1)S(1)} %convert_element_type.23), channel_id=1, source_target_pairs={{0,8},{8,0},{1,9},{9,1},{2,10},{10,2},{3,11},{11,3},{4,12},{12,4},... | collective-permute-start | bytes 737288 | tf_op jit(solution)/shard_map/ppermute | solution.py:27
  154.5 0.0 copy-done.1
  154.5 1.9 collective-permute-start.1
  156.4 8.4 %collective-permute-done = bf16[32,3840]{1,0:T(8,128)(2,1)S(1)} collective-permute-done((bf16[32,3840]{1,0:T(8,128)(2,1)S(1)}, bf16[32,3840]{1,0:T(8,128)(2,1)S(1)}, u32[]{:S(2)}, u32[]{:S(2)}) %collective-permute-start) | collective-permute-done | bytes 245792 | tf_op jit(solution)/shard_map/ppermute | solution.py:27
  164.9 1.1 convert_add_fusion
  165.9 1.1 collective-permute-done.1
  167.0 0.9 fusion.8
  167.9 14.3 %all_gather.19 = bf16[128,3840]{1,0:T(8,128)(2,1)S(1)} all-gather(bf16[32,3840]{1,0:T(8,128)(2,1)S(1)} %pad_maximum_fusion.1), channel_id=1, replica_groups=mesh['zl'=6,'core'=2,'x'=4,'zh'=2,'col'=8] {'x'}, dimensions={0}, use_global_device_ids=true | all-gather | bytes 1228800 | tf_op jit(solution)/shard_map/all_gather | solution.py:44
  182.2 0.6 copy.32
  182.8 1.0 copy.34
  183.9 1.5 all-to-all-done.1
  185.4 29.8 %all-to-all-start = ((bf16[12,128,2,160]{1,3,2,0:T(8,128)(2,1)}), bf16[12,128,2,160]{1,3,2,0:T(8,128)(2,1)S(1)}, u32[]{:S(2)}, u32[]{:S(2)}) async-start(bf16[12,128,2,160]{1,3,2,0:T(8,128)(2,1)} %copy.34), calls=%async_computation.1 | async-start | bytes 1966080 | tf_op jit(solution)/shard_map/all_to_all | solution.py:60
  215.2 0.0 reduce-scatter.5.cloned.1.call-start
  215.3 3.5 %fusion.3 = f32[128,512]{1,0:T(8,128)} fusion(bf16[128,2,12,160]{0,3,2,1:T(8,128)(2,1)S(1)} %bitcast.30, bf16[12,2,160,512]{3,2,1,0:T(8,128)(2,1)} %bitcast.27), kind=kOutput, calls=%fused_computation.5 | convolution fusion | flops 503316480 | bytes 5177344 | tf_op jit(solution)/shard_map/tkrj,rkjd->td/dot_general | solution.py:48
  218.8 0.0 reduce-scatter.5.cloned.1.call-update
  218.8 1.6 fusion.12
  220.4 39.3 %reduce-scatter.5.cloned.1.call-done = f32[16,512]{1,0:T(8,128)} async-done(((f32[128,512]{1,0:T(8,128)}), f32[16,512]{1,0:T(8,128)}) %reduce-scatter.5.cloned.1.call-update) | async-done | bytes 32784 | tf_op jit(solution)/shard_map/reduce_scatter | solution.py:47
  259.7 1.4 convert_element_type.29
  261.1 0.0 all-to-all-done
  261.1 1.2 reduce-precision_reduce_fusion
  262.2 0.1 multiply_convert_fusion
  262.3 0.7 fusion.13
  (1 shorter events, 0.0 us)
Async XLA Ops:
  7.2 70.8 %all-gather.5.cloned.1.call-start = ((), (), s32[]{:S(2)}) async-start(), calls=%async_computation.5 | async-start | bytes 2293760 | tf_op jit(solution)/shard_map/all_gather | solution.py:15
  9.0 92.0 %all-gather.7.cloned.1.call-start = ((), (), s32[]{:S(2)}) async-start(), calls=%async_computation.6 | async-start | bytes 5898240 | tf_op jit(solution)/shard_map/all_gather | solution.py:16
  78.0 64.6 %reduce-scatter.7.cloned.1.call-start = ((), (), s32[]{:S(2)}) async-start(), calls=%async_computation.7 | async-start | bytes 2457600 | tf_op jit(solution)/shard_map/reduce_scatter | solution.py:26
  104.4 1.9 copy-start
  106.3 48.2 %copy-start.1 = (bf16[16,1920]{1,0:T(8,128)(2,1)S(1)}, bf16[16,1920]{1,0:T(8,128)(2,1)}, u32[]{:S(2)}) copy-start(bf16[16,1920]{1,0:T(8,128)(2,1)} %param.7) | copy-start | bytes 184324
  107.6 77.7 %all-to-all-start.1 = ((bf16[12,128,512]{2,1,0:T(8,128)(2,1)}), bf16[12,128,512]{2,1,0:T(8,128)(2,1)S(1)}, u32[]{:S(2)}, u32[]{:S(2)}) async-start(bf16[12,128,512]{2,1,0:T(8,128)(2,1)} %broadcast_in_dim.2), calls=%async_computation.2 | async-start | bytes 3145728 | tf_op jit(solution)/shard_map/all_to_all | solution.py:19
  143.7 21.2 %collective-permute-start = (bf16[32,3840]{1,0:T(8,128)(2,1)S(1)}, bf16[32,3840]{1,0:T(8,128)(2,1)S(1)}, u32[]{:S(2)}, u32[]{:S(2)}) collective-permute-start(bf16[32,3840]{1,0:T(8,128)(2,1)S(1)} %convert_element_type.23), channel_id=1, source_target_pairs={{0,8},{8,0},{1,9},{9,1},{2,10},{10,2},{3,11},{11,3},{4,12},{12,4},... | collective-permute-start | bytes 737288 | tf_op jit(solution)/shard_map/ppermute | solution.py:27
  154.5 12.5 %collective-permute-start.1 = (bf16[16,1920]{1,0:T(8,128)(2,1)S(1)}, bf16[16,1920]{1,0:T(8,128)(2,1)S(1)}, u32[]{:S(2)}, u32[]{:S(2)}) collective-permute-start(bf16[16,1920]{1,0:T(8,128)(2,1)S(1)} %copy-done.1), channel_id=1, source_target_pairs={{0,8},{8,0},{1,9},{9,1},{2,10},{10,2},{3,11},{11,3},{4,12},{12,4},... | collective-permute-start | bytes 184328 | tf_op jit(solution)/shard_map/ppermute | solution.py:25
  185.4 75.7 %all-to-all-start = ((bf16[12,128,2,160]{1,3,2,0:T(8,128)(2,1)}), bf16[12,128,2,160]{1,3,2,0:T(8,128)(2,1)S(1)}, u32[]{:S(2)}, u32[]{:S(2)}) async-start(bf16[12,128,2,160]{1,3,2,0:T(8,128)(2,1)} %copy.34), calls=%async_computation.1 | async-start | bytes 1966080 | tf_op jit(solution)/shard_map/all_to_all | solution.py:60
  215.2 44.5 %reduce-scatter.5.cloned.1.call-start = ((), (), s32[]{:S(2)}) async-start(), calls=%async_computation.4 | async-start | bytes 294912 | tf_op jit(solution)/shard_map/reduce_scatter | solution.py:47
Sparse Core Ops, SparseCore 0:
  10.4 67.5 all-gather.4
  80.4 20.5 all-gather.6
  106.4 36.1 reduce-scatter.6
  218.9 40.7 reduce-scatter.4

commit v10 on v7

--- a/solution.py
+++ b/solution.py
@@ -21,8 +21,8 @@
     swap = [(0, 1), (1, 0)]
     upper = lax.axis_index("zh")
     partner_cot = lax.ppermute(cotangent, "zh", swap)
-    summed = lax.psum_scatter(partial, "x", scatter_dimension=0, tiled=True)
-    summed = summed + lax.ppermute(summed.astype(jnp.bfloat16), "zh", swap).astype(jnp.float32)
+    summed = lax.psum_scatter(partial.astype(jnp.bfloat16), "x", scatter_dimension=0, tiled=True)
+    summed = summed.astype(jnp.float32) + lax.ppermute(summed, "zh", swap).astype(jnp.float32)
     gate_pre = summed[:, :hidden_units]
     up_pre = summed[:, hidden_units:]
     sigmoid_val = jax.nn.sigmoid(gate_pre)

time: 261 us -> 260 us (level)
    all_to_all x1, waiting for transfers between devices: 0.01 us -> 8.3 us  [body(): all_tokens = lax.all_to_all(copies, REP, 0, 0, tiled=True)]
    reduce_scatter x1, waiting for transfers between devices: 25.8 us -> 20.7 us  [body(): lax.psum_scatter(partial.astype(jnp.bfloat16), 'x', scatter_dimension=0,...]
  transfers between devices with their start and end apart: 7 -> 7, of which waited for: 5 -> 6; matrix products, arithmetic and copies ran while one was open for 5% -> 4% of each run, Pallas kernels for 0% -> 0%
where the time goes in v10:
time: 260 us
  waiting for transfers between devices  163 us (63%)
  starting transfers between devices  48 us (18%)
  blocking collectives  15 us (6%)
  between operations  13.9 us (5%)
  matrix products  8.01 us (3%)
  other arithmetic  6.62 us (3%)
  local copies, waits for them, and re-layouts  5.15 us (2%)
    all_gather x1, waiting for transfers between devices, body(): stacked = lax.all_gather(pair, REP, axis=0, tiled=False)  84.8 us
    reduce_scatter x1, waiting for transfers between devices, body(): lax.psum_scatter(jnp.einsum('tkrj,rkjd->td', gathered.reshape(gathered.sh...  39.9 us
    all_to_all x1, starting transfers between devices, body(): owned = lax.all_to_all(by_owner, REP, 0, 0, tiled=True)  29.5 us
    reduce_scatter x1, waiting for transfers between devices, body(): lax.psum_scatter(partial.astype(jnp.bfloat16), 'x', scatter_dimension=0,...  20.7 us
    all_gather x1, blocking collectives, body(): gathered = lax.all_gather(pair_grads, 'x', axis=0, tiled=True)  15 us
    ppermute x1, starting transfers between devices, body(): lax.ppermute(summed, 'zh', swap).astype(jnp.float32)  10.1 us
    all_to_all x1, waiting for transfers between devices, body(): all_tokens = lax.all_to_all(copies, REP, 0, 0, tiled=True)  8.3 us
    ppermute x1, waiting for transfers between devices, body(): lax.ppermute(summed, 'zh', swap).astype(jnp.float32)  6.47 us
  transfers between devices with their start and end apart: 7, of which 6 were waited for; matrix products, arithmetic and copies ran while one was open for 4% of the time, Pallas kernels for 0%

profile of v10, /device:TPU:6, one launch (start us, length us, event | category | flops | bytes accessed | tf_op | source)
XLA Modules:
  0.0 259.8 jit_solution(11598826899317753599)
XLA Ops:
  7.2 0.0 all-gather.3.cloned.1.call-start
  7.2 1.7 pad_maximum_fusion
  8.9 0.0 all-gather.3.cloned.1.call-update
  9.0 0.0 reduce-scatter.7.cloned.1.call-start
  9.0 84.8 %all-gather.3.cloned.1.call-done = bf16[24,160,512]{2,1,0:T(8,128)(2,1)} async-done(((bf16[2,160,512]{2,1,0:T(8,128)(2,1)}), bf16[24,160,512]{2,1,0:T(8,128)(2,1)}) %all-gather.3.cloned.1.call-update) | async-done | bytes 3932176 | tf_op jit(solution)/shard_map/all_gather | solution.py:15
  93.8 0.0 copy-start
  93.8 3.3 %fusion.3 = bf16[128,2,12,160]{0,3,1,2:T(8,128)(2,1)S(1)} fusion(bf16[12,2,160,512]{3,2,1,0:T(8,128)(2,1)} %bitcast.25, bf16[128,512]{1,0:T(8,128)(2,1)} %param.4), kind=kOutput, calls=%fused_computation.5 | convolution fusion | flops 503808000 | bytes 5046272 | tf_op jit(solution)/shard_map/td,rkjd->tkrj/dot_general | solution.py:19
  97.1 0.1 copy.29
  97.2 0.0 copy-start.1
  97.2 1.3 copy.38
  98.6 0.0 reduce-scatter.7.cloned.1.call-update
  98.6 0.0 copy-done
  98.6 1.3 broadcast_in_dim.2
  99.9 6.2 %all-to-all-start.1 = ((bf16[12,128,512]{2,1,0:T(8,128)(2,1)}), bf16[12,128,512]{2,1,0:T(8,128)(2,1)S(1)}, u32[]{:S(2)}, u32[]{:S(2)}) async-start(bf16[12,128,512]{2,1,0:T(8,128)(2,1)} %broadcast_in_dim.2), calls=%async_computation.2 | async-start | bytes 3145728 | tf_op jit(solution)/shard_map/all_to_all | solution.py:17
  106.1 20.7 %reduce-scatter.7.cloned.1.call-done = bf16[32,3840]{1,0:T(8,128)(2,1)} async-done(((bf16[128,3840]{1,0:T(8,128)(2,1)}), bf16[32,3840]{1,0:T(8,128)(2,1)}) %reduce-scatter.7.cloned.1.call-update) | async-done | bytes 245776 | tf_op jit(solution)/shard_map/reduce_scatter | solution.py:24
  126.8 10.1 %collective-permute-start = (bf16[32,3840]{1,0:T(8,128)(2,1)}, bf16[32,3840]{1,0:T(8,128)(2,1)S(1)}, u32[]{:S(2)}, u32[]{:S(2)}) collective-permute-start(bf16[32,3840]{1,0:T(8,128)(2,1)} %reduce-scatter.7.cloned.1.call-done), channel_id=1, source_target_pairs={{0,8},{8,0},{1,9},{9,1},{2,10},{10,2},{3,11},{11,3},{4,12},{12,4},... | collective-permute-start | bytes 737288 | tf_op jit(solution)/shard_map/ppermute | solution.py:25
  137.0 0.0 copy-done.1
  137.0 2.0 collective-permute-start.1
  139.0 6.5 %collective-permute-done = bf16[32,3840]{1,0:T(8,128)(2,1)S(1)} collective-permute-done((bf16[32,3840]{1,0:T(8,128)(2,1)}, bf16[32,3840]{1,0:T(8,128)(2,1)S(1)}, u32[]{:S(2)}, u32[]{:S(2)}) %collective-permute-start) | collective-permute-done | bytes 245792 | tf_op jit(solution)/shard_map/ppermute | solution.py:25
  145.5 1.0 convert_add_fusion
  146.5 3.0 %collective-permute-done.1 = bf16[16,1920]{1,0:T(8,128)(2,1)S(1)} collective-permute-done((bf16[16,1920]{1,0:T(8,128)(2,1)S(1)}, bf16[16,1920]{1,0:T(8,128)(2,1)S(1)}, u32[]{:S(2)}, u32[]{:S(2)}) %collective-permute-start.1) | collective-permute-done | bytes 61472 | tf_op jit(solution)/shard_map/ppermute | solution.py:23
  149.5 0.8 fusion.9
  150.4 15.0 %all_gather.11 = bf16[128,3840]{1,0:T(8,128)(2,1)S(1)} all-gather(bf16[32,3840]{1,0:T(8,128)(2,1)S(1)} %pad_maximum_fusion.1), channel_id=1, replica_groups=mesh['zl'=6,'core'=2,'x'=4,'zh'=2,'col'=8] {'x'}, dimensions={0}, use_global_device_ids=true | all-gather | bytes 1228800 | tf_op jit(solution)/shard_map/all_gather | solution.py:42
  165.3 0.6 copy.32
  166.0 1.0 copy.34
  167.0 8.3 %all-to-all-done.1 = bf16[12,128,512]{2,1,0:T(8,128)(2,1)S(1)} async-done(((bf16[12,128,512]{2,1,0:T(8,128)(2,1)}), bf16[12,128,512]{2,1,0:T(8,128)(2,1)S(1)}, u32[]{:S(2)}, u32[]{:S(2)}) %all-to-all-start.1) | async-done | bytes 1572896 | tf_op jit(solution)/shard_map/all_to_all | solution.py:17
  175.3 29.5 %all-to-all-start = ((bf16[12,128,2,160]{1,3,2,0:T(8,128)(2,1)}), bf16[12,128,2,160]{1,3,2,0:T(8,128)(2,1)S(1)}, u32[]{:S(2)}, u32[]{:S(2)}) async-start(bf16[12,128,2,160]{1,3,2,0:T(8,128)(2,1)} %copy.34), calls=%async_computation.1 | async-start | bytes 1966080 | tf_op jit(solution)/shard_map/all_to_all | solution.py:58
  204.9 0.0 reduce-scatter.5.cloned.1.call-start
  204.9 3.5 %fusion.4 = f32[128,512]{1,0:T(8,128)} fusion(bf16[128,2,12,160]{0,3,2,1:T(8,128)(2,1)S(1)} %bitcast.28, bf16[12,2,160,512]{3,2,1,0:T(8,128)(2,1)} %bitcast.26), kind=kOutput, calls=%fused_computation.6 | convolution fusion | flops 503316480 | bytes 5177344 | tf_op jit(solution)/shard_map/tkrj,rkjd->td/dot_general | solution.py:46
  208.4 0.0 reduce-scatter.5.cloned.1.call-update
  208.5 1.6 fusion.13
  210.1 39.9 %reduce-scatter.5.cloned.1.call-done = f32[16,512]{1,0:T(8,128)} async-done(((f32[128,512]{1,0:T(8,128)}), f32[16,512]{1,0:T(8,128)}) %reduce-scatter.5.cloned.1.call-update) | async-done | bytes 32784 | tf_op jit(solution)/shard_map/reduce_scatter | solution.py:45
  249.9 1.4 convert_element_type.41
  251.3 0.0 all-to-all-done
  251.3 1.2 reduce-precision_reduce_fusion
  252.5 0.1 multiply_convert_fusion
  252.6 0.7 fusion.14
  (1 shorter events, 0.0 us)
Async XLA Ops:
  7.2 86.6 %all-gather.3.cloned.1.call-start = ((), (), s32[]{:S(2)}) async-start(), calls=%async_computation.5 | async-start | bytes 4259840 | tf_op jit(solution)/shard_map/all_gather | solution.py:15
  9.0 117.9 %reduce-scatter.7.cloned.1.call-start = ((), (), s32[]{:S(2)}) async-start(), calls=%async_computation.6 | async-start | bytes 1228800 | tf_op jit(solution)/shard_map/reduce_scatter | solution.py:24
  93.8 4.8 %copy-start = (bf16[128,512]{1,0:T(8,128)(2,1)S(1)}, bf16[128,512]{1,0:T(8,128)(2,1)}, u32[]{:S(2)}) copy-start(bf16[128,512]{1,0:T(8,128)(2,1)} %param.4) | copy-start | bytes 393220
  97.2 39.8 %copy-start.1 = (bf16[16,1920]{1,0:T(8,128)(2,1)S(1)}, bf16[16,1920]{1,0:T(8,128)(2,1)}, u32[]{:S(2)}) copy-start(bf16[16,1920]{1,0:T(8,128)(2,1)} %param.7) | copy-start | bytes 184324
  99.9 75.4 %all-to-all-start.1 = ((bf16[12,128,512]{2,1,0:T(8,128)(2,1)}), bf16[12,128,512]{2,1,0:T(8,128)(2,1)S(1)}, u32[]{:S(2)}, u32[]{:S(2)}) async-start(bf16[12,128,512]{2,1,0:T(8,128)(2,1)} %broadcast_in_dim.2), calls=%async_computation.2 | async-start | bytes 3145728 | tf_op jit(solution)/shard_map/all_to_all | solution.py:17
  126.8 18.6 %collective-permute-start = (bf16[32,3840]{1,0:T(8,128)(2,1)}, bf16[32,3840]{1,0:T(8,128)(2,1)S(1)}, u32[]{:S(2)}, u32[]{:S(2)}) collective-permute-start(bf16[32,3840]{1,0:T(8,128)(2,1)} %reduce-scatter.7.cloned.1.call-done), channel_id=1, source_target_pairs={{0,8},{8,0},{1,9},{9,1},{2,10},{10,2},{3,11},{11,3},{4,12},{12,4},... | collective-permute-start | bytes 737288 | tf_op jit(solution)/shard_map/ppermute | solution.py:25
  137.0 12.5 %collective-permute-start.1 = (bf16[16,1920]{1,0:T(8,128)(2,1)S(1)}, bf16[16,1920]{1,0:T(8,128)(2,1)S(1)}, u32[]{:S(2)}, u32[]{:S(2)}) collective-permute-start(bf16[16,1920]{1,0:T(8,128)(2,1)S(1)} %copy-done.1), channel_id=1, source_target_pairs={{0,8},{8,0},{1,9},{9,1},{2,10},{10,2},{3,11},{11,3},{4,12},{12,4},... | collective-permute-start | bytes 184328 | tf_op jit(solution)/shard_map/ppermute | solution.py:23
  175.3 76.0 %all-to-all-start = ((bf16[12,128,2,160]{1,3,2,0:T(8,128)(2,1)}), bf16[12,128,2,160]{1,3,2,0:T(8,128)(2,1)S(1)}, u32[]{:S(2)}, u32[]{:S(2)}) async-start(bf16[12,128,2,160]{1,3,2,0:T(8,128)(2,1)} %copy.34), calls=%async_computation.1 | async-start | bytes 1966080 | tf_op jit(solution)/shard_map/all_to_all | solution.py:58
  204.9 45.1 %reduce-scatter.5.cloned.1.call-start = ((), (), s32[]{:S(2)}) async-start(), calls=%async_computation.4 | async-start | bytes 294912 | tf_op jit(solution)/shard_map/reduce_scatter | solution.py:45
Sparse Core Ops, SparseCore 0:
  10.4 83.3 all-gather.2
  98.7 28.0 reduce-scatter.6
  209.1 40.7 reduce-scatter.4

commit v11 on v7

--- a/solution.py
+++ b/solution.py
@@ -39,7 +39,20 @@
     ).astype(jnp.bfloat16)
     grad_up_pre = (upstream * gated).astype(jnp.bfloat16)
     pair_grads = jnp.concatenate([grad_gate_pre, grad_up_pre], 1)
-    gathered = lax.all_gather(pair_grads, "x", axis=0, tiled=True)
+    rows = pair_grads.shape[0]
+    pieces = pair_grads.reshape(rows, 2, replicas, shard_units).transpose(2, 0, 1, 3)
+    owned_part = lax.all_to_all(pieces, REP, 0, 0, tiled=True)
+    n_x = lax.axis_size("x")
+    both = lax.all_gather(
+        jnp.stack([pair_grads.reshape(-1), owned_part.reshape(-1)]), "x", axis=1, tiled=False
+    )
+    gathered = both[0].reshape(n_x * rows, pair_grads.shape[1])
+    owned = (
+        both[1]
+        .reshape(n_x, replicas, rows, 2, shard_units)
+        .transpose(1, 0, 2, 3, 4)
+        .reshape(replicas, n_x * rows, 2, shard_units)
+    )
     own_rows = cotangent.shape[0]
     hidden = lax.dynamic_slice_in_dim(hidden, upper * own_rows, own_rows, 0)
     grad_tokens = lax.psum_scatter(
@@ -53,9 +66,6 @@
         scatter_dimension=0,
         tiled=True,
     )
-    rows = gathered.shape[0]
-    by_owner = gathered.reshape(rows, 2, replicas, shard_units).transpose(2, 0, 1, 3)
-    owned = lax.all_to_all(by_owner, REP, 0, 0, tiled=True)
     terms = jnp.einsum("qtkh,qtd->qkhd", owned, all_tokens, preferred_element_type=jnp.float32)
     rounded = lax.reduce_precision(terms, exponent_bits=8, mantissa_bits=7)
     averaged = jnp.sum(rounded, axis=0) * (1.0 / replicas)

time: 261 us -> 320 us (1.23)
  waiting for transfers between devices: 162 us -> 217 us
  local copies, waits for them, and re-layouts: 5.73 us -> 35.1 us
  blocking collectives: 14.7 us -> 0 us
  starting transfers between devices: 47.6 us -> 33.5 us
  matrix products: 8.01 us -> 12.1 us
    all_gather x0 -> x1, waiting for transfers between devices: none -> 35 us  [body(): lax.all_gather(jnp.stack([pair_grads.reshape(-1), owned_part.reshape(-1)]...]
    slice x0 -> x1, local copies, waits for them, and re-layouts: none -> 22 us  [body(): both[1].reshape(n_x, replicas, rows, 2, shard_units)]
    all_to_all x1, waiting for transfers between devices: 0.01 us -> 17 us  [body(): owned_part = lax.all_to_all(pieces, REP, 0, 0, tiled=True)]
    all_gather x1 -> x0, blocking collectives: 14.7 us -> none  [body(): gathered = lax.all_gather(pair_grads, 'x', axis=0, tiled=True)]
    all_to_all x1, starting transfers between devices: 28.6 us -> 15.5 us  [body(): owned_part = lax.all_to_all(pieces, REP, 0, 0, tiled=True)]
    reduce_scatter x1, waiting for transfers between devices: 25.8 us -> 33.3 us  [body(): summed = lax.psum_scatter(partial, 'x', scatter_dimension=0, tiled=True)]
    another operation x0 -> x3, local copies, waits for them, and re-layouts: none -> 5.28 us  [the longest x1 3.48 us: body(): gathered.reshape(gathered.shape[0], 2, replicas, shard_units)]
  transfers between devices with their start and end apart: 7 -> 8, of which waited for: 5 -> 7; matrix products, arithmetic and copies ran while one was open for 5% -> 13% of each run, Pallas kernels for 0% -> 0%
where the time goes in v11:
time: 320 us
  waiting for transfers between devices  217 us (68%)
  local copies, waits for them, and re-layouts  35.1 us (11%)
  starting transfers between devices  33.5 us (10%)
  between operations  13.9 us (4%)
  matrix products  12.1 us (4%)
  other arithmetic  8.02 us (3%)
    all_gather x1, waiting for transfers between devices, body(): stacked = lax.all_gather(pair, REP, axis=0, tiled=False)  84.8 us
    reduce_scatter x1, waiting for transfers between devices, body(): lax.psum_scatter(jnp.einsum('tkrj,rkjd->td', gathered.reshape(gathered.sh...  37 us
    all_gather x1, waiting for transfers between devices, body(): lax.all_gather(jnp.stack([pair_grads.reshape(-1), owned_part.reshape(-1)]...  35 us
    reduce_scatter x1, waiting for transfers between devices, body(): summed = lax.psum_scatter(partial, 'x', scatter_dimension=0, tiled=True)  33.3 us
    slice x1, local copies, waits for them, and re-layouts, body(): both[1].reshape(n_x, replicas, rows, 2, shard_units)  22 us
    all_to_all x1, waiting for transfers between devices, body(): owned_part = lax.all_to_all(pieces, REP, 0, 0, tiled=True)  17 us
    all_to_all x1, starting transfers between devices, body(): owned_part = lax.all_to_all(pieces, REP, 0, 0, tiled=True)  15.5 us
    ppermute x1, starting transfers between devices, body(): lax.ppermute(summed.astype(jnp.bfloat16), 'zh', swap).astype(jnp.float32)  10.8 us
  transfers between devices with their start and end apart: 8, of which 7 were waited for; matrix products, arithmetic and copies ran while one was open for 13% of the time, Pallas kernels for 0%

profile of v11, /device:TPU:6, one launch (start us, length us, event | category | flops | bytes accessed | tf_op | source)
XLA Modules:
  0.0 319.5 jit_solution(12623000080458505275)
XLA Ops:
  7.2 0.0 all-gather.5.cloned.1.call-start
  7.2 1.7 pad_maximum_fusion.1
  8.9 0.0 all-gather.5.cloned.1.call-update
  9.0 0.0 reduce-scatter.7.cloned.1.call-start
  9.0 84.8 %all-gather.5.cloned.1.call-done = bf16[24,160,512]{2,1,0:T(8,128)(2,1)} async-done(((bf16[2,160,512]{2,1,0:T(8,128)(2,1)}), bf16[24,160,512]{2,1,0:T(8,128)(2,1)}) %all-gather.5.cloned.1.call-update) | async-done | bytes 3932176 | tf_op jit(solution)/shard_map/all_gather | solution.py:15
  93.8 3.3 %convolution_bitcast_fusion = f32[128,2,12,160]{0,3,1,2:T(8,128)S(1)} fusion(bf16[12,2,160,512]{3,2,1,0:T(8,128)(2,1)} %bitcast.28, bf16[128,512]{1,0:T(8,128)(2,1)} %param.4), kind=kOutput, calls=%fused_computation.5 | convolution fusion | flops 503316480 | bytes 6029312 | tf_op jit(solution)/shard_map/td,rkjd->tkrj/dot_general | solution.py:19
  97.1 0.1 copy.46
  97.2 1.8 copy.59
  99.1 0.0 copy-start.1
  99.1 0.0 reduce-scatter.7.cloned.1.call-update
  99.1 33.3 %reduce-scatter.7.cloned.1.call-done = f32[32,3840]{1,0:T(8,128)} async-done(((f32[128,3840]{1,0:T(8,128)}), f32[32,3840]{1,0:T(8,128)}) %reduce-scatter.7.cloned.1.call-update) | async-done | bytes 491536 | tf_op jit(solution)/shard_map/reduce_scatter | solution.py:24
  132.4 1.1 convert_element_type.23
  133.4 10.8 %collective-permute-start = (bf16[32,3840]{1,0:T(8,128)(2,1)S(1)}, bf16[32,3840]{1,0:T(8,128)(2,1)S(1)}, u32[]{:S(2)}, u32[]{:S(2)}) collective-permute-start(bf16[32,3840]{1,0:T(8,128)(2,1)S(1)} %convert_element_type.23), channel_id=1, source_target_pairs={{0,8},{8,0},{1,9},{9,1},{2,10},{10,2},{3,11},{11,3},{4,12},{12,4},... | collective-permute-start | bytes 737288 | tf_op jit(solution)/shard_map/ppermute | solution.py:25
  144.3 0.0 copy-done.1
  144.3 1.9 collective-permute-start.1
  146.2 8.6 %collective-permute-done = bf16[32,3840]{1,0:T(8,128)(2,1)S(1)} collective-permute-done((bf16[32,3840]{1,0:T(8,128)(2,1)S(1)}, bf16[32,3840]{1,0:T(8,128)(2,1)S(1)}, u32[]{:S(2)}, u32[]{:S(2)}) %collective-permute-start) | collective-permute-done | bytes 245792 | tf_op jit(solution)/shard_map/ppermute | solution.py:25
  154.8 1.1 convert_add_fusion
  155.8 1.1 collective-permute-done.1
  156.9 0.1 fusion.11
  157.1 0.0 copy-start
  157.1 0.7 reshape.19
  157.8 1.0 copy.49
  158.8 15.5 %all-to-all-start = ((bf16[12,32,2,160]{3,1,2,0:T(8,128)(2,1)}), bf16[12,32,2,160]{3,1,2,0:T(8,128)(2,1)S(1)}, u32[]{:S(2)}, u32[]{:S(2)}) async-start(bf16[12,32,2,160]{3,1,2,0:T(8,128)(2,1)} %copy.49), calls=%async_computation | async-start | bytes 786432 | tf_op jit(solution)/shard_map/all_to_all | solution.py:44
  174.2 0.4 copy.61
  174.6 17.0 %all-to-all-done = bf16[12,32,2,160]{3,1,2,0:T(8,128)(2,1)S(1)} async-done(((bf16[12,32,2,160]{3,1,2,0:T(8,128)(2,1)}), bf16[12,32,2,160]{3,1,2,0:T(8,128)(2,1)S(1)}, u32[]{:S(2)}, u32[]{:S(2)}) %all-to-all-start) | async-done | bytes 245792 | tf_op jit(solution)/shard_map/all_to_all | solution.py:44
  191.6 0.0 copy-done
  191.6 1.3 broadcast_in_dim.2
  193.0 4.9 %all-to-all-start.1 = ((bf16[12,128,512]{2,1,0:T(8,128)(2,1)}), bf16[12,128,512]{2,1,0:T(8,128)(2,1)}, u32[]{:S(2)}, u32[]{:S(2)}) async-start(bf16[12,128,512]{2,1,0:T(8,128)(2,1)} %broadcast_in_dim.2), calls=%async_computation.2 | async-start | bytes 3145728 | tf_op jit(solution)/shard_map/all_to_all | solution.py:17
  197.9 0.0 all-gather.7.cloned.1.call-start
  197.9 0.4 copy.50
  198.3 0.4 stack_reshape.7
  198.8 1.9 pad_maximum_fusion
  200.7 0.0 all-gather.7.cloned.1.call-update
  200.7 0.2 reduce-scatter.5.cloned.1.call-start
  201.0 0.6 fusion.15
  201.6 35.0 %all-gather.7.cloned.1.call-done = bf16[2,491520]{1,0:T(2,128)(2,1)} async-done(((bf16[2,122880]{1,0:T(2,128)(2,1)}), bf16[2,491520]{1,0:T(2,128)(2,1)}) %all-gather.7.cloned.1.call-update) | async-done | bytes 1966096 | tf_op jit(solution)/shard_map/all_gather | solution.py:46
  236.7 22.0 %slice_reduce_fusion = (bf16[491520]{0:T(1024)(128)(2,1)S(1)}, bf16[491520]{0:T(1024)(128)(2,1)S(1)}) fusion(bf16[2,491520]{1,0:T(2,128)(2,1)} %all-gather.7.cloned.1.call-done), kind=kLoop, calls=%fused_computation.3 | loop fusion | bytes 3932160 | tf_op jit(solution)/shard_map/slice | solution.py:51
  258.7 3.5 %reshape_reshape_squeeze.3 = bf16[128,2,12,160]{3,2,1,0:T(8,128)(2,1)} reshape(bf16[491520]{0:T(1024)(128)(2,1)S(1)} %get-tuple-element.17) | data formatting | bytes 1966080 | tf_op jit(solution)/shard_map/reshape;reshape;squeeze | solution.py:61
  262.1 5.6 %fusion.4 = f32[128,512]{1,0:T(8,128)} fusion(bf16[12,2,160,512]{3,2,1,0:T(8,128)(2,1)} %bitcast.29, bf16[128,2,12,160]{3,2,1,0:T(8,128)(2,1)} %reshape_reshape_squeeze.3), kind=kOutput, calls=%fused_computation.8 | convolution fusion | flops 503316480 | bytes 5177344 | tf_op jit(solution)/shard_map/tkrj,rkjd->td/dot_general | solution.py:59
  267.8 0.0 reduce-scatter.5.cloned.1.call-update
  267.8 1.4 reshape_squeeze.3
  269.2 1.5 copy.53
  270.6 0.0 all-to-all-done.1
  270.6 3.2 reduce-precision_reduce_fusion
  273.8 0.1 multiply_convert_fusion
  273.9 0.7 fusion.17
  274.6 37.0 %reduce-scatter.5.cloned.1.call-done = f32[16,512]{1,0:T(8,128)} async-done(((f32[128,512]{1,0:T(8,128)}), f32[16,512]{1,0:T(8,128)}) %reduce-scatter.5.cloned.1.call-update) | async-done | bytes 32784 | tf_op jit(solution)/shard_map/reduce_scatter | solution.py:58
  311.6 1.4 convert_element_type.29
  (1 shorter events, 0.0 us)
Async XLA Ops:
  7.2 86.6 %all-gather.5.cloned.1.call-start = ((), (), s32[]{:S(2)}) async-start(), calls=%async_computation.5 | async-start | bytes 4259840 | tf_op jit(solution)/shard_map/all_gather | solution.py:15
  9.0 123.4 %reduce-scatter.7.cloned.1.call-start = ((), (), s32[]{:S(2)}) async-start(), calls=%async_computation.7 | async-start | bytes 2457600 | tf_op jit(solution)/shard_map/reduce_scatter | solution.py:24
  99.1 45.2 %copy-start.1 = (bf16[16,1920]{1,0:T(8,128)(2,1)S(1)}, bf16[16,1920]{1,0:T(8,128)(2,1)}, u32[]{:S(2)}) copy-start(bf16[16,1920]{1,0:T(8,128)(2,1)} %param.7) | copy-start | bytes 184324
  133.4 21.3 %collective-permute-start = (bf16[32,3840]{1,0:T(8,128)(2,1)S(1)}, bf16[32,3840]{1,0:T(8,128)(2,1)S(1)}, u32[]{:S(2)}, u32[]{:S(2)}) collective-permute-start(bf16[32,3840]{1,0:T(8,128)(2,1)S(1)} %convert_element_type.23), channel_id=1, source_target_pairs={{0,8},{8,0},{1,9},{9,1},{2,10},{10,2},{3,11},{11,3},{4,12},{12,4},... | collective-permute-start | bytes 737288 | tf_op jit(solution)/shard_map/ppermute | solution.py:25
  144.3 12.7 %collective-permute-start.1 = (bf16[16,1920]{1,0:T(8,128)(2,1)S(1)}, bf16[16,1920]{1,0:T(8,128)(2,1)S(1)}, u32[]{:S(2)}, u32[]{:S(2)}) collective-permute-start(bf16[16,1920]{1,0:T(8,128)(2,1)S(1)} %copy-done.1), channel_id=1, source_target_pairs={{0,8},{8,0},{1,9},{9,1},{2,10},{10,2},{3,11},{11,3},{4,12},{12,4},... | collective-permute-start | bytes 184328 | tf_op jit(solution)/shard_map/ppermute | solution.py:23
  157.1 34.6 %copy-start = (bf16[128,512]{1,0:T(8,128)(2,1)S(1)}, bf16[128,512]{1,0:T(8,128)(2,1)}, u32[]{:S(2)}) copy-start(bf16[128,512]{1,0:T(8,128)(2,1)} %param.4) | copy-start | bytes 393220
  158.8 32.9 %all-to-all-start = ((bf16[12,32,2,160]{3,1,2,0:T(8,128)(2,1)}), bf16[12,32,2,160]{3,1,2,0:T(8,128)(2,1)S(1)}, u32[]{:S(2)}, u32[]{:S(2)}) async-start(bf16[12,32,2,160]{3,1,2,0:T(8,128)(2,1)} %copy.49), calls=%async_computation | async-start | bytes 786432 | tf_op jit(solution)/shard_map/all_to_all | solution.py:44
  193.0 77.7 %all-to-all-start.1 = ((bf16[12,128,512]{2,1,0:T(8,128)(2,1)}), bf16[12,128,512]{2,1,0:T(8,128)(2,1)}, u32[]{:S(2)}, u32[]{:S(2)}) async-start(bf16[12,128,512]{2,1,0:T(8,128)(2,1)} %broadcast_in_dim.2), calls=%async_computation.2 | async-start | bytes 3145728 | tf_op jit(solution)/shard_map/all_to_all | solution.py:17
  197.9 38.8 %all-gather.7.cloned.1.call-start = ((), (), s32[]{:S(2)}) async-start(), calls=%async_computation.6 | async-start | bytes 2457600 | tf_op jit(solution)/shard_map/all_gather | solution.py:46
  200.7 110.9 %reduce-scatter.5.cloned.1.call-start = ((), (), s32[]{:S(2)}) async-start(), calls=%async_computation.4 | async-start | bytes 294912 | tf_op jit(solution)/shard_map/reduce_scatter | solution.py:58
Sparse Core Ops, SparseCore 0:
  10.4 83.3 all-gather.4
  99.2 33.1 reduce-scatter.6
  201.1 35.5 all-gather.6
  267.9 43.6 reduce-scatter.4

commit v12 on v7

--- a/solution.py
+++ b/solution.py
@@ -13,8 +13,14 @@
     pair = jnp.concatenate([gate_weight, up_weight], 0)
     shard_units = pair.shape[1]
     stacked = lax.all_gather(pair, REP, axis=0, tiled=False)
-    copies = jnp.broadcast_to(tokens[None], (replicas,) + tokens.shape)
-    all_tokens = lax.all_to_all(copies, REP, 0, 0, tiled=True)
+    n_col = lax.axis_size("col")
+    slab = tokens.shape[0] // n_col
+    mine = lax.dynamic_slice_in_dim(tokens, lax.axis_index("col") * slab, slab, 0)
+    copies = jnp.broadcast_to(mine[None], (replicas,) + mine.shape)
+    part = lax.all_to_all(copies, REP, 0, 0, tiled=True)
+    spread = jnp.broadcast_to(part[None], (n_col,) + part.shape)
+    all_tokens = lax.all_to_all(spread, "col", 0, 0, tiled=True)
+    all_tokens = all_tokens.transpose(1, 0, 2, 3).reshape(replicas, n_col * slab, tokens.shape[1])
     hidden_units = replicas * shard_units
     partial = jnp.einsum("td,rkjd->tkrj", tokens, stacked, preferred_element_type=jnp.float32)
     partial = partial.reshape(tokens.shape[0], 2 * hidden_units)

time: 261 us -> 248 us (0.950)
  waiting for transfers between devices: 162 us -> 141 us
  blocking collectives: 14.7 us -> 33.4 us
  starting transfers between devices: 47.6 us -> 35.8 us
    reduce_scatter x1, waiting for transfers between devices: 25.8 us -> 6.76 us  [body(): summed = lax.psum_scatter(partial, 'x', scatter_dimension=0, tiled=True)]
    all_to_all x0 -> x1, blocking collectives: none -> 18.4 us  [body(): part = lax.all_to_all(copies, REP, 0, 0, tiled=True)]
    all_to_all x1, starting transfers between devices: 28.6 us -> 16.2 us  [body(): owned = lax.all_to_all(by_owner, REP, 0, 0, tiled=True)]
    ppermute x1, waiting for transfers between devices: 3.98 us -> 1.09 us  [body(): partner_cot = lax.ppermute(cotangent, 'zh', swap)]
where the time goes in v12:
time: 248 us; the launch traced here: 247 us
  waiting for transfers between devices  141 us (57%)
  starting transfers between devices  35.8 us (14%)
  blocking collectives  33.4 us (13%)
  between operations  13.9 us (6%)
  matrix products  9.26 us (4%)
  other arithmetic  7.63 us (3%)
  local copies, waits for them, and re-layouts  6.92 us (3%)
    all_gather x1, waiting for transfers between devices, body(): stacked = lax.all_gather(pair, REP, axis=0, tiled=False)  84.8 us
    reduce_scatter x1, waiting for transfers between devices, body(): lax.psum_scatter(jnp.einsum('tkrj,rkjd->td', gathered.reshape(gathered.sh...  39.3 us
    all_to_all x1, blocking collectives, body(): part = lax.all_to_all(copies, REP, 0, 0, tiled=True)  18.4 us
    all_to_all x1, starting transfers between devices, body(): owned = lax.all_to_all(by_owner, REP, 0, 0, tiled=True)  16.2 us
    all_gather x1, blocking collectives, body(): gathered = lax.all_gather(pair_grads, 'x', axis=0, tiled=True)  15.1 us
    ppermute x1, starting transfers between devices, body(): lax.ppermute(summed.astype(jnp.bfloat16), 'zh', swap).astype(jnp.float32)  10.8 us
    ppermute x1, waiting for transfers between devices, body(): lax.ppermute(summed.astype(jnp.bfloat16), 'zh', swap).astype(jnp.float32)  8.57 us
    all_to_all x1, starting transfers between devices, body(): all_tokens = lax.all_to_all(spread, 'col', 0, 0, tiled=True)  6.77 us
  transfers between devices with their start and end apart: 7, of which 5 were waited for; matrix products, arithmetic and copies ran while one was open for 5% of the time, Pallas kernels for 0%

profile of v12, /device:TPU:6, one launch (start us, length us, event | category | flops | bytes accessed | tf_op | source)
XLA Modules:
  0.0 247.5 jit_solution(9021828798485084435)
XLA Ops:
  7.2 0.0 copy-start
  7.2 0.0 all-gather.3.cloned.1.call-start
  7.2 1.8 pad_maximum_fusion
  9.0 0.0 all-gather.3.cloned.1.call-update
  9.0 0.0 reduce-scatter.7.cloned.1.call-start
  9.1 84.8 %all-gather.3.cloned.1.call-done = bf16[24,160,512]{2,1,0:T(8,128)(2,1)} async-done(((bf16[2,160,512]{2,1,0:T(8,128)(2,1)}), bf16[24,160,512]{2,1,0:T(8,128)(2,1)}) %all-gather.3.cloned.1.call-update) | async-done | bytes 3932176 | tf_op jit(solution)/shard_map/all_gather | solution.py:15
  93.8 0.0 copy-done
  93.8 3.3 %convolution_bitcast_fusion = f32[128,2,12,160]{0,3,1,2:T(8,128)S(1)} fusion(bf16[12,2,160,512]{3,2,1,0:T(8,128)(2,1)} %bitcast.27, bf16[128,512]{1,0:T(8,128)(2,1)S(1)} %copy-done), kind=kOutput, calls=%fused_computation.3 | convolution fusion | flops 503316480 | bytes 6029312 | tf_op jit(solution)/shard_map/td,rkjd->tkrj/dot_general | solution.py:25
  97.1 0.1 copy.30
  97.3 1.9 copy.40
  99.1 0.0 copy-start.1
  99.1 0.0 reduce-scatter.7.cloned.1.call-update
  99.2 18.4 %all_to_all.15 = bf16[12,16,512]{2,1,0:T(8,128)(2,1)S(1)} all-to-all(bf16[12,16,512]{2,1,0:T(8,128)(2,1)S(1)} %broadcast_in_dim.4), channel_id=1, replica_groups=mesh['zl'=6,'core'=2,'x'=4,'zh'=2,'col'=8] {'zl','core'}, dimensions={0} | all-to-all | bytes 393216 | tf_op jit(solution)/shard_map/all_to_all | solution.py:20
  117.6 1.4 broadcast_in_dim.5
  118.9 6.8 %all-to-all-start.2 = ((bf16[8,12,16,512]{3,2,1,0:T(8,128)(2,1)}), bf16[8,12,16,512]{3,2,1,0:T(8,128)(2,1)S(1)}, u32[]{:S(2)}, u32[]{:S(2)}) async-start(bf16[8,12,16,512]{3,2,1,0:T(8,128)(2,1)} %broadcast_in_dim.5), calls=%async_computation.3 | async-start | bytes 3145728 | tf_op jit(solution)/shard_map/all_to_all | solution.py:22
  125.7 6.8 %reduce-scatter.7.cloned.1.call-done = f32[32,3840]{1,0:T(8,128)} async-done(((f32[128,3840]{1,0:T(8,128)}), f32[32,3840]{1,0:T(8,128)}) %reduce-scatter.7.cloned.1.call-update) | async-done | bytes 491536 | tf_op jit(solution)/shard_map/reduce_scatter | solution.py:30
  132.4 1.1 convert_element_type.23
  133.5 10.8 %collective-permute-start = (bf16[32,3840]{1,0:T(8,128)(2,1)S(1)}, bf16[32,3840]{1,0:T(8,128)(2,1)S(1)}, u32[]{:S(2)}, u32[]{:S(2)}) collective-permute-start(bf16[32,3840]{1,0:T(8,128)(2,1)S(1)} %convert_element_type.23), channel_id=1, source_target_pairs={{0,8},{8,0},{1,9},{9,1},{2,10},{10,2},{3,11},{11,3},{4,12},{12,4},... | collective-permute-start | bytes 737288 | tf_op jit(solution)/shard_map/ppermute | solution.py:31
  144.3 0.0 copy-done.1
  144.3 1.9 collective-permute-start.1
  146.2 8.6 %collective-permute-done = bf16[32,3840]{1,0:T(8,128)(2,1)S(1)} collective-permute-done((bf16[32,3840]{1,0:T(8,128)(2,1)S(1)}, bf16[32,3840]{1,0:T(8,128)(2,1)S(1)}, u32[]{:S(2)}, u32[]{:S(2)}) %collective-permute-start) | collective-permute-done | bytes 245792 | tf_op jit(solution)/shard_map/ppermute | solution.py:31
  154.8 1.1 convert_add_fusion
  155.9 1.1 collective-permute-done.1
  157.0 0.8 fusion.7
  157.8 15.1 %all_gather.11 = bf16[128,3840]{1,0:T(8,128)(2,1)} all-gather(bf16[32,3840]{1,0:T(8,128)(2,1)S(1)} %pad_maximum_fusion.1), channel_id=1, replica_groups=mesh['zl'=6,'core'=2,'x'=4,'zh'=2,'col'=8] {'x'}, dimensions={0}, use_global_device_ids=true | all-gather | bytes 1228800 | tf_op jit(solution)/shard_map/all_gather | solution.py:48
  172.9 1.6 copy.33
  174.5 1.0 copy.35
  175.5 0.0 all-to-all-done.2
  175.5 16.2 %all-to-all-start = ((bf16[12,128,2,160]{1,3,2,0:T(8,128)(2,1)}), bf16[12,128,2,160]{1,3,2,0:T(8,128)(2,1)}, u32[]{:S(2)}, u32[]{:S(2)}) async-start(bf16[12,128,2,160]{1,3,2,0:T(8,128)(2,1)} %copy.35), calls=%async_computation.1 | async-start | bytes 1966080 | tf_op jit(solution)/shard_map/all_to_all | solution.py:64
  191.7 0.0 reduce-scatter.5.cloned.1.call-start
  191.7 3.5 %fusion.2 = f32[128,512]{1,0:T(8,128)} fusion(bf16[128,2,12,160]{0,3,2,1:T(8,128)(2,1)S(1)} %bitcast.32, bf16[12,2,160,512]{3,2,1,0:T(8,128)(2,1)} %bitcast.28), kind=kOutput, calls=%fused_computation.4 | convolution fusion | flops 503316480 | bytes 5177344 | tf_op jit(solution)/shard_map/tkrj,rkjd->td/dot_general | solution.py:52
  195.3 0.0 reduce-scatter.5.cloned.1.call-update
  195.3 0.2 copy.36
  195.5 1.5 fusion.11
  197.0 39.3 %reduce-scatter.5.cloned.1.call-done = f32[16,512]{1,0:T(8,128)} async-done(((f32[128,512]{1,0:T(8,128)}), f32[16,512]{1,0:T(8,128)}) %reduce-scatter.5.cloned.1.call-update) | async-done | bytes 32784 | tf_op jit(solution)/shard_map/reduce_scatter | solution.py:51
  236.4 1.4 convert_element_type.29
  237.7 0.0 all-to-all-done
  237.7 2.4 reduce-precision_reduce_fusion
  240.2 0.1 multiply_convert_fusion
  240.2 0.7 fusion.12
  (3 shorter events, 0.0 us)
Async XLA Ops:
  7.2 86.7 %copy-start = (bf16[128,512]{1,0:T(8,128)(2,1)S(1)}, bf16[128,512]{1,0:T(8,128)(2,1)}, u32[]{:S(2)}) copy-start(bf16[128,512]{1,0:T(8,128)(2,1)} %param.4) | copy-start | bytes 393220
  7.2 86.6 %all-gather.3.cloned.1.call-start = ((), (), s32[]{:S(2)}) async-start(), calls=%async_computation.6 | async-start | bytes 4259840 | tf_op jit(solution)/shard_map/all_gather | solution.py:15
  9.0 123.4 %reduce-scatter.7.cloned.1.call-start = ((), (), s32[]{:S(2)}) async-start(), calls=%async_computation.7 | async-start | bytes 2457600 | tf_op jit(solution)/shard_map/reduce_scatter | solution.py:30
  99.1 45.2 %copy-start.1 = (bf16[16,1920]{1,0:T(8,128)(2,1)S(1)}, bf16[16,1920]{1,0:T(8,128)(2,1)}, u32[]{:S(2)}) copy-start(bf16[16,1920]{1,0:T(8,128)(2,1)} %param.7) | copy-start | bytes 184324
  118.9 56.6 %all-to-all-start.2 = ((bf16[8,12,16,512]{3,2,1,0:T(8,128)(2,1)}), bf16[8,12,16,512]{3,2,1,0:T(8,128)(2,1)S(1)}, u32[]{:S(2)}, u32[]{:S(2)}) async-start(bf16[8,12,16,512]{3,2,1,0:T(8,128)(2,1)} %broadcast_in_dim.5), calls=%async_computation.3 | async-start | bytes 3145728 | tf_op jit(solution)/shard_map/all_to_all | solution.py:22
  133.5 21.3 %collective-permute-start = (bf16[32,3840]{1,0:T(8,128)(2,1)S(1)}, bf16[32,3840]{1,0:T(8,128)(2,1)S(1)}, u32[]{:S(2)}, u32[]{:S(2)}) collective-permute-start(bf16[32,3840]{1,0:T(8,128)(2,1)S(1)} %convert_element_type.23), channel_id=1, source_target_pairs={{0,8},{8,0},{1,9},{9,1},{2,10},{10,2},{3,11},{11,3},{4,12},{12,4},... | collective-permute-start | bytes 737288 | tf_op jit(solution)/shard_map/ppermute | solution.py:31
  144.3 12.7 %collective-permute-start.1 = (bf16[16,1920]{1,0:T(8,128)(2,1)S(1)}, bf16[16,1920]{1,0:T(8,128)(2,1)S(1)}, u32[]{:S(2)}, u32[]{:S(2)}) collective-permute-start(bf16[16,1920]{1,0:T(8,128)(2,1)S(1)} %copy-done.1), channel_id=1, source_target_pairs={{0,8},{8,0},{1,9},{9,1},{2,10},{10,2},{3,11},{11,3},{4,12},{12,4},... | collective-permute-start | bytes 184328 | tf_op jit(solution)/shard_map/ppermute | solution.py:29
  175.5 62.2 %all-to-all-start = ((bf16[12,128,2,160]{1,3,2,0:T(8,128)(2,1)}), bf16[12,128,2,160]{1,3,2,0:T(8,128)(2,1)}, u32[]{:S(2)}, u32[]{:S(2)}) async-start(bf16[12,128,2,160]{1,3,2,0:T(8,128)(2,1)} %copy.35), calls=%async_computation.1 | async-start | bytes 1966080 | tf_op jit(solution)/shard_map/all_to_all | solution.py:64
  191.7 44.7 %reduce-scatter.5.cloned.1.call-start = ((), (), s32[]{:S(2)}) async-start(), calls=%async_computation.5 | async-start | bytes 294912 | tf_op jit(solution)/shard_map/reduce_scatter | solution.py:51
Sparse Core Ops, SparseCore 0:
  10.4 83.3 all-gather.2
  99.3 33.1 reduce-scatter.6
  195.6 40.6 reduce-scatter.4

commit v13 on v12

--- a/solution.py
+++ b/solution.py
@@ -27,8 +27,8 @@
     swap = [(0, 1), (1, 0)]
     upper = lax.axis_index("zh")
     partner_cot = lax.ppermute(cotangent, "zh", swap)
-    summed = lax.psum_scatter(partial, "x", scatter_dimension=0, tiled=True)
-    summed = summed + lax.ppermute(summed.astype(jnp.bfloat16), "zh", swap).astype(jnp.float32)
+    summed = lax.psum_scatter(partial.astype(jnp.bfloat16), "x", scatter_dimension=0, tiled=True)
+    summed = summed.astype(jnp.float32) + lax.ppermute(summed, "zh", swap).astype(jnp.float32)
     gate_pre = summed[:, :hidden_units]
     up_pre = summed[:, hidden_units:]
     sigmoid_val = jax.nn.sigmoid(gate_pre)

time: 248 us -> 239 us (0.964)
  starting transfers between devices: 35.8 us -> 31 us
  waiting for transfers between devices: 141 us -> 138 us
    reduce_scatter x1, waiting for transfers between devices: 6.76 us -> 1.71 us  [body(): lax.psum_scatter(partial.astype(jnp.bfloat16), 'x', scatter_dimension=0,...]
    ppermute x1, waiting for transfers between devices: 1.09 us -> 5.76 us  [body(): partner_cot = lax.ppermute(cotangent, 'zh', swap)]
    all_to_all x1, starting transfers between devices: 16.2 us -> 12 us  [body(): owned = lax.all_to_all(by_owner, REP, 0, 0, tiled=True)]
where the time goes in v13:
time: 239 us; the launch traced here: 238 us
  waiting for transfers between devices  138 us (58%)
  blocking collectives  33.1 us (14%)
  starting transfers between devices  31 us (13%)
  between operations  13.9 us (6%)
  matrix products  9.27 us (4%)
  other arithmetic  6.51 us (3%)
  local copies, waits for them, and re-layouts  6.34 us (3%)
    all_gather x1, waiting for transfers between devices, body(): stacked = lax.all_gather(pair, REP, axis=0, tiled=False)  84.8 us
    reduce_scatter x1, waiting for transfers between devices, body(): lax.psum_scatter(jnp.einsum('tkrj,rkjd->td', gathered.reshape(gathered.sh...  38.7 us
    all_to_all x1, blocking collectives, body(): part = lax.all_to_all(copies, REP, 0, 0, tiled=True)  18.3 us
    all_gather x1, blocking collectives, body(): gathered = lax.all_gather(pair_grads, 'x', axis=0, tiled=True)  14.8 us
    all_to_all x1, starting transfers between devices, body(): owned = lax.all_to_all(by_owner, REP, 0, 0, tiled=True)  12 us
    ppermute x1, starting transfers between devices, body(): lax.ppermute(summed, 'zh', swap).astype(jnp.float32)  10 us
    ppermute x1, waiting for transfers between devices, body(): lax.ppermute(summed, 'zh', swap).astype(jnp.float32)  7.06 us
    all_to_all x1, starting transfers between devices, body(): all_tokens = lax.all_to_all(spread, 'col', 0, 0, tiled=True)  6.78 us
  transfers between devices with their start and end apart: 7, of which 5 were waited for; matrix products, arithmetic and copies ran while one was open for 5% of the time, Pallas kernels for 0%

profile of v13, /device:TPU:6, one launch (start us, length us, event | category | flops | bytes accessed | tf_op | source)
XLA Modules:
  0.0 238.2 jit_solution(4834629853542888998)
XLA Ops:
  7.2 0.0 copy-start
  7.2 0.0 all-gather.3.cloned.1.call-start
  7.2 1.8 pad_maximum_fusion
  9.0 0.0 all-gather.3.cloned.1.call-update
  9.0 0.0 reduce-scatter.7.cloned.1.call-start
  9.1 84.8 %all-gather.3.cloned.1.call-done = bf16[24,160,512]{2,1,0:T(8,128)(2,1)} async-done(((bf16[2,160,512]{2,1,0:T(8,128)(2,1)}), bf16[24,160,512]{2,1,0:T(8,128)(2,1)}) %all-gather.3.cloned.1.call-update) | async-done | bytes 3932176 | tf_op jit(solution)/shard_map/all_gather | solution.py:15
  93.8 0.0 copy-done
  93.8 3.3 %fusion.2 = bf16[128,2,12,160]{0,3,1,2:T(8,128)(2,1)S(1)} fusion(bf16[12,2,160,512]{3,2,1,0:T(8,128)(2,1)} %bitcast.28, bf16[128,512]{1,0:T(8,128)(2,1)S(1)} %copy-done), kind=kOutput, calls=%fused_computation.4 | convolution fusion | flops 503808000 | bytes 5046272 | tf_op jit(solution)/shard_map/td,rkjd->tkrj/dot_general | solution.py:25
  97.1 0.1 copy.30
  97.2 0.0 copy-start.1
  97.2 1.3 copy.40
  98.5 0.0 reduce-scatter.7.cloned.1.call-update
  98.6 18.3 %all_to_all.15 = bf16[12,16,512]{2,1,0:T(8,128)(2,1)S(1)} all-to-all(bf16[12,16,512]{2,1,0:T(8,128)(2,1)S(1)} %broadcast_in_dim.4), channel_id=1, replica_groups=mesh['zl'=6,'core'=2,'x'=4,'zh'=2,'col'=8] {'zl','core'}, dimensions={0} | all-to-all | bytes 393216 | tf_op jit(solution)/shard_map/all_to_all | solution.py:20
  117.0 1.4 broadcast_in_dim.5
  118.3 6.8 %all-to-all-start.2 = ((bf16[8,12,16,512]{3,2,1,0:T(8,128)(2,1)}), bf16[8,12,16,512]{3,2,1,0:T(8,128)(2,1)S(1)}, u32[]{:S(2)}, u32[]{:S(2)}) async-start(bf16[8,12,16,512]{3,2,1,0:T(8,128)(2,1)} %broadcast_in_dim.5), calls=%async_computation.3 | async-start | bytes 3145728 | tf_op jit(solution)/shard_map/all_to_all | solution.py:22
  125.1 1.7 reduce-scatter.7.cloned.1.call-done
  126.8 10.0 %collective-permute-start = (bf16[32,3840]{1,0:T(8,128)(2,1)}, bf16[32,3840]{1,0:T(8,128)(2,1)S(1)}, u32[]{:S(2)}, u32[]{:S(2)}) collective-permute-start(bf16[32,3840]{1,0:T(8,128)(2,1)} %reduce-scatter.7.cloned.1.call-done), channel_id=1, source_target_pairs={{0,8},{8,0},{1,9},{9,1},{2,10},{10,2},{3,11},{11,3},{4,12},{12,4},... | collective-permute-start | bytes 737288 | tf_op jit(solution)/shard_map/ppermute | solution.py:31
  136.9 0.0 copy-done.1
  136.9 2.1 collective-permute-start.1
  139.0 7.1 %collective-permute-done = bf16[32,3840]{1,0:T(8,128)(2,1)S(1)} collective-permute-done((bf16[32,3840]{1,0:T(8,128)(2,1)}, bf16[32,3840]{1,0:T(8,128)(2,1)S(1)}, u32[]{:S(2)}, u32[]{:S(2)}) %collective-permute-start) | collective-permute-done | bytes 245792 | tf_op jit(solution)/shard_map/ppermute | solution.py:31
  146.1 1.0 convert_add_fusion
  147.1 5.8 %collective-permute-done.1 = bf16[16,1920]{1,0:T(8,128)(2,1)S(1)} collective-permute-done((bf16[16,1920]{1,0:T(8,128)(2,1)S(1)}, bf16[16,1920]{1,0:T(8,128)(2,1)S(1)}, u32[]{:S(2)}, u32[]{:S(2)}) %collective-permute-start.1) | collective-permute-done | bytes 61472 | tf_op jit(solution)/shard_map/ppermute | solution.py:29
  152.8 0.8 fusion.8
  153.6 14.8 %all_gather.11 = bf16[128,3840]{1,0:T(8,128)(2,1)} all-gather(bf16[32,3840]{1,0:T(8,128)(2,1)S(1)} %pad_maximum_fusion.1), channel_id=1, replica_groups=mesh['zl'=6,'core'=2,'x'=4,'zh'=2,'col'=8] {'x'}, dimensions={0}, use_global_device_ids=true | all-gather | bytes 1228800 | tf_op jit(solution)/shard_map/all_gather | solution.py:48
  168.4 1.6 copy.33
  170.0 1.0 copy.35
  171.0 0.0 all-to-all-done.2
  171.0 12.0 %all-to-all-start = ((bf16[12,128,2,160]{1,3,2,0:T(8,128)(2,1)}), bf16[12,128,2,160]{1,3,2,0:T(8,128)(2,1)}, u32[]{:S(2)}, u32[]{:S(2)}) async-start(bf16[12,128,2,160]{1,3,2,0:T(8,128)(2,1)} %copy.35), calls=%async_computation.1 | async-start | bytes 1966080 | tf_op jit(solution)/shard_map/all_to_all | solution.py:64
  183.0 0.0 reduce-scatter.5.cloned.1.call-start
  183.1 3.5 %fusion.3 = f32[128,512]{1,0:T(8,128)} fusion(bf16[128,2,12,160]{0,3,2,1:T(8,128)(2,1)S(1)} %bitcast.31, bf16[12,2,160,512]{3,2,1,0:T(8,128)(2,1)} %bitcast.29), kind=kOutput, calls=%fused_computation.5 | convolution fusion | flops 503316480 | bytes 5177344 | tf_op jit(solution)/shard_map/tkrj,rkjd->td/dot_general | solution.py:52
  186.6 0.0 reduce-scatter.5.cloned.1.call-update
  186.6 0.2 copy.36
  186.8 1.5 fusion.12
  188.3 38.7 %reduce-scatter.5.cloned.1.call-done = f32[16,512]{1,0:T(8,128)} async-done(((f32[128,512]{1,0:T(8,128)}), f32[16,512]{1,0:T(8,128)}) %reduce-scatter.5.cloned.1.call-update) | async-done | bytes 32784 | tf_op jit(solution)/shard_map/reduce_scatter | solution.py:51
  227.1 1.4 convert_element_type.41
  228.4 0.0 all-to-all-done
  228.4 2.4 %reduce-precision_reduce_fusion = f32[2,160,512]{2,1,0:T(8,128)S(1)} fusion(bf16[12,128,2,160]{1,3,2,0:T(8,128)(2,1)} %all-to-all-done, bf16[12,128,512,1]{2,1,3,0:T(8,128)(2,1)S(1)} %bitcast.33), kind=kOutput, calls=%fused_computation | convolution fusion | flops 507084800 | bytes 3211264 | tf_op jit(solution)/shard_map/qtkh,qtd->qkhd/dot_general | solution.py:65
  230.9 0.1 multiply_convert_fusion
  230.9 0.7 fusion.13
  (3 shorter events, 0.0 us)
Async XLA Ops:
  7.2 86.7 %copy-start = (bf16[128,512]{1,0:T(8,128)(2,1)S(1)}, bf16[128,512]{1,0:T(8,128)(2,1)}, u32[]{:S(2)}) copy-start(bf16[128,512]{1,0:T(8,128)(2,1)} %param.4) | copy-start | bytes 393220
  7.2 86.6 %all-gather.3.cloned.1.call-start = ((), (), s32[]{:S(2)}) async-start(), calls=%async_computation.6 | async-start | bytes 4259840 | tf_op jit(solution)/shard_map/all_gather | solution.py:15
  9.0 117.8 %reduce-scatter.7.cloned.1.call-start = ((), (), s32[]{:S(2)}) async-start(), calls=%async_computation.7 | async-start | bytes 1228800 | tf_op jit(solution)/shard_map/reduce_scatter | solution.py:30
  97.2 39.7 %copy-start.1 = (bf16[16,1920]{1,0:T(8,128)(2,1)S(1)}, bf16[16,1920]{1,0:T(8,128)(2,1)}, u32[]{:S(2)}) copy-start(bf16[16,1920]{1,0:T(8,128)(2,1)} %param.7) | copy-start | bytes 184324
  118.3 52.7 %all-to-all-start.2 = ((bf16[8,12,16,512]{3,2,1,0:T(8,128)(2,1)}), bf16[8,12,16,512]{3,2,1,0:T(8,128)(2,1)S(1)}, u32[]{:S(2)}, u32[]{:S(2)}) async-start(bf16[8,12,16,512]{3,2,1,0:T(8,128)(2,1)} %broadcast_in_dim.5), calls=%async_computation.3 | async-start | bytes 3145728 | tf_op jit(solution)/shard_map/all_to_all | solution.py:22
  126.8 19.2 %collective-permute-start = (bf16[32,3840]{1,0:T(8,128)(2,1)}, bf16[32,3840]{1,0:T(8,128)(2,1)S(1)}, u32[]{:S(2)}, u32[]{:S(2)}) collective-permute-start(bf16[32,3840]{1,0:T(8,128)(2,1)} %reduce-scatter.7.cloned.1.call-done), channel_id=1, source_target_pairs={{0,8},{8,0},{1,9},{9,1},{2,10},{10,2},{3,11},{11,3},{4,12},{12,4},... | collective-permute-start | bytes 737288 | tf_op jit(solution)/shard_map/ppermute | solution.py:31
  136.9 15.9 %collective-permute-start.1 = (bf16[16,1920]{1,0:T(8,128)(2,1)S(1)}, bf16[16,1920]{1,0:T(8,128)(2,1)S(1)}, u32[]{:S(2)}, u32[]{:S(2)}) collective-permute-start(bf16[16,1920]{1,0:T(8,128)(2,1)S(1)} %copy-done.1), channel_id=1, source_target_pairs={{0,8},{8,0},{1,9},{9,1},{2,10},{10,2},{3,11},{11,3},{4,12},{12,4},... | collective-permute-start | bytes 184328 | tf_op jit(solution)/shard_map/ppermute | solution.py:29
  171.0 57.4 %all-to-all-start = ((bf16[12,128,2,160]{1,3,2,0:T(8,128)(2,1)}), bf16[12,128,2,160]{1,3,2,0:T(8,128)(2,1)}, u32[]{:S(2)}, u32[]{:S(2)}) async-start(bf16[12,128,2,160]{1,3,2,0:T(8,128)(2,1)} %copy.35), calls=%async_computation.1 | async-start | bytes 1966080 | tf_op jit(solution)/shard_map/all_to_all | solution.py:64
  183.0 44.1 %reduce-scatter.5.cloned.1.call-start = ((), (), s32[]{:S(2)}) async-start(), calls=%async_computation.5 | async-start | bytes 294912 | tf_op jit(solution)/shard_map/reduce_scatter | solution.py:51
Sparse Core Ops, SparseCore 0:
  10.4 83.3 all-gather.2
  98.7 28.0 reduce-scatter.6
  187.2 39.8 reduce-scatter.4

commit v14 on v13

--- a/solution.py
+++ b/solution.py
@@ -54,7 +54,7 @@
             gathered.reshape(gathered.shape[0], 2, replicas, shard_units),
             stacked,
             preferred_element_type=jnp.float32,
-        ),
+        ).astype(jnp.bfloat16),
         "col",
         scatter_dimension=0,
         tiled=True,

time: 239 us -> 234 us (0.979)
  other arithmetic: 6.51 us -> 3.62 us
    reduce_scatter x1, waiting for transfers between devices: 38.7 us -> 5.36 us  [body(): lax.psum_scatter(jnp.einsum('tkrj,rkjd->td', gathered.reshape(gathered.sh...]
    all_to_all x1, waiting for transfers between devices: 0.01 us -> 31.1 us  [body(): owned = lax.all_to_all(by_owner, REP, 0, 0, tiled=True)]
  transfers between devices with their start and end apart: 7 -> 7, of which waited for: 5 -> 6; matrix products, arithmetic and copies ran while one was open for 5% -> 6% of each run, Pallas kernels for 0% -> 0%
where the time goes in v14:
time: 234 us
  waiting for transfers between devices  136 us (58%)
  blocking collectives  33 us (14%)
  starting transfers between devices  30.6 us (13%)
  between operations  13.9 us (6%)
  matrix products  9.31 us (4%)
  local copies, waits for them, and re-layouts  7.48 us (3%)
  other arithmetic  3.62 us (2%)
    all_gather x1, waiting for transfers between devices, body(): stacked = lax.all_gather(pair, REP, axis=0, tiled=False)  84.8 us
    all_to_all x1, waiting for transfers between devices, body(): owned = lax.all_to_all(by_owner, REP, 0, 0, tiled=True)  31.1 us
    all_to_all x1, blocking collectives, body(): part = lax.all_to_all(copies, REP, 0, 0, tiled=True)  18.4 us
    all_gather x1, blocking collectives, body(): gathered = lax.all_gather(pair_grads, 'x', axis=0, tiled=True)  14.6 us
    all_to_all x1, starting transfers between devices, body(): owned = lax.all_to_all(by_owner, REP, 0, 0, tiled=True)  11.5 us
    ppermute x1, starting transfers between devices, body(): lax.ppermute(summed, 'zh', swap).astype(jnp.float32)  10 us
    ppermute x1, waiting for transfers between devices, body(): lax.ppermute(summed, 'zh', swap).astype(jnp.float32)  7.09 us
    all_to_all x1, starting transfers between devices, body(): all_tokens = lax.all_to_all(spread, 'col', 0, 0, tiled=True)  6.78 us
  transfers between devices with their start and end apart: 7, of which 6 were waited for; matrix products, arithmetic and copies ran while one was open for 6% of the time, Pallas kernels for 0%

profile of v14, /device:TPU:6, one launch (start us, length us, event | category | flops | bytes accessed | tf_op | source)
XLA Modules:
  0.0 233.7 jit_solution(982665886296558619)
XLA Ops:
  7.2 0.0 copy-start
  7.2 0.0 all-gather.3.cloned.1.call-start
  7.2 1.8 pad_maximum_fusion
  9.0 0.0 all-gather.3.cloned.1.call-update
  9.0 0.0 reduce-scatter.7.cloned.1.call-start
  9.1 84.8 %all-gather.3.cloned.1.call-done = bf16[24,160,512]{2,1,0:T(8,128)(2,1)} async-done(((bf16[2,160,512]{2,1,0:T(8,128)(2,1)}), bf16[24,160,512]{2,1,0:T(8,128)(2,1)}) %all-gather.3.cloned.1.call-update) | async-done | bytes 3932176 | tf_op jit(solution)/shard_map/all_gather | solution.py:15
  93.8 0.0 copy-done
  93.8 3.3 %fusion.2 = bf16[128,2,12,160]{0,3,1,2:T(8,128)(2,1)S(1)} fusion(bf16[12,2,160,512]{3,2,1,0:T(8,128)(2,1)} %bitcast.30, bf16[128,512]{1,0:T(8,128)(2,1)S(1)} %copy-done), kind=kOutput, calls=%fused_computation.4 | convolution fusion | flops 503808000 | bytes 5046272 | tf_op jit(solution)/shard_map/td,rkjd->tkrj/dot_general | solution.py:25
  97.1 0.1 copy.30
  97.2 0.0 copy-start.2
  97.2 1.3 copy.40
  98.5 0.0 reduce-scatter.7.cloned.1.call-update
  98.6 18.4 %all_to_all.15 = bf16[12,16,512]{2,1,0:T(8,128)(2,1)S(1)} all-to-all(bf16[12,16,512]{2,1,0:T(8,128)(2,1)S(1)} %broadcast_in_dim.4), channel_id=1, replica_groups=mesh['zl'=6,'core'=2,'x'=4,'zh'=2,'col'=8] {'zl','core'}, dimensions={0} | all-to-all | bytes 393216 | tf_op jit(solution)/shard_map/all_to_all | solution.py:20
  116.9 1.4 broadcast_in_dim.5
  118.3 6.8 %all-to-all-start.2 = ((bf16[8,12,16,512]{3,2,1,0:T(8,128)(2,1)}), bf16[8,12,16,512]{3,2,1,0:T(8,128)(2,1)S(1)}, u32[]{:S(2)}, u32[]{:S(2)}) async-start(bf16[8,12,16,512]{3,2,1,0:T(8,128)(2,1)} %broadcast_in_dim.5), calls=%async_computation.3 | async-start | bytes 3145728 | tf_op jit(solution)/shard_map/all_to_all | solution.py:22
  125.1 1.7 reduce-scatter.7.cloned.1.call-done
  126.8 10.0 %collective-permute-start = (bf16[32,3840]{1,0:T(8,128)(2,1)}, bf16[32,3840]{1,0:T(8,128)(2,1)S(1)}, u32[]{:S(2)}, u32[]{:S(2)}) collective-permute-start(bf16[32,3840]{1,0:T(8,128)(2,1)} %reduce-scatter.7.cloned.1.call-done), channel_id=1, source_target_pairs={{0,8},{8,0},{1,9},{9,1},{2,10},{10,2},{3,11},{11,3},{4,12},{12,4},... | collective-permute-start | bytes 737288 | tf_op jit(solution)/shard_map/ppermute | solution.py:31
  136.9 0.0 copy-done.2
  136.9 2.1 collective-permute-start.1
  139.0 7.1 %collective-permute-done = bf16[32,3840]{1,0:T(8,128)(2,1)S(1)} collective-permute-done((bf16[32,3840]{1,0:T(8,128)(2,1)}, bf16[32,3840]{1,0:T(8,128)(2,1)S(1)}, u32[]{:S(2)}, u32[]{:S(2)}) %collective-permute-start) | collective-permute-done | bytes 245792 | tf_op jit(solution)/shard_map/ppermute | solution.py:31
  146.1 1.0 convert_add_fusion
  147.1 5.7 %collective-permute-done.1 = bf16[16,1920]{1,0:T(8,128)(2,1)S(1)} collective-permute-done((bf16[16,1920]{1,0:T(8,128)(2,1)S(1)}, bf16[16,1920]{1,0:T(8,128)(2,1)S(1)}, u32[]{:S(2)}, u32[]{:S(2)}) %collective-permute-start.1) | collective-permute-done | bytes 61472 | tf_op jit(solution)/shard_map/ppermute | solution.py:29
  152.8 0.1 fusion.11
  153.0 14.6 %all_gather.11 = bf16[128,3840]{1,0:T(8,128)(2,1)} all-gather(bf16[32,3840]{1,0:T(8,128)(2,1)S(1)} %pad_maximum_fusion.1), channel_id=1, replica_groups=mesh['zl'=6,'core'=2,'x'=4,'zh'=2,'col'=8] {'x'}, dimensions={0}, use_global_device_ids=true | all-gather | bytes 1228800 | tf_op jit(solution)/shard_map/all_gather | solution.py:48
  167.6 1.6 copy.33
  169.2 1.0 copy.35
  170.3 0.0 all-to-all-done.2
  170.3 11.5 %all-to-all-start = ((bf16[12,128,2,160]{1,3,2,0:T(8,128)(2,1)}), bf16[12,128,2,160]{1,3,2,0:T(8,128)(2,1)}, u32[]{:S(2)}, u32[]{:S(2)}) async-start(bf16[12,128,2,160]{1,3,2,0:T(8,128)(2,1)} %copy.35), calls=%async_computation.1 | async-start | bytes 1966080 | tf_op jit(solution)/shard_map/all_to_all | solution.py:64
  181.8 0.0 reduce-scatter.5.cloned.1.call-start
  181.9 1.3 copy.36
  183.2 0.0 copy-start.1
  183.2 3.6 %fusion.6 = bf16[128,512]{1,0:T(8,128)(2,1)} fusion(bf16[128,2,12,160]{0,3,2,1:T(8,128)(2,1)S(1)} %bitcast.33, bf16[12,2,160,512]{3,2,1,0:T(8,128)(2,1)} %bitcast.31), kind=kOutput, calls=%fused_computation.6 | convolution fusion | flops 503382016 | bytes 5046272 | tf_op jit(solution)/shard_map/tkrj,rkjd->td/dot_general | solution.py:52
  186.8 0.0 reduce-scatter.5.cloned.1.call-update
  186.8 0.6 fusion.15
  187.5 31.1 %all-to-all-done = bf16[12,128,2,160]{1,3,2,0:T(8,128)(2,1)} async-done(((bf16[12,128,2,160]{1,3,2,0:T(8,128)(2,1)}), bf16[12,128,2,160]{1,3,2,0:T(8,128)(2,1)}, u32[]{:S(2)}, u32[]{:S(2)}) %all-to-all-start) | async-done | bytes 983072 | tf_op jit(solution)/shard_map/all_to_all | solution.py:64
  218.5 0.0 copy-done.1
  218.5 2.4 %reduce-precision_reduce_fusion = f32[2,160,512]{2,1,0:T(8,128)S(1)} fusion(bf16[12,128,2,160]{1,3,2,0:T(8,128)(2,1)} %all-to-all-done, bf16[12,128,512,1]{2,1,3,0:T(8,128)(2,1)S(1)} %bitcast.35), kind=kOutput, calls=%fused_computation | convolution fusion | flops 507084800 | bytes 3211264 | tf_op jit(solution)/shard_map/qtkh,qtd->qkhd/dot_general | solution.py:65
  221.0 0.1 multiply_convert_fusion
  221.0 0.7 fusion.16
  221.8 5.4 %reduce-scatter.5.cloned.1.call-done = bf16[16,512]{1,0:T(8,128)(2,1)} async-done(((bf16[128,512]{1,0:T(8,128)(2,1)}), bf16[16,512]{1,0:T(8,128)(2,1)}) %reduce-scatter.5.cloned.1.call-update) | async-done | bytes 16400 | tf_op jit(solution)/shard_map/reduce_scatter | solution.py:51
  (3 shorter events, 0.0 us)
Async XLA Ops:
  7.2 86.7 %copy-start = (bf16[128,512]{1,0:T(8,128)(2,1)S(1)}, bf16[128,512]{1,0:T(8,128)(2,1)}, u32[]{:S(2)}) copy-start(bf16[128,512]{1,0:T(8,128)(2,1)} %param.4) | copy-start | bytes 393220
  7.2 86.6 %all-gather.3.cloned.1.call-start = ((), (), s32[]{:S(2)}) async-start(), calls=%async_computation.6 | async-start | bytes 4259840 | tf_op jit(solution)/shard_map/all_gather | solution.py:15
  9.0 117.8 %reduce-scatter.7.cloned.1.call-start = ((), (), s32[]{:S(2)}) async-start(), calls=%async_computation.7 | async-start | bytes 1228800 | tf_op jit(solution)/shard_map/reduce_scatter | solution.py:30
  97.2 39.7 %copy-start.2 = (bf16[16,1920]{1,0:T(8,128)(2,1)S(1)}, bf16[16,1920]{1,0:T(8,128)(2,1)}, u32[]{:S(2)}) copy-start(bf16[16,1920]{1,0:T(8,128)(2,1)} %param.7) | copy-start | bytes 184324
  118.3 52.0 %all-to-all-start.2 = ((bf16[8,12,16,512]{3,2,1,0:T(8,128)(2,1)}), bf16[8,12,16,512]{3,2,1,0:T(8,128)(2,1)S(1)}, u32[]{:S(2)}, u32[]{:S(2)}) async-start(bf16[8,12,16,512]{3,2,1,0:T(8,128)(2,1)} %broadcast_in_dim.5), calls=%async_computation.3 | async-start | bytes 3145728 | tf_op jit(solution)/shard_map/all_to_all | solution.py:22
  126.8 19.3 %collective-permute-start = (bf16[32,3840]{1,0:T(8,128)(2,1)}, bf16[32,3840]{1,0:T(8,128)(2,1)S(1)}, u32[]{:S(2)}, u32[]{:S(2)}) collective-permute-start(bf16[32,3840]{1,0:T(8,128)(2,1)} %reduce-scatter.7.cloned.1.call-done), channel_id=1, source_target_pairs={{0,8},{8,0},{1,9},{9,1},{2,10},{10,2},{3,11},{11,3},{4,12},{12,4},... | collective-permute-start | bytes 737288 | tf_op jit(solution)/shard_map/ppermute | solution.py:31
  136.9 15.9 %collective-permute-start.1 = (bf16[16,1920]{1,0:T(8,128)(2,1)S(1)}, bf16[16,1920]{1,0:T(8,128)(2,1)S(1)}, u32[]{:S(2)}, u32[]{:S(2)}) collective-permute-start(bf16[16,1920]{1,0:T(8,128)(2,1)S(1)} %copy-done.2), channel_id=1, source_target_pairs={{0,8},{8,0},{1,9},{9,1},{2,10},{10,2},{3,11},{11,3},{4,12},{12,4},... | collective-permute-start | bytes 184328 | tf_op jit(solution)/shard_map/ppermute | solution.py:29
  170.3 48.3 %all-to-all-start = ((bf16[12,128,2,160]{1,3,2,0:T(8,128)(2,1)}), bf16[12,128,2,160]{1,3,2,0:T(8,128)(2,1)}, u32[]{:S(2)}, u32[]{:S(2)}) async-start(bf16[12,128,2,160]{1,3,2,0:T(8,128)(2,1)} %copy.35), calls=%async_computation.1 | async-start | bytes 1966080 | tf_op jit(solution)/shard_map/all_to_all | solution.py:64
  181.8 45.3 %reduce-scatter.5.cloned.1.call-start = ((), (), s32[]{:S(2)}) async-start(), calls=%async_computation.5 | async-start | bytes 147456 | tf_op jit(solution)/shard_map/reduce_scatter | solution.py:51
  183.2 35.4 %copy-start.1 = (bf16[12,8,16,512]{3,2,1,0:T(8,128)(2,1)S(1)}, bf16[12,8,16,512]{3,2,1,0:T(8,128)(2,1)}, u32[]{:S(2)}) copy-start(bf16[12,8,16,512]{3,2,1,0:T(8,128)(2,1)} %copy.36) | copy-start | bytes 4718596
Sparse Core Ops, SparseCore 0:
  10.4 83.3 all-gather.2
  98.7 28.0 reduce-scatter.6
  186.9 40.1 reduce-scatter.4

commit v15 on v14

--- a/solution.py
+++ b/solution.py
@@ -22,11 +22,13 @@
     all_tokens = lax.all_to_all(spread, "col", 0, 0, tiled=True)
     all_tokens = all_tokens.transpose(1, 0, 2, 3).reshape(replicas, n_col * slab, tokens.shape[1])
     hidden_units = replicas * shard_units
+    swap = [(0, 1), (1, 0)]
+    partner_cot = lax.ppermute(cotangent, "zh", swap)
+    tokens, partner_cot = lax.optimization_barrier((tokens, partner_cot))
     partial = jnp.einsum("td,rkjd->tkrj", tokens, stacked, preferred_element_type=jnp.float32)
     partial = partial.reshape(tokens.shape[0], 2 * hidden_units)
     swap = [(0, 1), (1, 0)]
     upper = lax.axis_index("zh")
-    partner_cot = lax.ppermute(cotangent, "zh", swap)
     summed = lax.psum_scatter(partial.astype(jnp.bfloat16), "x", scatter_dimension=0, tiled=True)
     summed = summed.astype(jnp.float32) + lax.ppermute(summed, "zh", swap).astype(jnp.float32)
     gate_pre = summed[:, :hidden_units]

time: 234 us -> 232 us (level)
  waiting for transfers between devices: 136 us -> 118 us
  starting transfers between devices: 30.6 us -> 41.8 us
  blocking collectives: 33 us -> 37.4 us
    all_gather x1, waiting for transfers between devices: 84.8 us -> 65.8 us  [body(): stacked = lax.all_gather(pair, REP, axis=0, tiled=False)]
    ppermute x1, starting transfers between devices: 2.1 us -> 15.1 us  [body(): partner_cot = lax.ppermute(cotangent, 'zh', swap)]
    all_gather x1, blocking collectives: 14.6 us -> 19 us  [body(): gathered = lax.all_gather(pair_grads, 'x', axis=0, tiled=True)]
where the time goes in v15:
time: 232 us; the launch traced here: 231 us
  waiting for transfers between devices  118 us (51%)
  starting transfers between devices  41.8 us (18%)
  blocking collectives  37.4 us (16%)
  between operations  13.9 us (6%)
  matrix products  9.31 us (4%)
  local copies, waits for them, and re-layouts  7.47 us (3%)
  other arithmetic  3.62 us (2%)
    all_gather x1, waiting for transfers between devices, body(): stacked = lax.all_gather(pair, REP, axis=0, tiled=False)  65.8 us
    all_to_all x1, waiting for transfers between devices, body(): owned = lax.all_to_all(by_owner, REP, 0, 0, tiled=True)  31.1 us
    all_gather x1, blocking collectives, body(): gathered = lax.all_gather(pair_grads, 'x', axis=0, tiled=True)  19 us
    all_to_all x1, blocking collectives, body(): part = lax.all_to_all(copies, REP, 0, 0, tiled=True)  18.4 us
    ppermute x1, starting transfers between devices, body(): partner_cot = lax.ppermute(cotangent, 'zh', swap)  15.1 us
    ppermute x1, starting transfers between devices, body(): lax.ppermute(summed, 'zh', swap).astype(jnp.float32)  10 us
    all_to_all x1, starting transfers between devices, body(): owned = lax.all_to_all(by_owner, REP, 0, 0, tiled=True)  9.75 us
    ppermute x1, waiting for transfers between devices, body(): lax.ppermute(summed, 'zh', swap).astype(jnp.float32)  8.88 us
  transfers between devices with their start and end apart: 7, of which 6 were waited for; matrix products, arithmetic and copies ran while one was open for 6% of the time, Pallas kernels for 0%

profile of v15, /device:TPU:6, one launch (start us, length us, event | category | flops | bytes accessed | tf_op | source)
XLA Modules:
  0.0 231.0 jit_solution(11773241864887965055)
XLA Ops:
  7.2 0.0 copy-start
  7.2 0.0 all-gather.3.cloned.1.call-start
  7.2 1.8 pad_maximum_fusion
  9.0 0.0 all-gather.3.cloned.1.call-update
  9.0 0.0 reduce-scatter.7.cloned.1.call-start
  9.1 15.1 %collective-permute-start = (bf16[16,1920]{1,0:T(8,128)(2,1)}, bf16[16,1920]{1,0:T(8,128)(2,1)S(1)}, u32[]{:S(2)}, u32[]{:S(2)}) collective-permute-start(bf16[16,1920]{1,0:T(8,128)(2,1)} %param.7), channel_id=1, source_target_pairs={{0,8},{8,0},{1,9},{9,1},{2,10},{10,2},{3,11},{11,3},{4,12},{12,4},... | collective-permute-start | bytes 184328 | tf_op jit(solution)/shard_map/ppermute | solution.py:26
  24.2 3.8 %collective-permute-done = bf16[16,1920]{1,0:T(8,128)(2,1)S(1)} collective-permute-done((bf16[16,1920]{1,0:T(8,128)(2,1)}, bf16[16,1920]{1,0:T(8,128)(2,1)S(1)}, u32[]{:S(2)}, u32[]{:S(2)}) %collective-permute-start) | collective-permute-done | bytes 61472 | tf_op jit(solution)/shard_map/ppermute | solution.py:26
  28.0 65.8 %all-gather.3.cloned.1.call-done = bf16[24,160,512]{2,1,0:T(8,128)(2,1)} async-done(((bf16[2,160,512]{2,1,0:T(8,128)(2,1)}), bf16[24,160,512]{2,1,0:T(8,128)(2,1)}) %all-gather.3.cloned.1.call-update) | async-done | bytes 3932176 | tf_op jit(solution)/shard_map/all_gather | solution.py:15
  93.8 0.0 copy-done
  93.8 3.3 %fusion.2 = bf16[128,2,12,160]{0,3,1,2:T(8,128)(2,1)S(1)} fusion(bf16[12,2,160,512]{3,2,1,0:T(8,128)(2,1)} %bitcast.30, bf16[128,512]{1,0:T(8,128)(2,1)S(1)} %copy-done), kind=kOutput, calls=%fused_computation.4 | convolution fusion | flops 503808000 | bytes 5046272 | tf_op jit(solution)/shard_map/td,rkjd->tkrj/dot_general | solution.py:28
  97.1 0.1 copy.30
  97.2 1.3 copy.40
  98.5 0.0 copy-start.2
  98.5 0.0 reduce-scatter.7.cloned.1.call-update
  98.6 18.4 %all_to_all.15 = bf16[12,16,512]{2,1,0:T(8,128)(2,1)S(1)} all-to-all(bf16[12,16,512]{2,1,0:T(8,128)(2,1)S(1)} %broadcast_in_dim.4), channel_id=1, replica_groups=mesh['zl'=6,'core'=2,'x'=4,'zh'=2,'col'=8] {'zl','core'}, dimensions={0} | all-to-all | bytes 393216 | tf_op jit(solution)/shard_map/all_to_all | solution.py:20
  116.9 1.4 broadcast_in_dim.5
  118.3 6.8 %all-to-all-start.2 = ((bf16[8,12,16,512]{3,2,1,0:T(8,128)(2,1)}), bf16[8,12,16,512]{3,2,1,0:T(8,128)(2,1)S(1)}, u32[]{:S(2)}, u32[]{:S(2)}) async-start(bf16[8,12,16,512]{3,2,1,0:T(8,128)(2,1)} %broadcast_in_dim.5), calls=%async_computation.3 | async-start | bytes 3145728 | tf_op jit(solution)/shard_map/all_to_all | solution.py:22
  125.1 1.7 reduce-scatter.7.cloned.1.call-done
  126.8 10.0 %collective-permute-start.1 = (bf16[32,3840]{1,0:T(8,128)(2,1)}, bf16[32,3840]{1,0:T(8,128)(2,1)S(1)}, u32[]{:S(2)}, u32[]{:S(2)}) collective-permute-start(bf16[32,3840]{1,0:T(8,128)(2,1)} %reduce-scatter.7.cloned.1.call-done), channel_id=1, source_target_pairs={{0,8},{8,0},{1,9},{9,1},{2,10},{10,2},{3,11},{11,3},{4,12},{12,4},... | collective-permute-start | bytes 737288 | tf_op jit(solution)/shard_map/ppermute | solution.py:33
  136.9 8.9 %collective-permute-done.1 = bf16[32,3840]{1,0:T(8,128)(2,1)S(1)} collective-permute-done((bf16[32,3840]{1,0:T(8,128)(2,1)}, bf16[32,3840]{1,0:T(8,128)(2,1)S(1)}, u32[]{:S(2)}, u32[]{:S(2)}) %collective-permute-start.1) | collective-permute-done | bytes 245792 | tf_op jit(solution)/shard_map/ppermute | solution.py:33
  145.7 1.0 convert_add_fusion
  146.7 0.0 copy-done.2
  146.7 0.1 fusion.11
  146.9 19.0 %all_gather.11 = bf16[128,3840]{1,0:T(8,128)(2,1)} all-gather(bf16[32,3840]{1,0:T(8,128)(2,1)S(1)} %pad_maximum_fusion.1), channel_id=1, replica_groups=mesh['zl'=6,'core'=2,'x'=4,'zh'=2,'col'=8] {'x'}, dimensions={0}, use_global_device_ids=true | all-gather | bytes 1228800 | tf_op jit(solution)/shard_map/all_gather | solution.py:50
  166.0 1.6 copy.33
  167.6 1.0 copy.35
  168.6 0.0 all-to-all-done.2
  168.6 9.8 %all-to-all-start = ((bf16[12,128,2,160]{1,3,2,0:T(8,128)(2,1)}), bf16[12,128,2,160]{1,3,2,0:T(8,128)(2,1)}, u32[]{:S(2)}, u32[]{:S(2)}) async-start(bf16[12,128,2,160]{1,3,2,0:T(8,128)(2,1)} %copy.35), calls=%async_computation.1 | async-start | bytes 1966080 | tf_op jit(solution)/shard_map/all_to_all | solution.py:66
  178.4 0.0 reduce-scatter.5.cloned.1.call-start
  178.4 1.3 copy.36
  179.7 0.0 copy-start.1
  179.7 3.6 %fusion.6 = bf16[128,512]{1,0:T(8,128)(2,1)} fusion(bf16[128,2,12,160]{0,3,2,1:T(8,128)(2,1)S(1)} %bitcast.33, bf16[12,2,160,512]{3,2,1,0:T(8,128)(2,1)} %bitcast.31), kind=kOutput, calls=%fused_computation.6 | convolution fusion | flops 503382016 | bytes 5046272 | tf_op jit(solution)/shard_map/tkrj,rkjd->td/dot_general | solution.py:54
  183.3 0.0 reduce-scatter.5.cloned.1.call-update
  183.4 0.6 fusion.15
  184.0 31.1 %all-to-all-done = bf16[12,128,2,160]{1,3,2,0:T(8,128)(2,1)} async-done(((bf16[12,128,2,160]{1,3,2,0:T(8,128)(2,1)}), bf16[12,128,2,160]{1,3,2,0:T(8,128)(2,1)}, u32[]{:S(2)}, u32[]{:S(2)}) %all-to-all-start) | async-done | bytes 983072 | tf_op jit(solution)/shard_map/all_to_all | solution.py:66
  215.1 0.0 copy-done.1
  215.1 2.4 %reduce-precision_reduce_fusion = f32[2,160,512]{2,1,0:T(8,128)S(1)} fusion(bf16[12,128,2,160]{1,3,2,0:T(8,128)(2,1)} %all-to-all-done, bf16[12,128,512,1]{2,1,3,0:T(8,128)(2,1)S(1)} %bitcast.35), kind=kOutput, calls=%fused_computation | convolution fusion | flops 507084800 | bytes 3211264 | tf_op jit(solution)/shard_map/qtkh,qtd->qkhd/dot_general | solution.py:67
  217.5 0.1 multiply_convert_fusion
  217.6 0.7 fusion.16
  218.3 6.2 %reduce-scatter.5.cloned.1.call-done = bf16[16,512]{1,0:T(8,128)(2,1)} async-done(((bf16[128,512]{1,0:T(8,128)(2,1)}), bf16[16,512]{1,0:T(8,128)(2,1)}) %reduce-scatter.5.cloned.1.call-update) | async-done | bytes 16400 | tf_op jit(solution)/shard_map/reduce_scatter | solution.py:53
  (3 shorter events, 0.0 us)
Async XLA Ops:
  7.2 86.7 %copy-start = (bf16[128,512]{1,0:T(8,128)(2,1)S(1)}, bf16[128,512]{1,0:T(8,128)(2,1)}, u32[]{:S(2)}) copy-start(bf16[128,512]{1,0:T(8,128)(2,1)} %param.4) | copy-start | bytes 393220
  7.2 86.6 %all-gather.3.cloned.1.call-start = ((), (), s32[]{:S(2)}) async-start(), calls=%async_computation.6 | async-start | bytes 4259840 | tf_op jit(solution)/shard_map/all_gather | solution.py:15
  9.0 117.8 %reduce-scatter.7.cloned.1.call-start = ((), (), s32[]{:S(2)}) async-start(), calls=%async_computation.7 | async-start | bytes 1228800 | tf_op jit(solution)/shard_map/reduce_scatter | solution.py:32
  9.1 19.0 %collective-permute-start = (bf16[16,1920]{1,0:T(8,128)(2,1)}, bf16[16,1920]{1,0:T(8,128)(2,1)S(1)}, u32[]{:S(2)}, u32[]{:S(2)}) collective-permute-start(bf16[16,1920]{1,0:T(8,128)(2,1)} %param.7), channel_id=1, source_target_pairs={{0,8},{8,0},{1,9},{9,1},{2,10},{10,2},{3,11},{11,3},{4,12},{12,4},... | collective-permute-start | bytes 184328 | tf_op jit(solution)/shard_map/ppermute | solution.py:26
  98.5 48.2 %copy-start.2 = (bf16[16,1920]{1,0:T(8,128)(2,1)S(1)}, bf16[16,1920]{1,0:T(8,128)(2,1)}, u32[]{:S(2)}) copy-start(bf16[16,1920]{1,0:T(8,128)(2,1)} %param.7) | copy-start | bytes 184324
  118.3 50.3 %all-to-all-start.2 = ((bf16[8,12,16,512]{3,2,1,0:T(8,128)(2,1)}), bf16[8,12,16,512]{3,2,1,0:T(8,128)(2,1)S(1)}, u32[]{:S(2)}, u32[]{:S(2)}) async-start(bf16[8,12,16,512]{3,2,1,0:T(8,128)(2,1)} %broadcast_in_dim.5), calls=%async_computation.3 | async-start | bytes 3145728 | tf_op jit(solution)/shard_map/all_to_all | solution.py:22
  126.8 18.9 %collective-permute-start.1 = (bf16[32,3840]{1,0:T(8,128)(2,1)}, bf16[32,3840]{1,0:T(8,128)(2,1)S(1)}, u32[]{:S(2)}, u32[]{:S(2)}) collective-permute-start(bf16[32,3840]{1,0:T(8,128)(2,1)} %reduce-scatter.7.cloned.1.call-done), channel_id=1, source_target_pairs={{0,8},{8,0},{1,9},{9,1},{2,10},{10,2},{3,11},{11,3},{4,12},{12,4},... | collective-permute-start | bytes 737288 | tf_op jit(solution)/shard_map/ppermute | solution.py:33
  168.6 46.5 %all-to-all-start = ((bf16[12,128,2,160]{1,3,2,0:T(8,128)(2,1)}), bf16[12,128,2,160]{1,3,2,0:T(8,128)(2,1)}, u32[]{:S(2)}, u32[]{:S(2)}) async-start(bf16[12,128,2,160]{1,3,2,0:T(8,128)(2,1)} %copy.35), calls=%async_computation.1 | async-start | bytes 1966080 | tf_op jit(solution)/shard_map/all_to_all | solution.py:66
  178.4 46.1 %reduce-scatter.5.cloned.1.call-start = ((), (), s32[]{:S(2)}) async-start(), calls=%async_computation.5 | async-start | bytes 147456 | tf_op jit(solution)/shard_map/reduce_scatter | solution.py:53
  179.7 35.4 %copy-start.1 = (bf16[12,8,16,512]{3,2,1,0:T(8,128)(2,1)S(1)}, bf16[12,8,16,512]{3,2,1,0:T(8,128)(2,1)}, u32[]{:S(2)}) copy-start(bf16[12,8,16,512]{3,2,1,0:T(8,128)(2,1)} %copy.36) | copy-start | bytes 4718596
Sparse Core Ops, SparseCore 0:
  10.4 83.3 all-gather.2
  98.7 28.0 reduce-scatter.6
  183.5 40.9 reduce-scatter.4

commit v16 on v15

--- a/solution.py
+++ b/solution.py
@@ -24,7 +24,7 @@
     hidden_units = replicas * shard_units
     swap = [(0, 1), (1, 0)]
     partner_cot = lax.ppermute(cotangent, "zh", swap)
-    tokens, partner_cot = lax.optimization_barrier((tokens, partner_cot))
+    tokens, partner_cot, all_tokens = lax.optimization_barrier((tokens, partner_cot, all_tokens))
     partial = jnp.einsum("td,rkjd->tkrj", tokens, stacked, preferred_element_type=jnp.float32)
     partial = partial.reshape(tokens.shape[0], 2 * hidden_units)
     swap = [(0, 1), (1, 0)]

time: 232 us -> 231 us (level)
  blocking collectives: 37.4 us -> 41.4 us
  starting transfers between devices: 41.8 us -> 38.3 us
    all_gather x1, waiting for transfers between devices: 65.8 us -> 13.7 us  [body(): stacked = lax.all_gather(pair, REP, axis=0, tiled=False)]
    all_to_all x1, waiting for transfers between devices: 0.01 us -> 30.1 us  [body(): all_tokens = lax.all_to_all(spread, 'col', 0, 0, tiled=True)]
    reduce_scatter x1, waiting for transfers between devices: 1.73 us -> 26.7 us  [body(): lax.psum_scatter(partial.astype(jnp.bfloat16), 'x', scatter_dimension=0,...]
    all_to_all x1, blocking collectives: 18.4 us -> 24.3 us  [body(): part = lax.all_to_all(copies, REP, 0, 0, tiled=True)]
    ppermute x1, starting transfers between devices: 15.1 us -> 10 us  [body(): partner_cot = lax.ppermute(cotangent, 'zh', swap)]
    ppermute x1, waiting for transfers between devices: 3.82 us -> 0.01 us  [body(): partner_cot = lax.ppermute(cotangent, 'zh', swap)]
  transfers between devices with their start and end apart: 7 -> 7, of which waited for: 6 -> 6; matrix products, arithmetic and copies ran while one was open for 6% -> 4% of each run, Pallas kernels for 0% -> 0%
where the time goes in v16:
time: 231 us
  waiting for transfers between devices  118 us (51%)
  blocking collectives  41.4 us (18%)
  starting transfers between devices  38.3 us (17%)
  between operations  13.9 us (6%)
  matrix products  9.2 us (4%)
  local copies, waits for them, and re-layouts  6.53 us (3%)
  other arithmetic  3.64 us (2%)
    all_to_all x1, waiting for transfers between devices, body(): owned = lax.all_to_all(by_owner, REP, 0, 0, tiled=True)  32.5 us
    all_to_all x1, waiting for transfers between devices, body(): all_tokens = lax.all_to_all(spread, 'col', 0, 0, tiled=True)  30.1 us
    reduce_scatter x1, waiting for transfers between devices, body(): lax.psum_scatter(partial.astype(jnp.bfloat16), 'x', scatter_dimension=0,...  26.7 us
    all_to_all x1, blocking collectives, body(): part = lax.all_to_all(copies, REP, 0, 0, tiled=True)  24.3 us
    all_gather x1, blocking collectives, body(): gathered = lax.all_gather(pair_grads, 'x', axis=0, tiled=True)  17.1 us
    all_gather x1, waiting for transfers between devices, body(): stacked = lax.all_gather(pair, REP, axis=0, tiled=False)  13.7 us
    all_to_all x1, starting transfers between devices, body(): owned = lax.all_to_all(by_owner, REP, 0, 0, tiled=True)  11 us
    ppermute x1, starting transfers between devices, body(): lax.ppermute(summed, 'zh', swap).astype(jnp.float32)  10.1 us
  transfers between devices with their start and end apart: 7, of which 6 were waited for; matrix products, arithmetic and copies ran while one was open for 4% of the time, Pallas kernels for 0%

profile of v16, /device:TPU:6, one launch (start us, length us, event | category | flops | bytes accessed | tf_op | source)
XLA Modules:
  0.0 230.7 jit_solution(16028348259141942443)
XLA Ops:
  7.2 0.0 copy-start
  7.2 0.0 copy-start.2
  7.2 0.0 all-gather.3.cloned.1.call-start
  7.2 1.8 pad_maximum_fusion
  9.0 0.0 all-gather.3.cloned.1.call-update
  9.0 0.0 copy-done
  9.1 24.3 %all_to_all.15 = bf16[12,16,512]{2,1,0:T(8,128)(2,1)S(1)} all-to-all(bf16[12,16,512]{2,1,0:T(8,128)(2,1)S(1)} %broadcast_in_dim.4), channel_id=1, replica_groups=mesh['zl'=6,'core'=2,'x'=4,'zh'=2,'col'=8] {'zl','core'}, dimensions={0} | all-to-all | bytes 393216 | tf_op jit(solution)/shard_map/all_to_all | solution.py:20
  33.4 1.4 broadcast_in_dim.5
  34.7 7.1 %all-to-all-start.1 = ((bf16[8,12,16,512]{3,2,1,0:T(8,128)(2,1)}), bf16[8,12,16,512]{3,2,1,0:T(8,128)(2,1)S(1)}, u32[]{:S(2)}, u32[]{:S(2)}) async-start(bf16[8,12,16,512]{3,2,1,0:T(8,128)(2,1)} %broadcast_in_dim.5), calls=%async_computation.1 | async-start | bytes 3145728 | tf_op jit(solution)/shard_map/all_to_all | solution.py:22
  41.9 0.0 reduce-scatter.7.cloned.1.call-start
  41.9 0.0 copy-done.2
  41.9 10.0 %collective-permute-start = (bf16[16,1920]{1,0:T(8,128)(2,1)S(1)}, bf16[16,1920]{1,0:T(8,128)(2,1)S(1)}, u32[]{:S(2)}, u32[]{:S(2)}) collective-permute-start(bf16[16,1920]{1,0:T(8,128)(2,1)S(1)} %copy-done.2), channel_id=1, source_target_pairs={{0,8},{8,0},{1,9},{9,1},{2,10},{10,2},{3,11},{11,3},{4,12},{12,4},... | collective-permute-start | bytes 184328 | tf_op jit(solution)/shard_map/ppermute | solution.py:26
  52.0 30.1 %all-to-all-done.1 = bf16[8,12,16,512]{3,2,1,0:T(8,128)(2,1)S(1)} async-done(((bf16[8,12,16,512]{3,2,1,0:T(8,128)(2,1)}), bf16[8,12,16,512]{3,2,1,0:T(8,128)(2,1)S(1)}, u32[]{:S(2)}, u32[]{:S(2)}) %all-to-all-start.1) | async-done | bytes 1572896 | tf_op jit(solution)/shard_map/all_to_all | solution.py:22
  82.1 1.3 copy.41
  83.4 0.0 collective-permute-done
  83.4 13.7 %all-gather.3.cloned.1.call-done = bf16[24,160,512]{2,1,0:T(8,128)(2,1)} async-done(((bf16[2,160,512]{2,1,0:T(8,128)(2,1)}), bf16[24,160,512]{2,1,0:T(8,128)(2,1)}) %all-gather.3.cloned.1.call-update) | async-done | bytes 3932176 | tf_op jit(solution)/shard_map/all_gather | solution.py:15
  97.1 3.3 %fusion.3 = bf16[128,2,12,160]{0,3,1,2:T(8,128)(2,1)S(1)} fusion(bf16[12,2,160,512]{3,2,1,0:T(8,128)(2,1)} %bitcast.30, bf16[128,512]{1,0:T(8,128)(2,1)S(1)} %copy-done), kind=kOutput, calls=%fused_computation.5 | convolution fusion | flops 503808000 | bytes 5046272 | tf_op jit(solution)/shard_map/td,rkjd->tkrj/dot_general | solution.py:28
  100.4 0.1 copy.42
  100.5 1.3 copy.51
  101.8 0.0 reduce-scatter.7.cloned.1.call-update
  101.8 26.7 %reduce-scatter.7.cloned.1.call-done = bf16[32,3840]{1,0:T(8,128)(2,1)} async-done(((bf16[128,3840]{1,0:T(8,128)(2,1)}), bf16[32,3840]{1,0:T(8,128)(2,1)}) %reduce-scatter.7.cloned.1.call-update) | async-done | bytes 245776 | tf_op jit(solution)/shard_map/reduce_scatter | solution.py:32
  128.5 10.1 %collective-permute-start.1 = (bf16[32,3840]{1,0:T(8,128)(2,1)}, bf16[32,3840]{1,0:T(8,128)(2,1)S(1)}, u32[]{:S(2)}, u32[]{:S(2)}) collective-permute-start(bf16[32,3840]{1,0:T(8,128)(2,1)} %reduce-scatter.7.cloned.1.call-done), channel_id=1, source_target_pairs={{0,8},{8,0},{1,9},{9,1},{2,10},{10,2},{3,11},{11,3},{4,12},{12,4},... | collective-permute-start | bytes 737288 | tf_op jit(solution)/shard_map/ppermute | solution.py:33
  138.6 8.8 %collective-permute-done.1 = bf16[32,3840]{1,0:T(8,128)(2,1)S(1)} collective-permute-done((bf16[32,3840]{1,0:T(8,128)(2,1)}, bf16[32,3840]{1,0:T(8,128)(2,1)S(1)}, u32[]{:S(2)}, u32[]{:S(2)}) %collective-permute-start.1) | collective-permute-done | bytes 245792 | tf_op jit(solution)/shard_map/ppermute | solution.py:33
  147.3 1.0 convert_add_fusion
  148.3 0.1 fusion.12
  148.5 17.1 %all_gather.11 = bf16[128,3840]{1,0:T(8,128)(2,1)S(1)} all-gather(bf16[32,3840]{1,0:T(8,128)(2,1)S(1)} %pad_maximum_fusion.1), channel_id=1, replica_groups=mesh['zl'=6,'core'=2,'x'=4,'zh'=2,'col'=8] {'x'}, dimensions={0}, use_global_device_ids=true | all-gather | bytes 1228800 | tf_op jit(solution)/shard_map/all_gather | solution.py:50
  165.6 0.6 copy.45
  166.3 1.0 copy.47
  167.3 0.0 copy-start.1
  167.3 11.0 %all-to-all-start.2 = ((bf16[12,128,2,160]{1,3,2,0:T(8,128)(2,1)}), bf16[12,128,2,160]{1,3,2,0:T(8,128)(2,1)}, u32[]{:S(2)}, u32[]{:S(2)}) async-start(bf16[12,128,2,160]{1,3,2,0:T(8,128)(2,1)} %copy.47), calls=%async_computation.3 | async-start | bytes 1966080 | tf_op jit(solution)/shard_map/all_to_all | solution.py:66
  178.4 0.0 reduce-scatter.5.cloned.1.call-start
  178.4 3.5 %fusion.7 = bf16[128,512]{1,0:T(8,128)(2,1)} fusion(bf16[128,2,12,160]{0,3,2,1:T(8,128)(2,1)S(1)} %bitcast.33, bf16[12,2,160,512]{3,2,1,0:T(8,128)(2,1)} %bitcast.31), kind=kOutput, calls=%fused_computation.7 | convolution fusion | flops 503382016 | bytes 5046272 | tf_op jit(solution)/shard_map/tkrj,rkjd->td/dot_general | solution.py:54
  181.9 0.0 reduce-scatter.5.cloned.1.call-update
  181.9 0.6 fusion.16
  182.6 32.5 %all-to-all-done.2 = bf16[12,128,2,160]{1,3,2,0:T(8,128)(2,1)} async-done(((bf16[12,128,2,160]{1,3,2,0:T(8,128)(2,1)}), bf16[12,128,2,160]{1,3,2,0:T(8,128)(2,1)}, u32[]{:S(2)}, u32[]{:S(2)}) %all-to-all-start.2) | async-done | bytes 983072 | tf_op jit(solution)/shard_map/all_to_all | solution.py:66
  215.1 0.0 copy-done.1
  215.1 2.4 %reduce-precision_reduce_fusion = f32[2,160,512]{2,1,0:T(8,128)S(1)} fusion(bf16[12,128,2,160]{1,3,2,0:T(8,128)(2,1)} %all-to-all-done.2, bf16[12,128,512]{2,1,0:T(8,128)(2,1)S(1)} %bitcast.35), kind=kOutput, calls=%fused_computation | convolution fusion | flops 507084800 | bytes 3211264 | tf_op jit(solution)/shard_map/qtkh,qtd->qkhd/dot_general | solution.py:67
  217.5 0.1 multiply_convert_fusion
  217.6 0.7 fusion.17
  218.3 5.8 %reduce-scatter.5.cloned.1.call-done = bf16[16,512]{1,0:T(8,128)(2,1)} async-done(((bf16[128,512]{1,0:T(8,128)(2,1)}), bf16[16,512]{1,0:T(8,128)(2,1)}) %reduce-scatter.5.cloned.1.call-update) | async-done | bytes 16400 | tf_op jit(solution)/shard_map/reduce_scatter | solution.py:53
  (3 shorter events, 0.0 us)
Async XLA Ops:
  7.2 1.9 copy-start
  7.2 34.7 %copy-start.2 = (bf16[16,1920]{1,0:T(8,128)(2,1)S(1)}, bf16[16,1920]{1,0:T(8,128)(2,1)}, u32[]{:S(2)}) copy-start(bf16[16,1920]{1,0:T(8,128)(2,1)} %param.7) | copy-start | bytes 184324
  7.2 89.9 %all-gather.3.cloned.1.call-start = ((), (), s32[]{:S(2)}) async-start(), calls=%async_computation.6 | async-start | bytes 4259840 | tf_op jit(solution)/shard_map/all_gather | solution.py:15
  34.7 47.3 %all-to-all-start.1 = ((bf16[8,12,16,512]{3,2,1,0:T(8,128)(2,1)}), bf16[8,12,16,512]{3,2,1,0:T(8,128)(2,1)S(1)}, u32[]{:S(2)}, u32[]{:S(2)}) async-start(bf16[8,12,16,512]{3,2,1,0:T(8,128)(2,1)} %broadcast_in_dim.5), calls=%async_computation.1 | async-start | bytes 3145728 | tf_op jit(solution)/shard_map/all_to_all | solution.py:22
  41.9 86.6 %reduce-scatter.7.cloned.1.call-start = ((), (), s32[]{:S(2)}) async-start(), calls=%async_computation.7 | async-start | bytes 1228800 | tf_op jit(solution)/shard_map/reduce_scatter | solution.py:32
  41.9 41.5 %collective-permute-start = (bf16[16,1920]{1,0:T(8,128)(2,1)S(1)}, bf16[16,1920]{1,0:T(8,128)(2,1)S(1)}, u32[]{:S(2)}, u32[]{:S(2)}) collective-permute-start(bf16[16,1920]{1,0:T(8,128)(2,1)S(1)} %copy-done.2), channel_id=1, source_target_pairs={{0,8},{8,0},{1,9},{9,1},{2,10},{10,2},{3,11},{11,3},{4,12},{12,4},... | collective-permute-start | bytes 184328 | tf_op jit(solution)/shard_map/ppermute | solution.py:26
  128.5 18.9 %collective-permute-start.1 = (bf16[32,3840]{1,0:T(8,128)(2,1)}, bf16[32,3840]{1,0:T(8,128)(2,1)S(1)}, u32[]{:S(2)}, u32[]{:S(2)}) collective-permute-start(bf16[32,3840]{1,0:T(8,128)(2,1)} %reduce-scatter.7.cloned.1.call-done), channel_id=1, source_target_pairs={{0,8},{8,0},{1,9},{9,1},{2,10},{10,2},{3,11},{11,3},{4,12},{12,4},... | collective-permute-start | bytes 737288 | tf_op jit(solution)/shard_map/ppermute | solution.py:33
  167.3 47.8 %copy-start.1 = (bf16[8,12,16,512]{3,2,0,1:T(8,128)(2,1)S(1)}, bf16[8,12,16,512]{3,2,0,1:T(8,128)(2,1)}, u32[]{:S(2)}) copy-start(bf16[8,12,16,512]{3,2,0,1:T(8,128)(2,1)} %copy.41) | copy-start | bytes 4718596
  167.3 47.8 %all-to-all-start.2 = ((bf16[12,128,2,160]{1,3,2,0:T(8,128)(2,1)}), bf16[12,128,2,160]{1,3,2,0:T(8,128)(2,1)}, u32[]{:S(2)}, u32[]{:S(2)}) async-start(bf16[12,128,2,160]{1,3,2,0:T(8,128)(2,1)} %copy.47), calls=%async_computation.3 | async-start | bytes 1966080 | tf_op jit(solution)/shard_map/all_to_all | solution.py:66
  178.4 45.8 %reduce-scatter.5.cloned.1.call-start = ((), (), s32[]{:S(2)}) async-start(), calls=%async_computation.5 | async-start | bytes 147456 | tf_op jit(solution)/shard_map/reduce_scatter | solution.py:53
Sparse Core Ops, SparseCore 0:
  10.4 86.6 all-gather.2
  101.9 26.4 reduce-scatter.6
  183.1 40.9 reduce-scatter.4

commit v17 on v15

--- a/solution.py
+++ b/solution.py
@@ -47,7 +47,11 @@
     ).astype(jnp.bfloat16)
     grad_up_pre = (upstream * gated).astype(jnp.bfloat16)
     pair_grads = jnp.concatenate([grad_gate_pre, grad_up_pre], 1)
+    rows = pair_grads.shape[0]
+    pieces = pair_grads.reshape(rows, 2, replicas, shard_units).transpose(2, 0, 1, 3)
+    owned_part = lax.all_to_all(pieces, REP, 0, 0, tiled=True)
     gathered = lax.all_gather(pair_grads, "x", axis=0, tiled=True)
+    owned = lax.all_gather(owned_part, "x", axis=1, tiled=True)
     own_rows = cotangent.shape[0]
     hidden = lax.dynamic_slice_in_dim(hidden, upper * own_rows, own_rows, 0)
     grad_tokens = lax.psum_scatter(
@@ -61,9 +65,6 @@
         scatter_dimension=0,
         tiled=True,
     )
-    rows = gathered.shape[0]
-    by_owner = gathered.reshape(rows, 2, replicas, shard_units).transpose(2, 0, 1, 3)
-    owned = lax.all_to_all(by_owner, REP, 0, 0, tiled=True)
     terms = jnp.einsum("qtkh,qtd->qkhd", owned, all_tokens, preferred_element_type=jnp.float32)
     rounded = lax.reduce_precision(terms, exponent_bits=8, mantissa_bits=7)
     averaged = jnp.sum(rounded, axis=0) * (1.0 / replicas)

time: 232 us -> 233 us (level)
  blocking collectives: 37.4 us -> 57.5 us
  waiting for transfers between devices: 118 us -> 101 us
    all_to_all x1, waiting for transfers between devices: 31.1 us -> 0.01 us  [body(): owned_part = lax.all_to_all(pieces, REP, 0, 0, tiled=True)]
    reduce_scatter x1, waiting for transfers between devices: 1.73 us -> 26.7 us  [body(): lax.psum_scatter(partial.astype(jnp.bfloat16), 'x', scatter_dimension=0,...]
    all_gather x1, waiting for transfers between devices: 65.8 us -> 41.5 us  [body(): stacked = lax.all_gather(pair, REP, axis=0, tiled=False)]
    all_gather x0 -> x1, blocking collectives: none -> 18.7 us  [body(): owned = lax.all_gather(owned_part, 'x', axis=1, tiled=True)]
    reduce_scatter x1, waiting for transfers between devices: 6.17 us -> 20.2 us  [body(): lax.psum_scatter(jnp.einsum('tkrj,rkjd->td', gathered.reshape(gathered.sh...]
    all_to_all x1, blocking collectives: 18.4 us -> 24.3 us  [body(): part = lax.all_to_all(copies, REP, 0, 0, tiled=True)]
    ppermute x1, starting transfers between devices: 15.1 us -> 10 us  [body(): partner_cot = lax.ppermute(cotangent, 'zh', swap)]
    all_to_all x1, starting transfers between devices: 9.75 us -> 14.3 us  [body(): owned_part = lax.all_to_all(pieces, REP, 0, 0, tiled=True)]
  transfers between devices with their start and end apart: 7 -> 7, of which waited for: 6 -> 5; matrix products, arithmetic and copies ran while one was open for 6% -> 6% of each run, Pallas kernels for 0% -> 0%
where the time goes in v17:
time: 233 us
  waiting for transfers between devices  101 us (43%)
  blocking collectives  57.5 us (25%)
  starting transfers between devices  41.9 us (18%)
  between operations  13.9 us (6%)
  matrix products  8.32 us (4%)
  local copies, waits for them, and re-layouts  6.67 us (3%)
  other arithmetic  3.65 us (2%)
    all_gather x1, waiting for transfers between devices, body(): stacked = lax.all_gather(pair, REP, axis=0, tiled=False)  41.5 us
    reduce_scatter x1, waiting for transfers between devices, body(): lax.psum_scatter(partial.astype(jnp.bfloat16), 'x', scatter_dimension=0,...  26.7 us
    all_to_all x1, blocking collectives, body(): part = lax.all_to_all(copies, REP, 0, 0, tiled=True)  24.3 us
    reduce_scatter x1, waiting for transfers between devices, body(): lax.psum_scatter(jnp.einsum('tkrj,rkjd->td', gathered.reshape(gathered.sh...  20.2 us
    all_gather x1, blocking collectives, body(): owned = lax.all_gather(owned_part, 'x', axis=1, tiled=True)  18.7 us
    all_gather x1, blocking collectives, body(): gathered = lax.all_gather(pair_grads, 'x', axis=0, tiled=True)  14.5 us
    all_to_all x1, starting transfers between devices, body(): owned_part = lax.all_to_all(pieces, REP, 0, 0, tiled=True)  14.3 us
    ppermute x1, starting transfers between devices, body(): lax.ppermute(summed, 'zh', swap).astype(jnp.float32)  10.2 us
  transfers between devices with their start and end apart: 7, of which 5 were waited for; matrix products, arithmetic and copies ran while one was open for 6% of the time, Pallas kernels for 0%

profile of v17, /device:TPU:6, one launch (start us, length us, event | category | flops | bytes accessed | tf_op | source)
XLA Modules:
  0.0 232.7 jit_solution(11037978525745860661)
XLA Ops:
  7.2 0.0 copy-start
  7.2 0.0 all-gather.3.cloned.1.call-start
  7.2 1.8 pad_maximum_fusion
  9.0 0.0 all-gather.3.cloned.1.call-update
  9.0 0.0 copy-done
  9.1 24.3 %all_to_all.15 = bf16[12,16,512]{2,1,0:T(8,128)(2,1)S(1)} all-to-all(bf16[12,16,512]{2,1,0:T(8,128)(2,1)S(1)} %broadcast_in_dim.4), channel_id=1, replica_groups=mesh['zl'=6,'core'=2,'x'=4,'zh'=2,'col'=8] {'zl','core'}, dimensions={0} | all-to-all | bytes 393216 | tf_op jit(solution)/shard_map/all_to_all | solution.py:20
  33.4 1.4 broadcast_in_dim.5
  34.7 0.0 copy-start.2
  34.7 7.2 %all-to-all-start.2 = ((bf16[8,12,16,512]{3,2,1,0:T(8,128)(2,1)}), bf16[8,12,16,512]{3,2,1,0:T(8,128)(2,1)S(1)}, u32[]{:S(2)}, u32[]{:S(2)}) async-start(bf16[8,12,16,512]{3,2,1,0:T(8,128)(2,1)} %broadcast_in_dim.5), calls=%async_computation.3 | async-start | bytes 3145728 | tf_op jit(solution)/shard_map/all_to_all | solution.py:22
  42.0 0.0 reduce-scatter.7.cloned.1.call-start
  42.0 0.0 copy-done.2
  42.0 10.0 %collective-permute-start = (bf16[16,1920]{1,0:T(8,128)(2,1)S(1)}, bf16[16,1920]{1,0:T(8,128)(2,1)S(1)}, u32[]{:S(2)}, u32[]{:S(2)}) collective-permute-start(bf16[16,1920]{1,0:T(8,128)(2,1)S(1)} %copy-done.2), channel_id=1, source_target_pairs={{0,8},{8,0},{1,9},{9,1},{2,10},{10,2},{3,11},{11,3},{4,12},{12,4},... | collective-permute-start | bytes 184328 | tf_op jit(solution)/shard_map/ppermute | solution.py:26
  52.1 3.5 %collective-permute-done = bf16[16,1920]{1,0:T(8,128)(2,1)S(1)} collective-permute-done((bf16[16,1920]{1,0:T(8,128)(2,1)S(1)}, bf16[16,1920]{1,0:T(8,128)(2,1)S(1)}, u32[]{:S(2)}, u32[]{:S(2)}) %collective-permute-start) | collective-permute-done | bytes 61472 | tf_op jit(solution)/shard_map/ppermute | solution.py:26
  55.6 0.0 copy-start.4
  55.6 41.5 %all-gather.3.cloned.1.call-done = bf16[24,160,512]{2,1,0:T(8,128)(2,1)} async-done(((bf16[2,160,512]{2,1,0:T(8,128)(2,1)}), bf16[24,160,512]{2,1,0:T(8,128)(2,1)}) %all-gather.3.cloned.1.call-update) | async-done | bytes 3932176 | tf_op jit(solution)/shard_map/all_gather | solution.py:15
  97.2 0.0 copy-done.4
  97.2 3.3 %fusion.2 = bf16[128,2,12,160]{0,3,1,2:T(8,128)(2,1)S(1)} fusion(bf16[12,2,160,512]{3,2,1,0:T(8,128)(2,1)} %bitcast.31, bf16[128,512]{1,0:T(8,128)(2,1)S(1)} %copy-done), kind=kOutput, calls=%fused_computation.4 | convolution fusion | flops 503808000 | bytes 5046272 | tf_op jit(solution)/shard_map/td,rkjd->tkrj/dot_general | solution.py:28
  100.5 0.1 copy.30
  100.5 1.3 copy.40
  101.8 0.0 reduce-scatter.7.cloned.1.call-update
  101.9 26.7 %reduce-scatter.7.cloned.1.call-done = bf16[32,3840]{1,0:T(8,128)(2,1)} async-done(((bf16[128,3840]{1,0:T(8,128)(2,1)}), bf16[32,3840]{1,0:T(8,128)(2,1)}) %reduce-scatter.7.cloned.1.call-update) | async-done | bytes 245776 | tf_op jit(solution)/shard_map/reduce_scatter | solution.py:32
  128.6 0.0 copy-start.1
  128.6 10.2 %collective-permute-start.1 = (bf16[32,3840]{1,0:T(8,128)(2,1)}, bf16[32,3840]{1,0:T(8,128)(2,1)}, u32[]{:S(2)}, u32[]{:S(2)}) collective-permute-start(bf16[32,3840]{1,0:T(8,128)(2,1)} %reduce-scatter.7.cloned.1.call-done), channel_id=1, source_target_pairs={{0,8},{8,0},{1,9},{9,1},{2,10},{10,2},{3,11},{11,3},{4,12},{12,4},... | collective-permute-start | bytes 737288 | tf_op jit(solution)/shard_map/ppermute | solution.py:33
  138.8 0.0 all-to-all-done.2
  138.8 0.0 copy-start.3
  138.8 0.0 copy-start.5
  138.9 0.2 copy.36
  139.0 8.7 %collective-permute-done.1 = bf16[32,3840]{1,0:T(8,128)(2,1)} collective-permute-done((bf16[32,3840]{1,0:T(8,128)(2,1)}, bf16[32,3840]{1,0:T(8,128)(2,1)}, u32[]{:S(2)}, u32[]{:S(2)}) %collective-permute-start.1) | collective-permute-done | bytes 245792 | tf_op jit(solution)/shard_map/ppermute | solution.py:33
  147.7 0.0 copy-done.1
  147.7 1.0 convert_add_fusion
  148.7 0.0 copy-done.3
  148.7 0.0 copy-done.5
  148.7 0.1 fusion.11
  148.9 0.7 reshape.22
  149.6 1.0 copy.49
  150.6 14.3 %all-to-all-start = ((bf16[12,32,2,160]{3,1,2,0:T(8,128)(2,1)}), bf16[12,32,2,160]{3,1,2,0:T(8,128)(2,1)}, u32[]{:S(2)}, u32[]{:S(2)}) async-start(bf16[12,32,2,160]{3,1,2,0:T(8,128)(2,1)} %bitcast.29), calls=%async_computation.1 | async-start | bytes 786432 | tf_op jit(solution)/shard_map/all_to_all | solution.py:52
  164.9 0.0 reduce-scatter.5.cloned.1.call-start
  165.0 14.5 %all_gather.14 = bf16[128,3840]{1,0:T(8,128)(2,1)S(1)} all-gather(bf16[32,3840]{1,0:T(8,128)(2,1)S(1)} %pad_maximum_fusion.1), channel_id=1, replica_groups=mesh['zl'=6,'core'=2,'x'=4,'zh'=2,'col'=8] {'x'}, dimensions={0}, use_global_device_ids=true | all-gather | bytes 1228800 | tf_op jit(solution)/shard_map/all_gather | solution.py:53
  179.4 1.3 copy.33
  180.7 3.8 %fusion.6 = bf16[128,512]{1,0:T(8,128)(2,1)} fusion(bf16[128,2,12,160]{0,3,2,1:T(8,128)(2,1)} %bitcast.35, bf16[12,2,160,512]{3,2,1,0:T(8,128)(2,1)} %bitcast.32), kind=kOutput, calls=%fused_computation.6 | convolution fusion | flops 503382016 | bytes 5046272 | tf_op jit(solution)/shard_map/tkrj,rkjd->td/dot_general | solution.py:58
  184.5 0.0 reduce-scatter.5.cloned.1.call-update
  184.6 0.6 fusion.15
  185.2 0.0 all-to-all-done
  185.2 18.7 %all_gather.15 = bf16[12,128,2,160]{3,1,2,0:T(8,128)(2,1)S(1)} all-gather(bf16[12,32,2,160]{3,1,2,0:T(8,128)(2,1)} %all-to-all-done), channel_id=1, replica_groups=mesh['zl'=6,'core'=2,'x'=4,'zh'=2,'col'=8] {'x'}, dimensions={1}, use_global_device_ids=true | all-gather | bytes 1228800 | tf_op jit(solution)/shard_map/all_gather | solution.py:54
  203.9 1.2 reduce-precision_reduce_fusion
  205.2 0.1 multiply_convert_fusion
  205.2 0.7 fusion.16
  206.0 20.2 %reduce-scatter.5.cloned.1.call-done = bf16[16,512]{1,0:T(8,128)(2,1)} async-done(((bf16[128,512]{1,0:T(8,128)(2,1)}), bf16[16,512]{1,0:T(8,128)(2,1)}) %reduce-scatter.5.cloned.1.call-update) | async-done | bytes 16400 | tf_op jit(solution)/shard_map/reduce_scatter | solution.py:57
  (3 shorter events, 0.0 us)
Async XLA Ops:
  7.2 1.9 copy-start
  7.2 90.0 %all-gather.3.cloned.1.call-start = ((), (), s32[]{:S(2)}) async-start(), calls=%async_computation.6 | async-start | bytes 4259840 | tf_op jit(solution)/shard_map/all_gather | solution.py:15
  34.7 7.3 %copy-start.2 = (bf16[16,1920]{1,0:T(8,128)(2,1)S(1)}, bf16[16,1920]{1,0:T(8,128)(2,1)}, u32[]{:S(2)}) copy-start(bf16[16,1920]{1,0:T(8,128)(2,1)} %param.7) | copy-start | bytes 184324
  34.7 104.1 %all-to-all-start.2 = ((bf16[8,12,16,512]{3,2,1,0:T(8,128)(2,1)}), bf16[8,12,16,512]{3,2,1,0:T(8,128)(2,1)S(1)}, u32[]{:S(2)}, u32[]{:S(2)}) async-start(bf16[8,12,16,512]{3,2,1,0:T(8,128)(2,1)} %broadcast_in_dim.5), calls=%async_computation.3 | async-start | bytes 3145728 | tf_op jit(solution)/shard_map/all_to_all | solution.py:22
  42.0 86.6 %reduce-scatter.7.cloned.1.call-start = ((), (), s32[]{:S(2)}) async-start(), calls=%async_computation.7 | async-start | bytes 1228800 | tf_op jit(solution)/shard_map/reduce_scatter | solution.py:32
  42.0 13.6 %collective-permute-start = (bf16[16,1920]{1,0:T(8,128)(2,1)S(1)}, bf16[16,1920]{1,0:T(8,128)(2,1)S(1)}, u32[]{:S(2)}, u32[]{:S(2)}) collective-permute-start(bf16[16,1920]{1,0:T(8,128)(2,1)S(1)} %copy-done.2), channel_id=1, source_target_pairs={{0,8},{8,0},{1,9},{9,1},{2,10},{10,2},{3,11},{11,3},{4,12},{12,4},... | collective-permute-start | bytes 184328 | tf_op jit(solution)/shard_map/ppermute | solution.py:26
  55.6 41.5 %copy-start.4 = (bf16[16,1920]{1,0:T(8,128)(2,1)}, bf16[16,1920]{1,0:T(8,128)(2,1)S(1)}, u32[]{:S(2)}) copy-start(bf16[16,1920]{1,0:T(8,128)(2,1)S(1)} %collective-permute-done) | copy-start | bytes 184324
  128.6 19.1 %copy-start.1 = (bf16[32,3840]{1,0:T(8,128)(2,1)S(1)}, bf16[32,3840]{1,0:T(8,128)(2,1)}, u32[]{:S(2)}) copy-start(bf16[32,3840]{1,0:T(8,128)(2,1)} %reduce-scatter.7.cloned.1.call-done) | copy-start | bytes 737284
  128.6 19.1 %collective-permute-start.1 = (bf16[32,3840]{1,0:T(8,128)(2,1)}, bf16[32,3840]{1,0:T(8,128)(2,1)}, u32[]{:S(2)}, u32[]{:S(2)}) collective-permute-start(bf16[32,3840]{1,0:T(8,128)(2,1)} %reduce-scatter.7.cloned.1.call-done), channel_id=1, source_target_pairs={{0,8},{8,0},{1,9},{9,1},{2,10},{10,2},{3,11},{11,3},{4,12},{12,4},... | collective-permute-start | bytes 737288 | tf_op jit(solution)/shard_map/ppermute | solution.py:33
  138.8 9.9 %copy-start.3 = (bf16[16,1920]{1,0:T(8,128)(2,1)S(1)}, bf16[16,1920]{1,0:T(8,128)(2,1)}, u32[]{:S(2)}) copy-start(bf16[16,1920]{1,0:T(8,128)(2,1)} %param.7) | copy-start | bytes 184324
  138.8 9.9 %copy-start.5 = (bf16[16,1920]{1,0:T(8,128)(2,1)S(1)}, bf16[16,1920]{1,0:T(8,128)(2,1)}, u32[]{:S(2)}) copy-start(bf16[16,1920]{1,0:T(8,128)(2,1)} %copy-done.4) | copy-start | bytes 184324
  150.6 34.6 %all-to-all-start = ((bf16[12,32,2,160]{3,1,2,0:T(8,128)(2,1)}), bf16[12,32,2,160]{3,1,2,0:T(8,128)(2,1)}, u32[]{:S(2)}, u32[]{:S(2)}) async-start(bf16[12,32,2,160]{3,1,2,0:T(8,128)(2,1)} %bitcast.29), calls=%async_computation.1 | async-start | bytes 786432 | tf_op jit(solution)/shard_map/all_to_all | solution.py:52
  164.9 61.2 %reduce-scatter.5.cloned.1.call-start = ((), (), s32[]{:S(2)}) async-start(), calls=%async_computation.5 | async-start | bytes 147456 | tf_op jit(solution)/shard_map/reduce_scatter | solution.py:57
Sparse Core Ops, SparseCore 0:
  10.4 86.7 all-gather.2
  102.0 26.5 reduce-scatter.6
  184.7 41.4 reduce-scatter.4

commit v18 on v15

--- a/solution.py
+++ b/solution.py
@@ -18,6 +18,7 @@
     mine = lax.dynamic_slice_in_dim(tokens, lax.axis_index("col") * slab, slab, 0)
     copies = jnp.broadcast_to(mine[None], (replicas,) + mine.shape)
     part = lax.all_to_all(copies, REP, 0, 0, tiled=True)
+    tokens, part = lax.optimization_barrier((tokens, part))
     spread = jnp.broadcast_to(part[None], (n_col,) + part.shape)
     all_tokens = lax.all_to_all(spread, "col", 0, 0, tiled=True)
     all_tokens = all_tokens.transpose(1, 0, 2, 3).reshape(replicas, n_col * slab, tokens.shape[1])

time: 232 us -> 233 us (level)
  blocking collectives: 37.4 us -> 14.6 us
  waiting for transfers between devices: 118 us -> 130 us
  starting transfers between devices: 41.8 us -> 52.9 us
    reduce_scatter x1, waiting for transfers between devices: 1.73 us -> 21.6 us  [body(): lax.psum_scatter(partial.astype(jnp.bfloat16), 'x', scatter_dimension=0,...]
    all_to_all x1 -> x0, blocking collectives: 18.4 us -> none  [body(): part = lax.all_to_all(copies, REP, 0, 0, tiled=True)]
    all_to_all x0 -> x1, starting transfers between devices: none -> 12.1 us  [body(): part = lax.all_to_all(copies, REP, 0, 0, tiled=True)]
    all_gather x1, waiting for transfers between devices: 65.8 us -> 57.7 us  [body(): stacked = lax.all_gather(pair, REP, axis=0, tiled=False)]
    ppermute x1, starting transfers between devices: 15.1 us -> 10 us  [body(): partner_cot = lax.ppermute(cotangent, 'zh', swap)]
    all_gather x1, blocking collectives: 19 us -> 14.6 us  [body(): gathered = lax.all_gather(pair_grads, 'x', axis=0, tiled=True)]
    all_to_all x1, starting transfers between devices: 9.75 us -> 14.2 us  [body(): owned = lax.all_to_all(by_owner, REP, 0, 0, tiled=True)]
  transfers between devices with their start and end apart: 7 -> 8, of which waited for: 6 -> 7; matrix products, arithmetic and copies ran while one was open for 6% -> 6% of each run, Pallas kernels for 0% -> 0%
where the time goes in v18:
time: 233 us; the launch traced here: 232 us
  waiting for transfers between devices  130 us (56%)
  starting transfers between devices  52.9 us (23%)
  blocking collectives  14.6 us (6%)
  between operations  13.9 us (6%)
  matrix products  9.29 us (4%)
  local copies, waits for them, and re-layouts  8.18 us (4%)
  other arithmetic  3.63 us (2%)
    all_gather x1, waiting for transfers between devices, body(): stacked = lax.all_gather(pair, REP, axis=0, tiled=False)  57.7 us
    all_to_all x1, waiting for transfers between devices, body(): owned = lax.all_to_all(by_owner, REP, 0, 0, tiled=True)  31.1 us
    reduce_scatter x1, waiting for transfers between devices, body(): lax.psum_scatter(partial.astype(jnp.bfloat16), 'x', scatter_dimension=0,...  21.6 us
    all_gather x1, blocking collectives, body(): gathered = lax.all_gather(pair_grads, 'x', axis=0, tiled=True)  14.6 us
    all_to_all x1, starting transfers between devices, body(): owned = lax.all_to_all(by_owner, REP, 0, 0, tiled=True)  14.2 us
    all_to_all x1, starting transfers between devices, body(): part = lax.all_to_all(copies, REP, 0, 0, tiled=True)  12.1 us
    ppermute x1, starting transfers between devices, body(): partner_cot = lax.ppermute(cotangent, 'zh', swap)  10 us
    ppermute x1, starting transfers between devices, body(): lax.ppermute(summed, 'zh', swap).astype(jnp.float32)  9.89 us
  transfers between devices with their start and end apart: 8, of which 7 were waited for; matrix products, arithmetic and copies ran while one was open for 6% of the time, Pallas kernels for 0%

profile of v18, /device:TPU:6, one launch (start us, length us, event | category | flops | bytes accessed | tf_op | source)
XLA Modules:
  0.0 232.5 jit_solution(5040045483555431713)
XLA Ops:
  7.2 0.0 copy-start
  7.2 0.0 all-gather.3.cloned.1.call-start
  7.2 1.8 pad_maximum_fusion
  9.0 0.0 all-gather.3.cloned.1.call-update
  9.0 0.0 copy-done
  9.1 0.7 broadcast_in_dim.4
  9.7 12.1 %all-to-all-start = ((bf16[12,16,512]{2,1,0:T(8,128)(2,1)}), bf16[12,16,512]{2,1,0:T(8,128)(2,1)S(1)}, u32[]{:S(2)}, u32[]{:S(2)}) async-start(bf16[12,16,512]{2,1,0:T(8,128)(2,1)} %broadcast_in_dim.4), calls=%async_computation | async-start | bytes 393216 | tf_op jit(solution)/shard_map/all_to_all | solution.py:20
  21.9 0.0 reduce-scatter.7.cloned.1.call-start
  21.9 10.0 %collective-permute-start = (bf16[16,1920]{1,0:T(8,128)(2,1)}, bf16[16,1920]{1,0:T(8,128)(2,1)S(1)}, u32[]{:S(2)}, u32[]{:S(2)}) collective-permute-start(bf16[16,1920]{1,0:T(8,128)(2,1)} %param.7), channel_id=1, source_target_pairs={{0,8},{8,0},{1,9},{9,1},{2,10},{10,2},{3,11},{11,3},{4,12},{12,4},... | collective-permute-start | bytes 184328 | tf_op jit(solution)/shard_map/ppermute | solution.py:27
  32.0 2.3 all-to-all-done
  34.2 2.1 collective-permute-done
  36.4 57.7 %all-gather.3.cloned.1.call-done = bf16[24,160,512]{2,1,0:T(8,128)(2,1)} async-done(((bf16[2,160,512]{2,1,0:T(8,128)(2,1)}), bf16[24,160,512]{2,1,0:T(8,128)(2,1)}) %all-gather.3.cloned.1.call-update) | async-done | bytes 3932176 | tf_op jit(solution)/shard_map/all_gather | solution.py:15
  94.1 3.3 %fusion.2 = bf16[128,2,12,160]{0,3,1,2:T(8,128)(2,1)S(1)} fusion(bf16[12,2,160,512]{3,2,1,0:T(8,128)(2,1)} %bitcast.30, bf16[128,512]{1,0:T(8,128)(2,1)S(1)} %copy-done), kind=kOutput, calls=%fused_computation.4 | convolution fusion | flops 503808000 | bytes 5046272 | tf_op jit(solution)/shard_map/td,rkjd->tkrj/dot_general | solution.py:29
  97.4 0.1 copy.30
  97.5 1.3 copy.40
  98.8 0.0 copy-start.2
  98.8 0.0 reduce-scatter.7.cloned.1.call-update
  98.8 1.4 broadcast_in_dim.5
  100.2 6.5 %all-to-all-start.2 = ((bf16[8,12,16,512]{3,2,1,0:T(8,128)(2,1)}), bf16[8,12,16,512]{3,2,1,0:T(8,128)(2,1)S(1)}, u32[]{:S(2)}, u32[]{:S(2)}) async-start(bf16[8,12,16,512]{3,2,1,0:T(8,128)(2,1)} %broadcast_in_dim.5), calls=%async_computation.3 | async-start | bytes 3145728 | tf_op jit(solution)/shard_map/all_to_all | solution.py:23
  106.7 21.6 %reduce-scatter.7.cloned.1.call-done = bf16[32,3840]{1,0:T(8,128)(2,1)} async-done(((bf16[128,3840]{1,0:T(8,128)(2,1)}), bf16[32,3840]{1,0:T(8,128)(2,1)}) %reduce-scatter.7.cloned.1.call-update) | async-done | bytes 245776 | tf_op jit(solution)/shard_map/reduce_scatter | solution.py:33
  128.3 9.9 %collective-permute-start.1 = (bf16[32,3840]{1,0:T(8,128)(2,1)}, bf16[32,3840]{1,0:T(8,128)(2,1)S(1)}, u32[]{:S(2)}, u32[]{:S(2)}) collective-permute-start(bf16[32,3840]{1,0:T(8,128)(2,1)} %reduce-scatter.7.cloned.1.call-done), channel_id=1, source_target_pairs={{0,8},{8,0},{1,9},{9,1},{2,10},{10,2},{3,11},{11,3},{4,12},{12,4},... | collective-permute-start | bytes 737288 | tf_op jit(solution)/shard_map/ppermute | solution.py:34
  138.2 8.9 %collective-permute-done.1 = bf16[32,3840]{1,0:T(8,128)(2,1)S(1)} collective-permute-done((bf16[32,3840]{1,0:T(8,128)(2,1)}, bf16[32,3840]{1,0:T(8,128)(2,1)S(1)}, u32[]{:S(2)}, u32[]{:S(2)}) %collective-permute-start.1) | collective-permute-done | bytes 245792 | tf_op jit(solution)/shard_map/ppermute | solution.py:34
  147.2 1.0 convert_add_fusion
  148.1 0.0 copy-done.2
  148.2 0.1 fusion.11
  148.3 14.6 %all_gather.11 = bf16[128,3840]{1,0:T(8,128)(2,1)} all-gather(bf16[32,3840]{1,0:T(8,128)(2,1)S(1)} %pad_maximum_fusion.1), channel_id=1, replica_groups=mesh['zl'=6,'core'=2,'x'=4,'zh'=2,'col'=8] {'x'}, dimensions={0}, use_global_device_ids=true | all-gather | bytes 1228800 | tf_op jit(solution)/shard_map/all_gather | solution.py:51
  162.9 1.6 copy.33
  164.5 1.0 copy.35
  165.6 0.0 all-to-all-done.2
  165.6 14.2 %all-to-all-start.1 = ((bf16[12,128,2,160]{1,3,2,0:T(8,128)(2,1)}), bf16[12,128,2,160]{1,3,2,0:T(8,128)(2,1)}, u32[]{:S(2)}, u32[]{:S(2)}) async-start(bf16[12,128,2,160]{1,3,2,0:T(8,128)(2,1)} %copy.35), calls=%async_computation.2 | async-start | bytes 1966080 | tf_op jit(solution)/shard_map/all_to_all | solution.py:67
  179.8 0.0 reduce-scatter.5.cloned.1.call-start
  179.8 1.3 copy.36
  181.2 0.0 copy-start.1
  181.2 3.6 %fusion.6 = bf16[128,512]{1,0:T(8,128)(2,1)} fusion(bf16[128,2,12,160]{0,3,2,1:T(8,128)(2,1)S(1)} %bitcast.33, bf16[12,2,160,512]{3,2,1,0:T(8,128)(2,1)} %bitcast.31), kind=kOutput, calls=%fused_computation.6 | convolution fusion | flops 503382016 | bytes 5046272 | tf_op jit(solution)/shard_map/tkrj,rkjd->td/dot_general | solution.py:55
  184.7 0.0 reduce-scatter.5.cloned.1.call-update
  184.8 0.6 fusion.15
  185.4 31.1 %all-to-all-done.1 = bf16[12,128,2,160]{1,3,2,0:T(8,128)(2,1)} async-done(((bf16[12,128,2,160]{1,3,2,0:T(8,128)(2,1)}), bf16[12,128,2,160]{1,3,2,0:T(8,128)(2,1)}, u32[]{:S(2)}, u32[]{:S(2)}) %all-to-all-start.1) | async-done | bytes 983072 | tf_op jit(solution)/shard_map/all_to_all | solution.py:67
  216.5 0.0 copy-done.1
  216.5 2.4 %reduce-precision_reduce_fusion = f32[2,160,512]{2,1,0:T(8,128)S(1)} fusion(bf16[12,128,2,160]{1,3,2,0:T(8,128)(2,1)} %all-to-all-done.1, bf16[12,128,512,1]{2,1,3,0:T(8,128)(2,1)S(1)} %bitcast.35), kind=kOutput, calls=%fused_computation | convolution fusion | flops 507084800 | bytes 3211264 | tf_op jit(solution)/shard_map/qtkh,qtd->qkhd/dot_general | solution.py:68
  218.9 0.1 multiply_convert_fusion
  219.0 0.7 fusion.16
  219.7 6.2 %reduce-scatter.5.cloned.1.call-done = bf16[16,512]{1,0:T(8,128)(2,1)} async-done(((bf16[128,512]{1,0:T(8,128)(2,1)}), bf16[16,512]{1,0:T(8,128)(2,1)}) %reduce-scatter.5.cloned.1.call-update) | async-done | bytes 16400 | tf_op jit(solution)/shard_map/reduce_scatter | solution.py:54
  (2 shorter events, 0.0 us)
Async XLA Ops:
  7.2 1.9 copy-start
  7.2 86.9 %all-gather.3.cloned.1.call-start = ((), (), s32[]{:S(2)}) async-start(), calls=%async_computation.6 | async-start | bytes 4259840 | tf_op jit(solution)/shard_map/all_gather | solution.py:15
  9.7 24.5 %all-to-all-start = ((bf16[12,16,512]{2,1,0:T(8,128)(2,1)}), bf16[12,16,512]{2,1,0:T(8,128)(2,1)S(1)}, u32[]{:S(2)}, u32[]{:S(2)}) async-start(bf16[12,16,512]{2,1,0:T(8,128)(2,1)} %broadcast_in_dim.4), calls=%async_computation | async-start | bytes 393216 | tf_op jit(solution)/shard_map/all_to_all | solution.py:20
  21.9 106.5 %reduce-scatter.7.cloned.1.call-start = ((), (), s32[]{:S(2)}) async-start(), calls=%async_computation.7 | async-start | bytes 1228800 | tf_op jit(solution)/shard_map/reduce_scatter | solution.py:33
  21.9 14.4 %collective-permute-start = (bf16[16,1920]{1,0:T(8,128)(2,1)}, bf16[16,1920]{1,0:T(8,128)(2,1)S(1)}, u32[]{:S(2)}, u32[]{:S(2)}) collective-permute-start(bf16[16,1920]{1,0:T(8,128)(2,1)} %param.7), channel_id=1, source_target_pairs={{0,8},{8,0},{1,9},{9,1},{2,10},{10,2},{3,11},{11,3},{4,12},{12,4},... | collective-permute-start | bytes 184328 | tf_op jit(solution)/shard_map/ppermute | solution.py:27
  98.8 49.4 %copy-start.2 = (bf16[16,1920]{1,0:T(8,128)(2,1)S(1)}, bf16[16,1920]{1,0:T(8,128)(2,1)}, u32[]{:S(2)}) copy-start(bf16[16,1920]{1,0:T(8,128)(2,1)} %param.7) | copy-start | bytes 184324
  100.2 65.4 %all-to-all-start.2 = ((bf16[8,12,16,512]{3,2,1,0:T(8,128)(2,1)}), bf16[8,12,16,512]{3,2,1,0:T(8,128)(2,1)S(1)}, u32[]{:S(2)}, u32[]{:S(2)}) async-start(bf16[8,12,16,512]{3,2,1,0:T(8,128)(2,1)} %broadcast_in_dim.5), calls=%async_computation.3 | async-start | bytes 3145728 | tf_op jit(solution)/shard_map/all_to_all | solution.py:23
  128.3 18.8 %collective-permute-start.1 = (bf16[32,3840]{1,0:T(8,128)(2,1)}, bf16[32,3840]{1,0:T(8,128)(2,1)S(1)}, u32[]{:S(2)}, u32[]{:S(2)}) collective-permute-start(bf16[32,3840]{1,0:T(8,128)(2,1)} %reduce-scatter.7.cloned.1.call-done), channel_id=1, source_target_pairs={{0,8},{8,0},{1,9},{9,1},{2,10},{10,2},{3,11},{11,3},{4,12},{12,4},... | collective-permute-start | bytes 737288 | tf_op jit(solution)/shard_map/ppermute | solution.py:34
  165.6 50.9 %all-to-all-start.1 = ((bf16[12,128,2,160]{1,3,2,0:T(8,128)(2,1)}), bf16[12,128,2,160]{1,3,2,0:T(8,128)(2,1)}, u32[]{:S(2)}, u32[]{:S(2)}) async-start(bf16[12,128,2,160]{1,3,2,0:T(8,128)(2,1)} %copy.35), calls=%async_computation.2 | async-start | bytes 1966080 | tf_op jit(solution)/shard_map/all_to_all | solution.py:67
  179.8 46.2 %reduce-scatter.5.cloned.1.call-start = ((), (), s32[]{:S(2)}) async-start(), calls=%async_computation.5 | async-start | bytes 147456 | tf_op jit(solution)/shard_map/reduce_scatter | solution.py:54
  181.2 35.3 %copy-start.1 = (bf16[12,8,16,512]{3,2,1,0:T(8,128)(2,1)S(1)}, bf16[12,8,16,512]{3,2,1,0:T(8,128)(2,1)}, u32[]{:S(2)}) copy-start(bf16[12,8,16,512]{3,2,1,0:T(8,128)(2,1)} %copy.36) | copy-start | bytes 4718596
Sparse Core Ops, SparseCore 0:
  10.4 83.6 all-gather.2
  98.9 29.3 reduce-scatter.6
  184.9 40.9 reduce-scatter.4
